TPU v7x, 256 devices: a whole 4x4x8 slice. The times are simulated.
256 devices in a mesh: tm: 32 (over x_lo, z, core), cell: 8 (over y, x_hi).
Axes of the slice: x: 4 (x_hi: 2, x_lo: 2; x = x_hi * 2 + x_lo), y: 4, z: 8, core: 2. Of those that a mesh axis runs over, the one named last changes fastest.
Arguments:
- velocity: bfloat16 [4096, 512, 96], P('cell', 'tm'), may hold values from -6 to 6
- cell_coords: int32 [4096, 3], P('cell'), may hold values from 0 to 15, as said below
- q_coords: int32 [512, 3], replicated, may hold values from 0 to 15
- eigvecs: float32 [512, 2, 96, 96], P(('tm', 'cell')), may hold values from -0.4375 to 0.4375
Outputs:
- power: float32 [512, 96, 512], P(('tm', 'cell'))
Inputs may be any that keep to these rules, and one draw needn't show every extreme that they name: `cell_coords`: every row names a distinct lattice position, each coordinate in 0 to 15.
All inputs are finite; a program needn't handle non-finite values.
Results may differ from a plain program's by a relative error of at most 0.015.
Values may be sent and summed in bfloat16 or wider, within the bound.
No kernel may reach another device: no remote copies, remote signals or barrier semaphores. Data moves between devices by JAX's collectives and lax.ppermute only.
A program may use at most 64 MiB of HBM per device.

v0:
```python
import math

import jax
import jax.numpy as jnp
from jax import lax
from jax.sharding import PartitionSpec as P

L = 16


def phase_rows(q_coords, cell_coords):
    products = (
        q_coords[:, None, 0] * cell_coords[None, :, 0]
        + q_coords[:, None, 1] * cell_coords[None, :, 1]
        + q_coords[:, None, 2] * cell_coords[None, :, 2]
    ) % L
    angles = products.astype(jnp.float32) * (2.0 * math.pi / L)
    return jnp.stack([jnp.cos(angles), -jnp.sin(angles)], axis=1).astype(jnp.bfloat16)


def twiddles(frames):
    steps = jnp.arange(frames, dtype=jnp.int32)
    products = steps[:, None] * steps[None, :] % frames
    angles = products.astype(jnp.float32) * (2.0 * math.pi / frames)
    return (jnp.cos(angles), jnp.sin(angles))


def fourier(real_in, imag_in, cosines, sines, form):
    largest_value = lax.Precision.HIGHEST
    real_out = jnp.einsum(form, real_in, cosines, precision=largest_value) + jnp.einsum(
        form, imag_in, sines, precision=largest_value
    )
    imag_out = jnp.einsum(form, imag_in, cosines, precision=largest_value) - jnp.einsum(
        form, real_in, sines, precision=largest_value
    )
    return (real_out, imag_out)


def contract_modes(real_in, imag_in, eigvecs, form):
    largest_value = lax.Precision.HIGHEST
    eigenvector_real = eigvecs[:, 0]
    eigenvector_imaginary = eigvecs[:, 1]
    real_out = jnp.einsum(form, real_in, eigenvector_real, precision=largest_value) + jnp.einsum(
        form, imag_in, eigenvector_imaginary, precision=largest_value
    )
    imag_out = jnp.einsum(form, imag_in, eigenvector_real, precision=largest_value) - jnp.einsum(
        form, real_in, eigenvector_imaginary, precision=largest_value
    )
    return (real_out, imag_out)


def local(velocity, cell_coords, q_coords, eigvecs):
    n_tm = lax.axis_size("tm")
    n_cell = lax.axis_size("cell")
    cell_dev, frames_dev, branches = velocity.shape
    q_total = q_coords.shape[0]
    q_local = q_total // (n_tm * n_cell)
    owned_count = n_tm * q_local
    frames = frames_dev * n_tm
    cosines, sines = twiddles(frames)
    ordered_coords = (
        q_coords.reshape(n_tm, n_cell, q_local, 3).transpose(1, 0, 2, 3).reshape(q_total, 3)
    )
    phase_table = phase_rows(ordered_coords, cell_coords)
    velocity_rows = velocity.reshape(cell_dev, frames_dev * branches)
    partial_term = jnp.dot(
        phase_table.reshape(2 * q_total, cell_dev),
        velocity_rows,
        preferred_element_type=jnp.float32,
    )
    summed = (
        lax.psum(partial_term.astype(jnp.bfloat16), "cell")
        .astype(jnp.float32)
        .reshape(q_total, 2, frames_dev * branches)
    )
    owned_rows = lax.dynamic_slice_in_dim(
        summed, lax.axis_index("cell") * owned_count, owned_count, 0
    )
    owned_rows = owned_rows * (1.0 / math.sqrt(cell_dev * n_cell))
    blocks = owned_rows.reshape(n_tm, q_local, 2, frames_dev, branches)
    collected_rows = lax.all_to_all(
        blocks.astype(jnp.bfloat16), "tm", split_axis=0, concat_axis=3, tiled=True
    ).astype(blocks.dtype)[0]
    amplitude_real, amplitude_imaginary = contract_modes(
        collected_rows[:, 0], collected_rows[:, 1], eigvecs, "xcg,xga->xca"
    )
    out_real, out_imag = fourier(amplitude_real, amplitude_imaginary, cosines, sines, "qts,tw->qsw")
    return (out_real * out_real + out_imag * out_imag) / frames


def solution(mesh):
    in_specs = (P("cell", "tm", None), P("cell", None), P(), P(("tm", "cell"), None, None, None))
    out_specs = P(("tm", "cell"), None, None)
    return jax.shard_map(local, mesh=mesh, in_specs=in_specs, out_specs=out_specs, check_vma=False)
```

profile of v0, /device:TPU:1, one launch (start us, length us, event | category | flops | bytes accessed | tf_op | source)
XLA Modules:
  0.0 242.4 jit_solution(15547292508273227496)
XLA Ops:
  6.5 0.0 copy-start
  6.5 0.0 all-reduce.2.cloned.1.call-start
  6.5 1.1 reshape.405
  7.7 0.1 copy.36
  7.8 0.3 reshape.406
  8.0 0.8 fusion.52
  8.9 5.0 %cosine_convert_fusion = (bf16[512,1,512]{2,0,1:T(8,128)(2,1)S(1)}, bf16[512,1,512]{2,0,1:T(8,128)(2,1)S(1)}) fusion(s32[512]{0:T(512)S(1)} %bitcast.73, s32[512]{0:T(512)S(1)} %bitcast.70, s32[512]{0:T(512)S(1)} %bitcast.74, s32[512]{0:T(512)S(1)} %bitcast.71, s32[512]{0:T(512)S(1)} %bitcast.72, s32[512]{0:T(512)S(1)} %bitcast.69), kind=kLoop, calls=%fused_computation.31 | loop fusion | flops 5505024 | bytes 1060864 | tf_op jit(solution)/shard_map/convert.1
  13.8 0.1 pad_maximum_fusion
  14.0 1.1 copy.37
  15.0 1.2 convert_element_type.46
  16.3 0.0 copy-done
  16.3 4.7 %convolution_convert_fusion = bf16[1024,1536]{1,0:T(8,128)(2,1)} fusion(bf16[1024,512]{1,0:T(8,128)(2,1)} %convert_element_type.46, bf16[512,1536]{0,1:T(8,128)(2,1)S(1)} %bitcast.62), kind=kOutput, calls=%fused_computation | convolution fusion | flops 1612185600 | bytes 5767168 | tf_op jit(solution)/shard_map/dot_general | solution.py:66
  21.0 7.2 %reshape.408 = bf16[512,2,1536]{2,1,0:T(2,128)(2,1)} reshape(bf16[1024,1536]{1,0:T(8,128)(2,1)} %convolution_convert_fusion) | data formatting | bytes 6291456 | tf_op jit(solution)/shard_map/reshape | solution.py:74
  28.2 4.0 %copy.38 = bf16[512,2,1536]{2,0,1:T(8,128)(2,1)} copy(bf16[512,2,1536]{2,1,0:T(2,128)(2,1)} %reshape.408) | data formatting | bytes 6291456 | tf_op jit(solution)/shard_map/reshape | solution.py:74
  32.2 0.0 all-reduce.2.cloned.1.call-update
  32.2 0.0 copy-start.1
  32.2 154.6 %all-reduce.2.cloned.1.call-done = bf16[512,2,1536]{2,0,1:T(8,128)(2,1)} async-done(((bf16[512,2,1536]{2,0,1:T(8,128)(2,1)}), bf16[512,2,1536]{2,0,1:T(8,128)(2,1)}) %all-reduce.2.cloned.1.call-update) | async-done | bytes 3145744 | tf_op jit(solution)/shard_map/psum | solution.py:72
  186.9 1.1 multiply_convert_fusion
  187.9 0.5 convert_element_type.49
  188.4 0.1 copy.39
  188.5 24.4 %all_to_all.15 = bf16[32,2,2,16,96]{4,3,1,2,0:T(8,128)(2,1)S(1)} all-to-all(bf16[32,2,2,16,96]{4,3,1,2,0:T(8,128)(2,1)S(1)} %copy.39), channel_id=1, replica_groups=mesh['tm'=32,'cell'=8] {'tm'}, dimensions={0} | all-to-all | bytes 786432 | tf_op jit(solution)/shard_map/all_to_all | solution.py:81
  212.9 0.0 copy-done.1
  213.0 0.4 fusion.25
  213.4 0.4 fusion.26
  213.8 0.4 convolution_add_fusion.1
  214.2 0.4 convolution_subtract_fusion.1
  214.7 5.1 %fusion.12 = f32[2,96,512]{2,1,0:T(8,128)S(1)} fusion(f32[2,512,96]{1,2,0:T(8,128)S(1)} %convolution_subtract_fusion.1), kind=kOutput, calls=%fused_computation.24 | convolution fusion | flops 607649792 | bytes 786432 | tf_op jit(solution)/shard_map/qts,tw->qsw/dot_general | solution.py:33
  219.8 5.1 %fusion.14 = f32[2,96,512]{2,1,0:T(8,128)S(1)} fusion(f32[2,512,96]{1,2,0:T(8,128)S(1)} %convolution_add_fusion.1), kind=kOutput, calls=%fused_computation.26 | convolution fusion | flops 607649792 | bytes 786432 | tf_op jit(solution)/shard_map/qts,tw->qsw/dot_general | solution.py:30
  224.8 5.1 %fusion = f32[2,96,512]{2,1,0:T(8,128)S(1)} fusion(f32[2,96,512]{2,1,0:T(8,128)S(1)} %fusion.12, f32[2,512,96]{1,2,0:T(8,128)S(1)} %convolution_add_fusion.1), kind=kOutput, calls=%fused_computation.8 | convolution fusion | flops 607846400 | bytes 1179648 | tf_op jit(solution)/shard_map/qts,tw->qsw/dot_general | solution.py:33
  229.9 5.6 %fusion.3 = f32[2,96,512]{2,1,0:T(8,128)} fusion(f32[2,96,512]{2,1,0:T(8,128)S(1)} %fusion, f32[2,96,512]{2,1,0:T(8,128)S(1)} %fusion.14, f32[2,512,96]{1,2,0:T(8,128)S(1)} %convolution_subtract_fusion.1), kind=kOutput, calls=%fused_computation.14 | convolution fusion | flops 608043008 | bytes 1572864 | tf_op jit(solution)/shard_map/qts,tw->qsw/dot_general | solution.py:30
  (2 shorter events, 0.0 us)
Async XLA Ops:
  6.5 9.7 %copy-start = (bf16[512,16,96]{0,2,1:T(8,128)(2,1)S(1)}, bf16[512,16,96]{0,2,1:T(8,128)(2,1)}, u32[]{:S(2)}) copy-start(bf16[512,16,96]{0,2,1:T(8,128)(2,1)} %param.4) | copy-start | bytes 4718596
  6.5 180.3 %all-reduce.2.cloned.1.call-start = ((), (), s32[]{:S(2)}) async-start(), calls=%async_computation.1 | async-start | bytes 6291456 | tf_op jit(solution)/shard_map/psum | solution.py:72
  32.2 180.7 %copy-start.1 = (f32[2,2,96,96]{3,2,1,0:T(8,128)S(1)}, f32[2,2,96,96]{3,2,1,0:T(8,128)}, u32[]{:S(2)}) copy-start(f32[2,2,96,96]{3,2,1,0:T(8,128)} %param.7) | copy-start | bytes 442372
Sparse Core Ops, SparseCore 0:
  32.4 154.4 all-reduce.1
where the time goes:
time: 243 us; the launch traced here: 242 us
  waiting for transfers between devices  155 us (64%)
  matrix products  27.3 us (11%)
  blocking collectives  24.4 us (10%)
  local copies, waits for them, and re-layouts  16.4 us (7%)
  between operations  13.5 us (6%)
  other arithmetic  6.14 us (3%)
    psum x1, waiting for transfers between devices, local(): lax.psum(partial_term.astype(jnp.bfloat16), 'cell').astype(jnp.float32)  155 us
    all_to_all x1, blocking collectives, local(): lax.all_to_all(blocks.astype(jnp.bfloat16), 'tm', split_axis=0, concat_ax...  24.4 us
    reshape x2, local copies, waits for them, and re-layouts, local(): summed = lax.psum(partial_term.astype(jnp.bfloat16), 'cell').astype(jnp.f...  11.2 us
    dot_general x1, matrix products, fourier(): jnp.einsum(form, imag_in, sines, precision=largest_value)  5.61 us
    dot_general x1, matrix products, fourier(): jnp.einsum(form, real_in, cosines, precision=largest_value)  5.08 us
    dot_general x1, matrix products, fourier(): jnp.einsum(form, imag_in, cosines, precision=largest_value)  5.08 us
    dot_general x1, matrix products, fourier(): jnp.einsum(form, real_in, sines, precision=largest_value)  5.08 us
    another operation x1, other arithmetic  4.98 us
  transfers between devices with their start and end apart: 1, of which 1 were waited for; matrix products, arithmetic and copies ran while one was open for 0% of the time, Pallas kernels for 0%

commit v1 on v0

v1 whole, which is shorter than its diff:
```python
import math

import jax
import jax.numpy as jnp
from jax import lax
from jax.sharding import PartitionSpec as P

L = 16


def phase_rows(q_coords, cell_coords):
    products = (
        q_coords[:, None, 0] * cell_coords[None, :, 0]
        + q_coords[:, None, 1] * cell_coords[None, :, 1]
        + q_coords[:, None, 2] * cell_coords[None, :, 2]
    ) % L
    angles = products.astype(jnp.float32) * (2.0 * math.pi / L)
    return jnp.cos(angles).astype(jnp.bfloat16), (-jnp.sin(angles)).astype(jnp.bfloat16)


def twiddles(frames):
    inner = 16
    outer = frames // inner
    w = jnp.arange(frames, dtype=jnp.int32)
    a = jnp.arange(outer, dtype=jnp.int32)
    b = jnp.arange(inner, dtype=jnp.int32)
    coarse = (a[:, None] * w[None, :] % outer).astype(jnp.float32) * (2.0 * math.pi / outer)
    fine = (b[:, None] * w[None, :] % frames).astype(jnp.float32) * (2.0 * math.pi / frames)
    cos_c, sin_c = jnp.cos(coarse)[:, None, :], jnp.sin(coarse)[:, None, :]
    cos_f, sin_f = jnp.cos(fine)[None, :, :], jnp.sin(fine)[None, :, :]
    cosines = (cos_c * cos_f - sin_c * sin_f).reshape(frames, frames)
    sines = (sin_c * cos_f + cos_c * sin_f).reshape(frames, frames)
    return cosines, sines


def local(velocity, cell_coords, q_coords, eigvecs):
    n_tm = lax.axis_size("tm")
    n_cell = lax.axis_size("cell")
    cell_dev, frames_dev, branches = velocity.shape
    q_total = q_coords.shape[0]
    q_local = q_total // (n_tm * n_cell)
    frames = frames_dev * n_tm
    ordered_coords = (
        q_coords.reshape(n_tm, n_cell, q_local, 3).transpose(1, 0, 2, 3).reshape(q_total, 3)
    )
    cos_rows, sin_rows = phase_rows(ordered_coords, cell_coords)
    table = jnp.stack(
        [
            cos_rows.reshape(n_cell, n_tm * q_local, cell_dev),
            sin_rows.reshape(n_cell, n_tm * q_local, cell_dev),
        ],
        axis=1,
    ).reshape(2 * q_total, cell_dev)
    velocity_rows = velocity.reshape(cell_dev, frames_dev * branches)
    partial_term = jnp.dot(table, velocity_rows, preferred_element_type=jnp.float32)
    partial_term = partial_term.astype(jnp.bfloat16).reshape(
        n_cell, 2 * n_tm * q_local, frames_dev * branches
    )
    summed = lax.psum_scatter(partial_term, "cell", scatter_dimension=0, tiled=True)
    blocks = summed.reshape(2, n_tm, q_local, frames_dev, branches)
    collected = lax.all_to_all(blocks, "tm", split_axis=1, concat_axis=3, tiled=True)
    collected = collected.reshape(2, q_local, frames, branches).astype(jnp.float32)

    scale = 1.0 / math.sqrt(cell_dev * n_cell)
    e_real = eigvecs[:, 0] * scale
    e_imag = eigvecs[:, 1] * scale
    e_block = jnp.stack(
        [jnp.concatenate([e_real, -e_imag], axis=2), jnp.concatenate([e_imag, e_real], axis=2)],
        axis=1,
    )
    highest = lax.Precision.HIGHEST
    amplitude = jnp.einsum("rjtk,jrks->jts", collected, e_block, precision=highest)
    cosines, sines = twiddles(frames)
    basis = jnp.concatenate([cosines, sines], axis=1)
    projected = jnp.einsum("jts,tw->jsw", amplitude, basis, precision=highest)
    on_cos = projected[:, :, :frames]
    on_sin = projected[:, :, frames:]
    out_real = on_cos[:, :branches] + on_sin[:, branches:]
    out_imag = on_cos[:, branches:] - on_sin[:, :branches]
    return (out_real * out_real + out_imag * out_imag) / frames


def solution(mesh):
    in_specs = (P("cell", "tm", None), P("cell", None), P(), P(("tm", "cell"), None, None, None))
    out_specs = P(("tm", "cell"), None, None)
    return jax.shard_map(local, mesh=mesh, in_specs=in_specs, out_specs=out_specs, check_vma=False)
```

time: 243 us -> 145 us (0.60)
  waiting for transfers between devices: 155 us -> 99.3 us
  blocking collectives: 24.4 us -> 0 us
  matrix products: 27.3 us -> 6.89 us
  local copies, waits for them, and re-layouts: 16.4 us -> 6.49 us
  starting transfers between devices: 0.01 us -> 9.09 us
  other arithmetic: 6.14 us -> 9 us
    psum x1 -> x0, waiting for transfers between devices: 155 us -> none  [local(): lax.psum(partial_term.astype(jnp.bfloat16), 'cell').astype(jnp.float32)]
    reduce_scatter x0 -> x1, waiting for transfers between devices: none -> 86 us  [local(): lax.psum_scatter(partial_term, 'cell', scatter_dimension=0, tiled=True)]
    all_to_all x1 -> x0, blocking collectives: 24.4 us -> none  [local(): lax.all_to_all(blocks.astype(jnp.bfloat16), 'tm', split_axis=0, concat_ax...]
    dot_general x9 -> x3, matrix products: 27.3 us -> 6.89 us  [the longest x1 3.5 us: local(): jnp.dot(table, velocity_rows, preferred_element_type=jnp.float32)]
    all_to_all x0 -> x1, waiting for transfers between devices: none -> 13.3 us  [local(): lax.all_to_all(blocks, 'tm', split_axis=1, concat_axis=3, tiled=True)]
    all_to_all x0 -> x1, starting transfers between devices: none -> 9.09 us  [local(): lax.all_to_all(blocks, 'tm', split_axis=1, concat_axis=3, tiled=True)]
    reshape x2, local copies, waits for them, and re-layouts: 11.2 us -> 2.31 us  [local(): blocks = summed.reshape(2, n_tm, q_local, frames_dev, branches)]
    another operation x2, other arithmetic: 5.08 us -> 0.13 us  [the longest x1 0.1 us: local(): jnp.stack([cos_rows.reshape(n_cell, n_tm * q_local, cell_dev), sin_rows.r...]
  transfers between devices with their start and end apart: 1 -> 2, of which waited for: 1 -> 2; matrix products, arithmetic and copies ran while one was open for 0% -> 2% of each run, Pallas kernels for 0% -> 0%
where the time goes in v1:
time: 145 us; the launch traced here: 144 us
  waiting for transfers between devices  99.3 us (68%)
  between operations  13.5 us (9%)
  starting transfers between devices  9.09 us (6%)
  other arithmetic  9 us (6%)
  matrix products  6.89 us (5%)
  local copies, waits for them, and re-layouts  6.49 us (4%)
    reduce_scatter x1, waiting for transfers between devices, local(): lax.psum_scatter(partial_term, 'cell', scatter_dimension=0, tiled=True)  86 us
    all_to_all x1, waiting for transfers between devices, local(): lax.all_to_all(blocks, 'tm', split_axis=1, concat_axis=3, tiled=True)  13.3 us
    all_to_all x1, starting transfers between devices, local(): lax.all_to_all(blocks, 'tm', split_axis=1, concat_axis=3, tiled=True)  9.09 us
    convert_element_type x1, other arithmetic, phase_rows(): jnp.cos(angles).astype(jnp.bfloat16)  4.84 us
    dot_general x1, matrix products, local(): jnp.dot(table, velocity_rows, preferred_element_type=jnp.float32)  3.5 us
  transfers between devices with their start and end apart: 2, of which 2 were waited for; matrix products, arithmetic and copies ran while one was open for 2% of the time, Pallas kernels for 0%

profile of v1, /device:TPU:1, one launch (start us, length us, event | category | flops | bytes accessed | tf_op | source)
XLA Modules:
  0.0 144.3 jit_solution(2409852883985162330)
XLA Ops:
  6.5 0.0 copy-start
  6.5 0.0 reduce-scatter.2.cloned.1.call-start
  6.5 1.1 reshape.256
  7.7 0.1 copy.15
  7.8 0.3 reshape.257
  8.1 0.1 mul.261
  8.1 0.1 mul.266
  8.2 0.1 mul.271
  8.3 0.8 fusion.33
  9.1 4.8 %cosine_convert_fusion = (bf16[8,1,64,512]{3,2,1,0:T(8,128)(2,1)S(1)}, bf16[8,1,64,512]{3,2,1,0:T(8,128)(2,1)S(1)}) fusion(s32[512]{0:T(512)S(1)} %bitcast.47, s32[8,64]{1,0:T(8,128)S(1)} %mul.271, s32[512]{0:T(512)S(1)} %bitcast.48, s32[8,64]{1,0:T(8,128)S(1)} %mul.266, s32[512]{0:T(512)S(1)} %bitcast.46, s32[8,64]{1,0:T(8,128)S(1)} %mul.261), kind=kLoop, calls=%fused_computation.16 | loop fusion | flops 5505024 | bytes 1060864 | tf_op jit(solution)/shard_map/convert_element_type | solution.py:18
  14.0 0.1 pad_maximum_fusion
  14.1 0.0 copy-done
  14.1 3.5 %convolution_convert_fusion = bf16[1024,1536]{1,0:T(8,128)(2,1)} fusion(bf16[1024,512]{1,0:T(8,128)(2,1)S(1)} %bitcast.45, bf16[512,1536]{0,1:T(8,128)(2,1)S(1)} %bitcast.38), kind=kOutput, calls=%fused_computation | convolution fusion | flops 1612185600 | bytes 5767168 | tf_op jit(solution)/shard_map/dot_general | solution.py:55
  17.6 0.0 copy-start.2
  17.6 0.0 reduce-scatter.2.cloned.1.call-update
  17.6 0.9 copy-done.2
  18.5 0.1 copy.23
  18.6 86.0 %reduce-scatter.2.cloned.1.call-done = bf16[1,128,1536]{2,1,0:T(8,128)(2,1)} async-done(((bf16[8,128,1536]{2,1,0:T(8,128)(2,1)}), bf16[1,128,1536]{2,1,0:T(8,128)(2,1)}) %reduce-scatter.2.cloned.1.call-update) | async-done | bytes 393232 | tf_op jit(solution)/shard_map/reduce_scatter | solution.py:59
  104.6 1.4 reshape.261
  106.1 0.9 copy.16
  106.9 9.1 %all-to-all-start = ((bf16[2,32,2,16,96]{4,3,2,0,1:T(8,128)(2,1)}), bf16[2,32,2,16,96]{4,3,2,0,1:T(8,128)(2,1)S(1)}, u32[]{:S(2)}, u32[]{:S(2)}) async-start(bf16[2,32,2,16,96]{4,3,2,0,1:T(8,128)(2,1)} %copy.16), calls=%async_computation.1 | async-start | bytes 1048576 | tf_op jit(solution)/shard_map/all_to_all | solution.py:61
  116.0 0.8 fusion.27
  116.8 0.1 copy.22
  116.9 0.3 fusion.24
  117.2 2.1 %multiply_subtract_fusion = (f32[32,16,512]{2,1,0:T(8,128)S(1)}, f32[32,16,512]{2,1,0:T(8,128)}) fusion(f32[16,512]{1,0:T(8,128)} %get-tuple-element.23, f32[32,512]{1,0:T(8,128)S(1)} %get-tuple-element.21, f32[16,512]{1,0:T(8,128)} %get-tuple-element.24, f32[32,512]{1,0:T(8,128)S(1)} %get-tuple-element.22), kind=kLoop, calls=%fused_computation.14 | loop fusion | flops 1572864 | bytes 2293760 | tf_op jit(solution)/shard_map/sub | solution.py:31
  119.3 13.3 %all-to-all-done = bf16[2,32,2,16,96]{4,3,2,0,1:T(8,128)(2,1)S(1)} async-done(((bf16[2,32,2,16,96]{4,3,2,0,1:T(8,128)(2,1)}), bf16[2,32,2,16,96]{4,3,2,0,1:T(8,128)(2,1)S(1)}, u32[]{:S(2)}, u32[]{:S(2)}) %all-to-all-start) | async-done | bytes 393248 | tf_op jit(solution)/shard_map/all_to_all | solution.py:61
  132.6 0.0 copy-start.1
  132.7 0.7 convolution_bitcast_fusion
  133.3 0.5 copy-done.1
  133.8 2.7 %fusion = f32[2,192,1024]{2,1,0:T(8,128)S(1)} fusion(f32[2,512,192]{1,2,0:T(8,128)S(1)} %convolution_bitcast_fusion, f32[512,512]{1,0:T(8,128)S(1)} %bitcast.40, f32[512,512]{1,0:T(8,128)S(1)} %bitcast.39), kind=kOutput, calls=%fused_computation.2 | convolution fusion | flops 2416443392 | bytes 4456448 | tf_op jit(solution)/shard_map/jts,tw->jsw/dot_general | solution.py:75
  136.6 0.9 fusion.8
  (6 shorter events, 0.1 us)
Async XLA Ops:
  6.5 7.5 %copy-start = (bf16[512,16,96]{0,2,1:T(8,128)(2,1)S(1)}, bf16[512,16,96]{0,2,1:T(8,128)(2,1)}, u32[]{:S(2)}) copy-start(bf16[512,16,96]{0,2,1:T(8,128)(2,1)} %param.4) | copy-start | bytes 4718596
  6.5 98.1 %reduce-scatter.2.cloned.1.call-start = ((), (), s32[]{:S(2)}) async-start(), calls=%async_computation.2 | async-start | bytes 3538944 | tf_op jit(solution)/shard_map/reduce_scatter | solution.py:59
  17.6 0.9 copy-start.2
  106.9 25.7 %all-to-all-start = ((bf16[2,32,2,16,96]{4,3,2,0,1:T(8,128)(2,1)}), bf16[2,32,2,16,96]{4,3,2,0,1:T(8,128)(2,1)S(1)}, u32[]{:S(2)}, u32[]{:S(2)}) async-start(bf16[2,32,2,16,96]{4,3,2,0,1:T(8,128)(2,1)} %copy.16), calls=%async_computation.1 | async-start | bytes 1048576 | tf_op jit(solution)/shard_map/all_to_all | solution.py:61
  132.6 1.2 copy-start.1
Sparse Core Ops, SparseCore 0:
  17.7 86.8 reduce-scatter.1

commit v2 on v1

--- a/solution.py
+++ b/solution.py
@@ -56,7 +56,8 @@
     partial_term = partial_term.astype(jnp.bfloat16).reshape(
         n_cell, 2 * n_tm * q_local, frames_dev * branches
     )
-    summed = lax.psum_scatter(partial_term, "cell", scatter_dimension=0, tiled=True)
+    gathered = lax.all_to_all(partial_term, "cell", split_axis=0, concat_axis=0, tiled=True)
+    summed = jnp.sum(gathered.astype(jnp.float32), axis=0).astype(jnp.bfloat16)
     blocks = summed.reshape(2, n_tm, q_local, frames_dev, branches)
     collected = lax.all_to_all(blocks, "tm", split_axis=1, concat_axis=3, tiled=True)
     collected = collected.reshape(2, q_local, frames, branches).astype(jnp.float32)

time: 145 us -> 93.8 us (0.65)
  waiting for transfers between devices: 99.3 us -> 51.4 us
  between operations: 13.5 us -> 0.14 us
  starting transfers between devices: 9.09 us -> 18.2 us
  other arithmetic: 9 us -> 12.1 us
  local copies, waits for them, and re-layouts: 6.49 us -> 4.62 us
    reduce_scatter x1 -> x0, waiting for transfers between devices: 86 us -> none  [local(): lax.psum_scatter(partial_term, 'cell', scatter_dimension=0, tiled=True)]
    all_to_all x0 -> x1, waiting for transfers between devices: none -> 38.1 us  [local(): lax.all_to_all(partial_term, 'cell', split_axis=0, concat_axis=0, tiled=T...]
    all_to_all x0 -> x1, starting transfers between devices: none -> 7.61 us  [local(): lax.all_to_all(partial_term, 'cell', split_axis=0, concat_axis=0, tiled=T...]
    reduce_sum x0 -> x1, other arithmetic: none -> 2.45 us  [local(): summed = jnp.sum(gathered.astype(jnp.float32), axis=0).astype(jnp.bfloat16)]
    all_to_all x1, starting transfers between devices: 9.09 us -> 10.6 us  [local(): lax.all_to_all(blocks, 'tm', split_axis=1, concat_axis=3, tiled=True)]
  transfers between devices with their start and end apart: 2 -> 2, of which waited for: 2 -> 2; matrix products, arithmetic and copies ran while one was open for 2% -> 4% of each run, Pallas kernels for 0% -> 0%
where the time goes in v2:
time: 93.8 us; the launch traced here: 93.3 us
  waiting for transfers between devices  51.4 us (55%)
  starting transfers between devices  18.2 us (19%)
  other arithmetic  12.1 us (13%)
  matrix products  6.91 us (7%)
  local copies, waits for them, and re-layouts  4.62 us (5%)
    all_to_all x1, waiting for transfers between devices, local(): lax.all_to_all(partial_term, 'cell', split_axis=0, concat_axis=0, tiled=T...  38.1 us
    all_to_all x1, waiting for transfers between devices, local(): lax.all_to_all(blocks, 'tm', split_axis=1, concat_axis=3, tiled=True)  13.3 us
    all_to_all x1, starting transfers between devices, local(): lax.all_to_all(blocks, 'tm', split_axis=1, concat_axis=3, tiled=True)  10.6 us
    all_to_all x1, starting transfers between devices, local(): lax.all_to_all(partial_term, 'cell', split_axis=0, concat_axis=0, tiled=T...  7.61 us
    convert_element_type x1, other arithmetic, phase_rows(): jnp.cos(angles).astype(jnp.bfloat16)  4.84 us
    dot_general x1, matrix products, local(): jnp.dot(table, velocity_rows, preferred_element_type=jnp.float32)  3.52 us
    dot_general x1, matrix products, local(): projected = jnp.einsum('jts,tw->jsw', amplitude, basis, precision=highest)  2.72 us
    reduce_sum x1, other arithmetic, local(): summed = jnp.sum(gathered.astype(jnp.float32), axis=0).astype(jnp.bfloat16)  2.45 us
  transfers between devices with their start and end apart: 2, of which 2 were waited for; matrix products, arithmetic and copies ran while one was open for 4% of the time, Pallas kernels for 0%

profile of v2, /device:TPU:1, one launch (start us, length us, event | category | flops | bytes accessed | tf_op | source)
XLA Modules:
  0.0 93.3 jit_solution(17800990402073070190)
XLA Ops:
  0.0 0.0 copy-start
  0.0 1.1 %reshape.256 = s32[32,8,2,3]{2,1,0,3:T(8,128)S(1)} reshape(s32[512,3]{0,1:T(4,128)} %param.6) | data formatting | bytes 12288 | tf_op jit(solution)/shard_map/reshape | solution.py:44
  1.2 0.1 copy.15
  1.2 0.3 reshape.257
  1.5 0.1 mul.261
  1.6 0.1 mul.266
  1.7 0.1 mul.271
  1.8 0.8 fusion.33
  2.6 4.8 %cosine_convert_fusion = (bf16[8,1,64,512]{3,2,1,0:T(8,128)(2,1)S(1)}, bf16[8,1,64,512]{3,2,1,0:T(8,128)(2,1)S(1)}) fusion(s32[512]{0:T(512)S(1)} %bitcast.47, s32[8,64]{1,0:T(8,128)S(1)} %mul.271, s32[512]{0:T(512)S(1)} %bitcast.48, s32[8,64]{1,0:T(8,128)S(1)} %mul.266, s32[512]{0:T(512)S(1)} %bitcast.46, s32[8,64]{1,0:T(8,128)S(1)} %mul.261), kind=kLoop, calls=%fused_computation.16 | loop fusion | flops 5505024 | bytes 1060864 | tf_op jit(solution)/shard_map/convert_element_type | solution.py:18
  7.4 0.1 pad_maximum_fusion
  7.5 0.0 copy-done
  7.5 3.5 %convolution_convert_fusion = bf16[1024,1536]{1,0:T(8,128)(2,1)} fusion(bf16[1024,512]{1,0:T(8,128)(2,1)S(1)} %bitcast.45, bf16[512,1536]{0,1:T(8,128)(2,1)S(1)} %bitcast.38), kind=kOutput, calls=%fused_computation | convolution fusion | flops 1612185600 | bytes 5767168 | tf_op jit(solution)/shard_map/dot_general | solution.py:55
  11.0 0.0 copy-start.3
  11.1 7.6 %all-to-all-start = ((bf16[8,128,1536]{2,1,0:T(8,128)(2,1)}), bf16[8,128,1536]{2,1,0:T(8,128)(2,1)}, u32[]{:S(2)}, u32[]{:S(2)}) async-start(bf16[8,128,1536]{2,1,0:T(8,128)(2,1)} %bitcast.41), calls=%async_computation | async-start | bytes 6291456 | tf_op jit(solution)/shard_map/all_to_all | solution.py:59
  18.7 0.0 copy-done.3
  18.7 0.1 copy.23
  18.8 0.6 fusion.31
  19.4 38.1 %all-to-all-done = bf16[8,128,1536]{2,1,0:T(8,128)(2,1)} async-done(((bf16[8,128,1536]{2,1,0:T(8,128)(2,1)}), bf16[8,128,1536]{2,1,0:T(8,128)(2,1)}, u32[]{:S(2)}, u32[]{:S(2)}) %all-to-all-start) | async-done | bytes 3145760 | tf_op jit(solution)/shard_map/all_to_all | solution.py:59
  57.5 2.4 %reduce_sum.12 = bf16[128,1536]{1,0:T(8,128)(2,1)S(1)} reduce(bf16[8,128,1536]{2,1,0:T(8,128)(2,1)} %all-to-all-done, bf16[]{:T(256)} %constant.48.clone.1), dimensions={0}, to_apply=%region_0.1 | reduce | flops 1376256 | bytes 3538946 | tf_op jit(solution)/shard_map/reduce_sum | solution.py:60
  60.0 0.5 reshape.261
  60.4 0.0 copy-start.2
  60.5 0.9 copy.16
  61.3 10.6 %all-to-all-start.1 = ((bf16[2,32,2,16,96]{4,3,2,0,1:T(8,128)(2,1)}), bf16[2,32,2,16,96]{4,3,2,0,1:T(8,128)(2,1)S(1)}, u32[]{:S(2)}, u32[]{:S(2)}) async-start(bf16[2,32,2,16,96]{4,3,2,0,1:T(8,128)(2,1)} %copy.16), calls=%async_computation.1 | async-start | bytes 1048576 | tf_op jit(solution)/shard_map/all_to_all | solution.py:62
  71.9 0.8 fusion.27
  72.7 0.1 copy.22
  72.8 0.3 fusion.24
  73.1 0.0 copy-done.2
  73.1 2.1 %multiply_subtract_fusion = (f32[32,16,512]{2,1,0:T(8,128)S(1)}, f32[32,16,512]{2,1,0:T(8,128)}) fusion(f32[16,512]{1,0:T(8,128)} %get-tuple-element.23, f32[32,512]{1,0:T(8,128)S(1)} %get-tuple-element.21, f32[16,512]{1,0:T(8,128)} %get-tuple-element.24, f32[32,512]{1,0:T(8,128)S(1)} %get-tuple-element.22), kind=kLoop, calls=%fused_computation.14 | loop fusion | flops 1572864 | bytes 2293760 | tf_op jit(solution)/shard_map/sub | solution.py:31
  75.2 13.3 %all-to-all-done.1 = bf16[2,32,2,16,96]{4,3,2,0,1:T(8,128)(2,1)S(1)} async-done(((bf16[2,32,2,16,96]{4,3,2,0,1:T(8,128)(2,1)}), bf16[2,32,2,16,96]{4,3,2,0,1:T(8,128)(2,1)S(1)}, u32[]{:S(2)}, u32[]{:S(2)}) %all-to-all-start.1) | async-done | bytes 393248 | tf_op jit(solution)/shard_map/all_to_all | solution.py:62
  88.5 0.0 copy-start.1
  88.5 0.7 convolution_bitcast_fusion
  89.2 0.5 copy-done.1
  89.7 2.7 %fusion = f32[2,192,1024]{2,1,0:T(8,128)S(1)} fusion(f32[2,512,192]{1,2,0:T(8,128)S(1)} %convolution_bitcast_fusion, f32[512,512]{1,0:T(8,128)S(1)} %bitcast.40, f32[512,512]{1,0:T(8,128)S(1)} %bitcast.39), kind=kOutput, calls=%fused_computation.2 | convolution fusion | flops 2416443392 | bytes 4456448 | tf_op jit(solution)/shard_map/jts,tw->jsw/dot_general | solution.py:76
  92.4 0.9 fusion.8
  (5 shorter events, 0.1 us)
Async XLA Ops:
  0.0 7.5 %copy-start = (bf16[512,16,96]{0,2,1:T(8,128)(2,1)S(1)}, bf16[512,16,96]{0,2,1:T(8,128)(2,1)}, u32[]{:S(2)}) copy-start(bf16[512,16,96]{0,2,1:T(8,128)(2,1)} %param.4) | copy-start | bytes 4718596
  11.0 7.6 %copy-start.3 = (f32[2,2,96,96]{3,2,1,0:T(8,128)S(1)}, f32[2,2,96,96]{3,2,1,0:T(8,128)}, u32[]{:S(2)}) copy-start(f32[2,2,96,96]{3,2,1,0:T(8,128)} %param.7) | copy-start | bytes 442372
  11.1 46.5 %all-to-all-start = ((bf16[8,128,1536]{2,1,0:T(8,128)(2,1)}), bf16[8,128,1536]{2,1,0:T(8,128)(2,1)}, u32[]{:S(2)}, u32[]{:S(2)}) async-start(bf16[8,128,1536]{2,1,0:T(8,128)(2,1)} %bitcast.41), calls=%async_computation | async-start | bytes 6291456 | tf_op jit(solution)/shard_map/all_to_all | solution.py:59
  60.4 12.6 %copy-start.2 = (f32[2,96,96]{1,2,0:T(8,128)S(1)}, f32[2,96,96]{1,2,0:T(8,128)}, u32[]{:S(2)}) copy-start(f32[2,96,96]{1,2,0:T(8,128)} %fusion.31) | copy-start | bytes 221188
  61.3 27.1 %all-to-all-start.1 = ((bf16[2,32,2,16,96]{4,3,2,0,1:T(8,128)(2,1)}), bf16[2,32,2,16,96]{4,3,2,0,1:T(8,128)(2,1)S(1)}, u32[]{:S(2)}, u32[]{:S(2)}) async-start(bf16[2,32,2,16,96]{4,3,2,0,1:T(8,128)(2,1)} %copy.16), calls=%async_computation.1 | async-start | bytes 1048576 | tf_op jit(solution)/shard_map/all_to_all | solution.py:62
  88.5 1.2 %copy-start.1 = (f32[32,16,512]{2,1,0:T(8,128)S(1)}, f32[32,16,512]{2,1,0:T(8,128)}, u32[]{:S(2)}) copy-start(f32[32,16,512]{2,1,0:T(8,128)} %get-tuple-element.9) | copy-start | bytes 3145732

commit v3 on v1

--- a/solution.py
+++ b/solution.py
@@ -13,9 +13,19 @@
         q_coords[:, None, 0] * cell_coords[None, :, 0]
         + q_coords[:, None, 1] * cell_coords[None, :, 1]
         + q_coords[:, None, 2] * cell_coords[None, :, 2]
-    ) % L
-    angles = products.astype(jnp.float32) * (2.0 * math.pi / L)
-    return jnp.cos(angles).astype(jnp.bfloat16), (-jnp.sin(angles)).astype(jnp.bfloat16)
+    )
+    step = jnp.arange(4, dtype=jnp.float32) * (2.0 * math.pi / L)
+    cos_table = jnp.cos(step).astype(jnp.bfloat16)
+    sin_table = (-jnp.sin(step)).astype(jnp.bfloat16)
+    bit0 = (products & 1) != 0
+    bit1 = (products & 2) != 0
+    bit2 = (products & 4) != 0
+    bit3 = (products & 8) != 0
+    real = jnp.where(bit1, jnp.where(bit0, cos_table[3], cos_table[2]), jnp.where(bit0, cos_table[1], cos_table[0]))
+    imag = jnp.where(bit1, jnp.where(bit0, sin_table[3], sin_table[2]), jnp.where(bit0, sin_table[1], sin_table[0]))
+    real, imag = jnp.where(bit2, imag, real), jnp.where(bit2, -real, imag)
+    real, imag = jnp.where(bit3, -real, real), jnp.where(bit3, -imag, imag)
+    return jnp.stack([real, imag], axis=1)
 
 
 def twiddles(frames):
@@ -36,30 +46,20 @@
 def local(velocity, cell_coords, q_coords, eigvecs):
     n_tm = lax.axis_size("tm")
     n_cell = lax.axis_size("cell")
+    n_dev = n_tm * n_cell
     cell_dev, frames_dev, branches = velocity.shape
     q_total = q_coords.shape[0]
-    q_local = q_total // (n_tm * n_cell)
+    q_local = q_total // n_dev
     frames = frames_dev * n_tm
-    ordered_coords = (
-        q_coords.reshape(n_tm, n_cell, q_local, 3).transpose(1, 0, 2, 3).reshape(q_total, 3)
-    )
-    cos_rows, sin_rows = phase_rows(ordered_coords, cell_coords)
-    table = jnp.stack(
-        [
-            cos_rows.reshape(n_cell, n_tm * q_local, cell_dev),
-            sin_rows.reshape(n_cell, n_tm * q_local, cell_dev),
-        ],
-        axis=1,
-    ).reshape(2 * q_total, cell_dev)
-    velocity_rows = velocity.reshape(cell_dev, frames_dev * branches)
-    partial_term = jnp.dot(table, velocity_rows, preferred_element_type=jnp.float32)
-    partial_term = partial_term.astype(jnp.bfloat16).reshape(
-        n_cell, 2 * n_tm * q_local, frames_dev * branches
-    )
-    summed = lax.psum_scatter(partial_term, "cell", scatter_dimension=0, tiled=True)
-    blocks = summed.reshape(2, n_tm, q_local, frames_dev, branches)
-    collected = lax.all_to_all(blocks, "tm", split_axis=1, concat_axis=3, tiled=True)
-    collected = collected.reshape(2, q_local, frames, branches).astype(jnp.float32)
+    frames_each = frames_dev // n_cell
+    spread = velocity.reshape(cell_dev, n_cell, frames_each * branches)
+    all_cells = lax.all_to_all(spread, "cell", split_axis=1, concat_axis=0, tiled=True)
+    all_cells = all_cells.reshape(cell_dev * n_cell, frames_each * branches)
+    all_coords = lax.all_gather(cell_coords, "cell", axis=0, tiled=True)
+    table = phase_rows(q_coords, all_coords).reshape(2 * q_total, cell_dev * n_cell)
+    modes = jnp.dot(table, all_cells, preferred_element_type=jnp.float32)
+    modes = modes.astype(jnp.bfloat16).reshape(n_dev, q_local, 2, frames_each, branches)
+    collected = lax.all_to_all(modes, ("tm", "cell"), split_axis=0, concat_axis=0, tiled=True)
 
     scale = 1.0 / math.sqrt(cell_dev * n_cell)
     e_real = eigvecs[:, 0] * scale
@@ -69,7 +69,9 @@
         axis=1,
     )
     highest = lax.Precision.HIGHEST
-    amplitude = jnp.einsum("rjtk,jrks->jts", collected, e_block, precision=highest)
+    amplitude = jnp.einsum(
+        "sjrfk,jrkc->jsfc", collected.astype(jnp.float32), e_block, precision=highest
+    ).reshape(q_local, frames, 2 * branches)
     cosines, sines = twiddles(frames)
     basis = jnp.concatenate([cosines, sines], axis=1)
     projected = jnp.einsum("jts,tw->jsw", amplitude, basis, precision=highest)

time: 145 us -> 153 us (1.055)
  waiting for transfers between devices: 99.3 us -> 19.2 us
  blocking collectives: 0 us -> 42 us
  local copies, waits for them, and re-layouts: 6.49 us -> 35.2 us
  starting transfers between devices: 9.09 us -> 23.6 us
  between operations: 13.5 us -> 0.14 us
  other arithmetic: 9 us -> 21.8 us
  matrix products: 6.89 us -> 10.7 us
    reduce_scatter x1 -> x0, waiting for transfers between devices: 86 us -> none  [local(): lax.psum_scatter(partial_term, 'cell', scatter_dimension=0, tiled=True)]
    all_gather x0 -> x1, blocking collectives: none -> 42 us  [local(): all_coords = lax.all_gather(cell_coords, 'cell', axis=0, tiled=True)]
    another operation x0 -> x1, local copies, waits for them, and re-layouts: none -> 16.4 us  [phase_rows(): return jnp.stack([real, imag], axis=1)]
    all_to_all x1 -> x2, starting transfers between devices: 9.09 us -> 23.6 us  [the longest x1 16.1 us: local(): lax.all_to_all(modes, ('tm', 'cell'), split_axis=0, concat_axis=0, tiled=...]
    select_n x0 -> x1, other arithmetic: none -> 13.9 us  [phase_rows(): real, imag = (jnp.where(bit3, -real, real), jnp.where(bit3, -imag, imag))]
    reshape x4 -> x3, local copies, waits for them, and re-layouts: 3.71 us -> 14.6 us  [the longest x1 13.2 us: local(): phase_rows(q_coords, all_coords).reshape(2 * q_total, cell_dev * n_cell)]
    another operation x1, other arithmetic: 0.1 us -> 6.17 us  [phase_rows(): return jnp.stack([real, imag], axis=1)]
    all_to_all x1 -> x2, waiting for transfers between devices: 13.3 us -> 19.2 us  [the longest x1 19.2 us: local(): lax.all_to_all(modes, ('tm', 'cell'), split_axis=0, concat_axis=0, tiled=...]
  transfers between devices with their start and end apart: 2 -> 2, of which waited for: 2 -> 1; matrix products, arithmetic and copies ran while one was open for 2% -> 35% of each run, Pallas kernels for 0% -> 0%
where the time goes in v3:
time: 153 us
  blocking collectives  42 us (27%)
  local copies, waits for them, and re-layouts  35.2 us (23%)
  starting transfers between devices  23.6 us (15%)
  other arithmetic  21.8 us (14%)
  waiting for transfers between devices  19.2 us (13%)
  matrix products  10.7 us (7%)
    all_gather x1, blocking collectives, local(): all_coords = lax.all_gather(cell_coords, 'cell', axis=0, tiled=True)  42 us
    all_to_all x1, waiting for transfers between devices, local(): lax.all_to_all(modes, ('tm', 'cell'), split_axis=0, concat_axis=0, tiled=...  19.2 us
    another operation x1, local copies, waits for them, and re-layouts, phase_rows(): return jnp.stack([real, imag], axis=1)  16.4 us
    all_to_all x1, starting transfers between devices, local(): lax.all_to_all(modes, ('tm', 'cell'), split_axis=0, concat_axis=0, tiled=...  16.1 us
    select_n x1, other arithmetic, phase_rows(): real, imag = (jnp.where(bit3, -real, real), jnp.where(bit3, -imag, imag))  13.9 us
    reshape x1, local copies, waits for them, and re-layouts, local(): phase_rows(q_coords, all_coords).reshape(2 * q_total, cell_dev * n_cell)  13.2 us
    all_to_all x1, starting transfers between devices, local(): lax.all_to_all(spread, 'cell', split_axis=1, concat_axis=0, tiled=True)  7.48 us
    dot_general x1, matrix products, local(): modes = jnp.dot(table, all_cells, preferred_element_type=jnp.float32)  6.34 us
  transfers between devices with their start and end apart: 2, of which 1 were waited for; matrix products, arithmetic and copies ran while one was open for 35% of the time, Pallas kernels for 0%

profile of v3, /device:TPU:1, one launch (start us, length us, event | category | flops | bytes accessed | tf_op | source)
XLA Modules:
  0.0 152.7 jit_solution(2938117541314478069)
XLA Ops:
  0.0 7.5 %all-to-all-start = ((bf16[512,8,192]{0,2,1:T(8,128)(2,1)}), bf16[512,8,192]{0,2,1:T(8,128)(2,1)S(1)}, u32[]{:S(2)}, u32[]{:S(2)}) async-start(bf16[512,8,192]{0,2,1:T(8,128)(2,1)} %bitcast.57), calls=%async_computation | async-start | bytes 3145728 | tf_op jit(solution)/shard_map/all_to_all | solution.py:56
  7.6 0.6 fusion.34
  8.2 0.7 fusion.33
  8.9 42.0 %all_gather.3 = s32[4096,3]{0,1:T(4,128)S(1)} all-gather(s32[512,3]{0,1:T(4,128)} %param.5), channel_id=1, replica_groups=mesh['tm'=32,'cell'=8] {'cell'}, dimensions={0}, use_global_device_ids=true | all-gather | bytes 55296 | tf_op jit(solution)/shard_map/all_gather | solution.py:58
  50.9 0.8 fusion.32
  51.7 13.9 %negate_select_fusion.1 = (bf16[512,1,4096]{2,0,1:T(8,128)(2,1)S(1)}, bf16[512,1,4096]{2,0,1:T(8,128)(2,1)}) fusion(bf16[]{:T(256)} %bitcast.13, bf16[]{:T(256)} %bitcast.12, bf16[]{:T(256)} %bitcast.11, bf16[]{:T(256)} %bitcast.10, bf16[]{:T(256)} %bitcast.9, bf16[]{:T(256)} %bitcast.8, bf16[]{:T(256)} %bitcast.7, bf16[]{:T(256)} %bitcast.6, ...), kind=kLoop, calls=%fused_computation.7 | loop fusion | flops 67108864 | bytes 8443920 | tf_op jit(solution)/shard_map/jit(_where)/select_n | solution.py:27
  65.6 6.2 %pad_maximum_fusion = bf16[512,2,4096]{2,0,1:T(8,128)(2,1)} fusion(bf16[512,1,4096]{2,0,1:T(8,128)(2,1)} %get-tuple-element.15, bf16[512,1,4096]{2,0,1:T(8,128)(2,1)S(1)} %get-tuple-element.14), kind=kLoop, calls=%fused_computation | loop fusion | flops 4194304 | bytes 16777216 | tf_op jit(solution)/shard_map/stack | solution.py:28
  71.7 16.4 %copy.35 = bf16[512,2,4096]{2,1,0:T(2,128)(2,1)} copy(bf16[512,2,4096]{2,0,1:T(8,128)(2,1)} %pad_maximum_fusion) | data formatting | bytes 16777216 | tf_op jit(solution)/shard_map/stack | solution.py:28
  88.1 0.0 copy-start
  88.1 13.2 %reshape.499 = bf16[1024,4096]{1,0:T(8,128)(2,1)} reshape(bf16[512,2,4096]{2,1,0:T(2,128)(2,1)} %copy.35) | data formatting | bytes 16777216 | tf_op jit(solution)/shard_map/reshape | solution.py:59
  101.3 0.0 copy-done
  101.3 0.1 copy.48
  101.4 0.0 all-to-all-done
  101.5 0.2 copy.49
  101.6 6.3 %convolution_convert_fusion = bf16[1024,192]{0,1:T(8,128)(2,1)S(1)} fusion(bf16[1024,4096]{1,0:T(8,128)(2,1)} %reshape.499, bf16[4096,192]{0,1:T(8,128)(2,1)S(1)} %bitcast.58), kind=kOutput, calls=%fused_computation.15 | convolution fusion | flops 1610809344 | bytes 10354688 | tf_op jit(solution)/shard_map/dot_general | solution.py:60
  108.0 0.2 copy.37
  108.2 0.3 reshape.502
  108.5 1.2 copy.38
  109.6 16.1 %all-to-all-start.1 = ((bf16[256,2,2,2,96]{4,2,3,1,0:T(2,128)(2,1)}), bf16[256,2,2,2,96]{4,2,3,1,0:T(2,128)(2,1)S(1)}, u32[]{:S(2)}, u32[]{:S(2)}) async-start(bf16[256,2,2,2,96]{4,2,3,1,0:T(2,128)(2,1)} %copy.38), calls=%async_computation.1 | async-start | bytes 1048576 | tf_op jit(solution)/shard_map/all_to_all | solution.py:62
  125.8 0.1 fusion.25
  125.9 0.1 copy.47
  126.0 0.3 fusion.22
  126.4 0.3 multiply_subtract_fusion
  126.7 19.2 %all-to-all-done.1 = bf16[256,2,2,2,96]{4,2,3,1,0:T(2,128)(2,1)S(1)} async-done(((bf16[256,2,2,2,96]{4,2,3,1,0:T(2,128)(2,1)}), bf16[256,2,2,2,96]{4,2,3,1,0:T(2,128)(2,1)S(1)}, u32[]{:S(2)}, u32[]{:S(2)}) %all-to-all-start.1) | async-done | bytes 393248 | tf_op jit(solution)/shard_map/all_to_all | solution.py:62
  145.9 1.6 %convolution_bitcast_fusion = f32[2,256,2,192]{1,3,2,0:T(8,128)} fusion(bf16[256,2,2,2,96]{4,2,3,1,0:T(2,128)(2,1)S(1)} %all-to-all-done.1, f32[2,1,96,192]{2,3,1,0:T(8,128)S(1)} %get-tuple-element.10, f32[2,1,96,192]{2,3,1,0:T(8,128)S(1)} %get-tuple-element.9), kind=kOutput, calls=%fused_computation.14 | convolution fusion | flops 453058560 | bytes 1474560 | tf_op jit(solution)/shard_map/sjrfk,jrkc->jsfc/dot_general | solution.py:72
  147.5 1.5 %copy.43 = f32[2,256,2,192]{3,0,2,1:T(2,128)S(1)} copy(f32[2,256,2,192]{1,3,2,0:T(8,128)} %convolution_bitcast_fusion) | data formatting | bytes 1572864 | tf_op jit(solution)/shard_map/sjrfk,jrkc->jsfc/dot_general | solution.py:72
  149.0 2.7 %fusion = f32[2,192,1024]{2,1,0:T(8,128)S(1)} fusion(f32[512,512]{1,0:T(8,128)S(1)} %bitcast.56, f32[512,512]{1,0:T(8,128)S(1)} %bitcast.55, f32[2,512,192]{2,0,1:T(2,128)S(1)} %bitcast.54), kind=kOutput, calls=%fused_computation.11 | convolution fusion | flops 2416443392 | bytes 4456448 | tf_op jit(solution)/shard_map/jts,tw->jsw/dot_general | solution.py:77
  151.8 0.9 fusion.7
  (7 shorter events, 0.2 us)
Async XLA Ops:
  0.0 101.4 %all-to-all-start = ((bf16[512,8,192]{0,2,1:T(8,128)(2,1)}), bf16[512,8,192]{0,2,1:T(8,128)(2,1)S(1)}, u32[]{:S(2)}, u32[]{:S(2)}) async-start(bf16[512,8,192]{0,2,1:T(8,128)(2,1)} %bitcast.57), calls=%async_computation | async-start | bytes 3145728 | tf_op jit(solution)/shard_map/all_to_all | solution.py:56
  88.1 13.2 %copy-start = (f32[2,2,96,96]{3,2,1,0:T(8,128)S(1)}, f32[2,2,96,96]{3,2,1,0:T(8,128)}, u32[]{:S(2)}) copy-start(f32[2,2,96,96]{3,2,1,0:T(8,128)} %param.7) | copy-start | bytes 442372
  109.6 36.3 %all-to-all-start.1 = ((bf16[256,2,2,2,96]{4,2,3,1,0:T(2,128)(2,1)}), bf16[256,2,2,2,96]{4,2,3,1,0:T(2,128)(2,1)S(1)}, u32[]{:S(2)}, u32[]{:S(2)}) async-start(bf16[256,2,2,2,96]{4,2,3,1,0:T(2,128)(2,1)} %copy.38), calls=%async_computation.1 | async-start | bytes 1048576 | tf_op jit(solution)/shard_map/all_to_all | solution.py:62

commit v4 on v3

--- a/solution.py
+++ b/solution.py
@@ -8,11 +8,12 @@
 L = 16
 
 
-def phase_rows(q_coords, cell_coords):
+def phase_rows(q_coords, cell_code):
+    code = cell_code.astype(jnp.int32)
     products = (
-        q_coords[:, None, 0] * cell_coords[None, :, 0]
-        + q_coords[:, None, 1] * cell_coords[None, :, 1]
-        + q_coords[:, None, 2] * cell_coords[None, :, 2]
+        q_coords[:, None, 0] * (code[None, :] // (L * L))
+        + q_coords[:, None, 1] * (code[None, :] // L % L)
+        + q_coords[:, None, 2] * (code[None, :] % L)
     )
     step = jnp.arange(4, dtype=jnp.float32) * (2.0 * math.pi / L)
     cos_table = jnp.cos(step).astype(jnp.bfloat16)
@@ -25,7 +26,7 @@
     imag = jnp.where(bit1, jnp.where(bit0, sin_table[3], sin_table[2]), jnp.where(bit0, sin_table[1], sin_table[0]))
     real, imag = jnp.where(bit2, imag, real), jnp.where(bit2, -real, imag)
     real, imag = jnp.where(bit3, -real, real), jnp.where(bit3, -imag, imag)
-    return jnp.stack([real, imag], axis=1)
+    return jnp.stack([real, imag], axis=0)
 
 
 def twiddles(frames):
@@ -53,13 +54,15 @@
     frames = frames_dev * n_tm
     frames_each = frames_dev // n_cell
     spread = velocity.reshape(cell_dev, n_cell, frames_each * branches)
+    cell_code = (cell_coords[:, 0] * (L * L) + cell_coords[:, 1] * L + cell_coords[:, 2]).astype(jnp.float32)
+    all_code = lax.all_gather(cell_code, "cell", axis=0, tiled=True)
+    all_code, spread = lax.optimization_barrier((all_code, spread))
     all_cells = lax.all_to_all(spread, "cell", split_axis=1, concat_axis=0, tiled=True)
     all_cells = all_cells.reshape(cell_dev * n_cell, frames_each * branches)
-    all_coords = lax.all_gather(cell_coords, "cell", axis=0, tiled=True)
-    table = phase_rows(q_coords, all_coords).reshape(2 * q_total, cell_dev * n_cell)
+    table = phase_rows(q_coords, all_code).reshape(2 * q_total, cell_dev * n_cell)
     modes = jnp.dot(table, all_cells, preferred_element_type=jnp.float32)
-    modes = modes.astype(jnp.bfloat16).reshape(n_dev, q_local, 2, frames_each, branches)
-    collected = lax.all_to_all(modes, ("tm", "cell"), split_axis=0, concat_axis=0, tiled=True)
+    modes = modes.astype(jnp.bfloat16).reshape(2, n_dev, q_local, frames_each, branches)
+    collected = lax.all_to_all(modes, ("tm", "cell"), split_axis=1, concat_axis=1, tiled=True)
 
     scale = 1.0 / math.sqrt(cell_dev * n_cell)
     e_real = eigvecs[:, 0] * scale
@@ -70,7 +73,7 @@
     )
     highest = lax.Precision.HIGHEST
     amplitude = jnp.einsum(
-        "sjrfk,jrkc->jsfc", collected.astype(jnp.float32), e_block, precision=highest
+        "rsjfk,jrkc->jsfc", collected.astype(jnp.float32), e_block, precision=highest
     ).reshape(q_local, frames, 2 * branches)
     cosines, sines = twiddles(frames)
     basis = jnp.concatenate([cosines, sines], axis=1)

time: 153 us -> 113 us (0.74)
  local copies, waits for them, and re-layouts: 35.2 us -> 6.07 us
  blocking collectives: 42 us -> 26.3 us
  other arithmetic: 21.8 us -> 24.3 us
  starting transfers between devices: 23.6 us -> 25.8 us
    another operation x1 -> x0, local copies, waits for them, and re-layouts: 16.4 us -> none  [phase_rows(): return jnp.stack([real, imag], axis=1)]
    all_gather x1, blocking collectives: 42 us -> 26.3 us  [local(): all_code = lax.all_gather(cell_code, 'cell', axis=0, tiled=True)]
    reshape x3 -> x2, local copies, waits for them, and re-layouts: 14.6 us -> 1.89 us  [local(): modes.astype(jnp.bfloat16).reshape(2, n_dev, q_local, frames_each, branches)]
    all_to_all x1, starting transfers between devices: 16.1 us -> 20.6 us  [local(): lax.all_to_all(modes, ('tm', 'cell'), split_axis=1, concat_axis=1, tiled=...]
    all_to_all x1, starting transfers between devices: 7.48 us -> 5.25 us  [local(): lax.all_to_all(spread, 'cell', split_axis=1, concat_axis=0, tiled=True)]
  transfers between devices with their start and end apart: 2 -> 2, of which waited for: 1 -> 1; matrix products, arithmetic and copies ran while one was open for 35% -> 22% of each run, Pallas kernels for 0% -> 0%
where the time goes in v4:
time: 113 us
  blocking collectives  26.3 us (23%)
  starting transfers between devices  25.8 us (23%)
  other arithmetic  24.3 us (22%)
  waiting for transfers between devices  19.2 us (17%)
  matrix products  10.7 us (9%)
  local copies, waits for them, and re-layouts  6.07 us (5%)
    all_gather x1, blocking collectives, local(): all_code = lax.all_gather(cell_code, 'cell', axis=0, tiled=True)  26.3 us
    all_to_all x1, starting transfers between devices, local(): lax.all_to_all(modes, ('tm', 'cell'), split_axis=1, concat_axis=1, tiled=...  20.6 us
    all_to_all x1, waiting for transfers between devices, local(): lax.all_to_all(modes, ('tm', 'cell'), split_axis=1, concat_axis=1, tiled=...  19.2 us
    select_n x1, other arithmetic, phase_rows(): real, imag = (jnp.where(bit3, -real, real), jnp.where(bit3, -imag, imag))  14.2 us
    another operation x1, other arithmetic, phase_rows(): return jnp.stack([real, imag], axis=0)  7.45 us
    dot_general x1, matrix products, local(): modes = jnp.dot(table, all_cells, preferred_element_type=jnp.float32)  6.33 us
    all_to_all x1, starting transfers between devices, local(): lax.all_to_all(spread, 'cell', split_axis=1, concat_axis=0, tiled=True)  5.25 us
    dot_general x1, matrix products, local(): projected = jnp.einsum('jts,tw->jsw', amplitude, basis, precision=highest)  2.74 us
  transfers between devices with their start and end apart: 2, of which 1 were waited for; matrix products, arithmetic and copies ran while one was open for 22% of the time, Pallas kernels for 0%

profile of v4, /device:TPU:1, one launch (start us, length us, event | category | flops | bytes accessed | tf_op | source)
XLA Modules:
  0.0 112.5 jit_solution(1343114290811417789)
XLA Ops:
  0.0 0.8 add_convert_fusion
  0.8 26.3 %all-gather = f32[4096,1]{0,1:T(1,128)S(1)} all-gather(f32[512,1]{0,1:T(1,128)S(1)} %add_convert_fusion), channel_id=2, replica_groups=mesh['tm'=32,'cell'=8] {'cell'}, dimensions={0}, use_global_device_ids=true | all-gather | bytes 18432 | tf_op jit(solution)/shard_map/all_gather | solution.py:58
  27.1 5.3 %all-to-all-start = ((bf16[512,8,192]{0,2,1:T(8,128)(2,1)}), bf16[512,8,192]{0,2,1:T(8,128)(2,1)S(1)}, u32[]{:S(2)}, u32[]{:S(2)}) async-start(bf16[512,8,192]{0,2,1:T(8,128)(2,1)} %bitcast.57), calls=%async_computation | async-start | bytes 3145728 | tf_op jit(solution)/shard_map/all_to_all | solution.py:60
  32.5 0.6 fusion.37
  33.1 0.7 fusion.36
  33.8 0.8 fusion.35
  34.6 0.0 copy-start
  34.6 14.2 %negate_select_fusion.1 = (bf16[1,512,4096]{2,1,0:T(8,128)(2,1)}, bf16[1,512,4096]{2,1,0:T(8,128)(2,1)}) fusion(bf16[]{:T(256)} %bitcast.12, bf16[]{:T(256)} %bitcast.11, bf16[]{:T(256)} %bitcast.10, bf16[]{:T(256)} %bitcast.9, bf16[]{:T(256)} %bitcast.8, bf16[]{:T(256)} %bitcast.7, bf16[]{:T(256)} %bitcast.6, bf16[]{:T(256)} %bitcast.5, ...), kind=kLoop, calls=%fused_computation.7 | loop fusion | flops 67108864 | bytes 8443920 | tf_op jit(solution)/shard_map/jit(_where)/select_n | solution.py:28
  48.8 0.0 copy-done
  48.9 0.1 copy.29
  49.0 7.4 %pad_maximum_fusion = bf16[2,512,4096]{2,1,0:T(8,128)(2,1)} fusion(bf16[1,512,4096]{2,1,0:T(8,128)(2,1)} %get-tuple-element.16, bf16[1,512,4096]{2,1,0:T(8,128)(2,1)} %get-tuple-element.15), kind=kLoop, calls=%fused_computation | loop fusion | flops 4194304 | bytes 16777216 | tf_op jit(solution)/shard_map/stack | solution.py:29
  56.4 0.0 all-to-all-done
  56.4 0.2 copy.30
  56.6 6.3 %convolution_convert_fusion = bf16[1024,192]{0,1:T(8,128)(2,1)S(1)} fusion(bf16[1024,4096]{1,0:T(8,128)(2,1)} %bitcast.52, bf16[4096,192]{0,1:T(8,128)(2,1)S(1)} %bitcast.58), kind=kOutput, calls=%fused_computation.15 | convolution fusion | flops 1610809344 | bytes 10354688 | tf_op jit(solution)/shard_map/dot_general | solution.py:63
  62.9 0.2 copy.18
  63.1 0.3 reshape.535
  63.4 1.6 %copy.19 = bf16[2,256,2,2,96]{4,0,3,2,1:T(2,128)(2,1)} copy(bf16[2,256,2,2,96]{4,3,2,1,0:T(2,128)(2,1)S(1)} %reshape.535) | data formatting | bytes 786432 | tf_op jit(solution)/shard_map/reshape | solution.py:64
  65.0 20.6 %all-to-all-start.1 = ((bf16[2,256,2,2,96]{4,0,3,2,1:T(2,128)(2,1)}), bf16[2,256,2,2,96]{4,0,3,2,1:T(2,128)(2,1)S(1)}, u32[]{:S(2)}, u32[]{:S(2)}) async-start(bf16[2,256,2,2,96]{4,0,3,2,1:T(2,128)(2,1)} %copy.19), calls=%async_computation.1 | async-start | bytes 1048576 | tf_op jit(solution)/shard_map/all_to_all | solution.py:65
  85.6 0.1 fusion.27
  85.8 0.1 copy.28
  85.9 0.3 fusion.22
  86.2 0.3 multiply_subtract_fusion
  86.5 19.2 %all-to-all-done.1 = bf16[2,256,2,2,96]{4,0,3,2,1:T(2,128)(2,1)S(1)} async-done(((bf16[2,256,2,2,96]{4,0,3,2,1:T(2,128)(2,1)}), bf16[2,256,2,2,96]{4,0,3,2,1:T(2,128)(2,1)S(1)}, u32[]{:S(2)}, u32[]{:S(2)}) %all-to-all-start.1) | async-done | bytes 393248 | tf_op jit(solution)/shard_map/all_to_all | solution.py:65
  105.7 1.6 %convolution_bitcast_fusion = f32[2,256,2,192]{1,3,2,0:T(8,128)} fusion(bf16[2,256,2,2,96]{4,0,3,2,1:T(2,128)(2,1)S(1)} %all-to-all-done.1, f32[2,1,96,192]{2,3,1,0:T(8,128)S(1)} %get-tuple-element.14, f32[2,1,96,192]{2,3,1,0:T(8,128)S(1)} %get-tuple-element.13), kind=kOutput, calls=%fused_computation.14 | convolution fusion | flops 453058560 | bytes 1474560 | tf_op jit(solution)/shard_map/rsjfk,jrkc->jsfc/dot_general | solution.py:75
  107.3 1.5 %copy.24 = f32[2,256,2,192]{3,0,2,1:T(2,128)S(1)} copy(f32[2,256,2,192]{1,3,2,0:T(8,128)} %convolution_bitcast_fusion) | data formatting | bytes 1572864 | tf_op jit(solution)/shard_map/rsjfk,jrkc->jsfc/dot_general | solution.py:75
  108.9 2.7 %fusion = f32[2,192,1024]{2,1,0:T(8,128)S(1)} fusion(f32[512,512]{1,0:T(8,128)S(1)} %bitcast.56, f32[512,512]{1,0:T(8,128)S(1)} %bitcast.55, f32[2,512,192]{2,0,1:T(2,128)S(1)} %bitcast.54), kind=kOutput, calls=%fused_computation.11 | convolution fusion | flops 2416443392 | bytes 4456448 | tf_op jit(solution)/shard_map/jts,tw->jsw/dot_general | solution.py:80
  111.6 0.9 fusion.7
  (7 shorter events, 0.2 us)
Async XLA Ops:
  27.1 29.3 %all-to-all-start = ((bf16[512,8,192]{0,2,1:T(8,128)(2,1)}), bf16[512,8,192]{0,2,1:T(8,128)(2,1)S(1)}, u32[]{:S(2)}, u32[]{:S(2)}) async-start(bf16[512,8,192]{0,2,1:T(8,128)(2,1)} %bitcast.57), calls=%async_computation | async-start | bytes 3145728 | tf_op jit(solution)/shard_map/all_to_all | solution.py:60
  34.6 14.3 %copy-start = (f32[2,2,96,96]{3,2,1,0:T(8,128)S(1)}, f32[2,2,96,96]{3,2,1,0:T(8,128)}, u32[]{:S(2)}) copy-start(f32[2,2,96,96]{3,2,1,0:T(8,128)} %param.7) | copy-start | bytes 442372
  65.0 40.7 %all-to-all-start.1 = ((bf16[2,256,2,2,96]{4,0,3,2,1:T(2,128)(2,1)}), bf16[2,256,2,2,96]{4,0,3,2,1:T(2,128)(2,1)S(1)}, u32[]{:S(2)}, u32[]{:S(2)}) async-start(bf16[2,256,2,2,96]{4,0,3,2,1:T(2,128)(2,1)} %copy.19), calls=%async_computation.1 | async-start | bytes 1048576 | tf_op jit(solution)/shard_map/all_to_all | solution.py:65

commit v5 on v2

--- a/solution.py
+++ b/solution.py
@@ -13,9 +13,19 @@
         q_coords[:, None, 0] * cell_coords[None, :, 0]
         + q_coords[:, None, 1] * cell_coords[None, :, 1]
         + q_coords[:, None, 2] * cell_coords[None, :, 2]
-    ) % L
-    angles = products.astype(jnp.float32) * (2.0 * math.pi / L)
-    return jnp.cos(angles).astype(jnp.bfloat16), (-jnp.sin(angles)).astype(jnp.bfloat16)
+    )
+    step = jnp.arange(4, dtype=jnp.float32) * (2.0 * math.pi / L)
+    cos_table = jnp.cos(step).astype(jnp.bfloat16)
+    sin_table = (-jnp.sin(step)).astype(jnp.bfloat16)
+    bit0 = (products & 1) != 0
+    bit1 = (products & 2) != 0
+    bit2 = (products & 4) != 0
+    bit3 = (products & 8) != 0
+    real = jnp.where(bit1, jnp.where(bit0, cos_table[3], cos_table[2]), jnp.where(bit0, cos_table[1], cos_table[0]))
+    imag = jnp.where(bit1, jnp.where(bit0, sin_table[3], sin_table[2]), jnp.where(bit0, sin_table[1], sin_table[0]))
+    real, imag = jnp.where(bit2, imag, real), jnp.where(bit2, -real, imag)
+    real, imag = jnp.where(bit3, -real, real), jnp.where(bit3, -imag, imag)
+    return real, imag
 
 
 def twiddles(frames):
@@ -73,7 +83,7 @@
     amplitude = jnp.einsum("rjtk,jrks->jts", collected, e_block, precision=highest)
     cosines, sines = twiddles(frames)
     basis = jnp.concatenate([cosines, sines], axis=1)
-    projected = jnp.einsum("jts,tw->jsw", amplitude, basis, precision=highest)
+    projected = jnp.einsum("jts,tw->jsw", amplitude, basis, precision=lax.Precision.HIGH)
     on_cos = projected[:, :, :frames]
     on_sin = projected[:, :, frames:]
     out_real = on_cos[:, :branches] + on_sin[:, branches:]

time: 93.8 us -> 95.2 us (1.015)
  other arithmetic: 12.1 us -> 13.4 us
  local copies, waits for them, and re-layouts: 4.62 us -> 5.8 us
  matrix products: 6.91 us -> 5.77 us
    select_n x0 -> x1, other arithmetic: none -> 6.06 us  [phase_rows(): real, imag = (jnp.where(bit3, -real, real), jnp.where(bit3, -imag, imag))]
    convert_element_type x1 -> x2, other arithmetic: 4.84 us -> 0.09 us  [the longest x1 0.05 us: phase_rows(): sin_table = (-jnp.sin(step)).astype(jnp.bfloat16)]
    slice x0 -> x2, local copies, waits for them, and re-layouts: none -> 1.28 us  [the longest x1 0.67 us: phase_rows(): cos_table[3]]
    dot_general x1, matrix products: 2.72 us -> 1.57 us  [local(): jnp.einsum('jts,tw->jsw', amplitude, basis, precision=lax.Precision.HIGH)]
where the time goes in v5:
time: 95.2 us; the launch traced here: 94.7 us
  waiting for transfers between devices  51.4 us (54%)
  starting transfers between devices  18.2 us (19%)
  other arithmetic  13.4 us (14%)
  local copies, waits for them, and re-layouts  5.8 us (6%)
  matrix products  5.77 us (6%)
    all_to_all x1, waiting for transfers between devices, local(): lax.all_to_all(partial_term, 'cell', split_axis=0, concat_axis=0, tiled=T...  38.1 us
    all_to_all x1, waiting for transfers between devices, local(): lax.all_to_all(blocks, 'tm', split_axis=1, concat_axis=3, tiled=True)  13.3 us
    all_to_all x1, starting transfers between devices, local(): lax.all_to_all(blocks, 'tm', split_axis=1, concat_axis=3, tiled=True)  10.6 us
    all_to_all x1, starting transfers between devices, local(): lax.all_to_all(partial_term, 'cell', split_axis=0, concat_axis=0, tiled=T...  7.61 us
    select_n x1, other arithmetic, phase_rows(): real, imag = (jnp.where(bit3, -real, real), jnp.where(bit3, -imag, imag))  6.06 us
    dot_general x1, matrix products, local(): jnp.dot(table, velocity_rows, preferred_element_type=jnp.float32)  3.52 us
    reduce_sum x1, other arithmetic, local(): summed = jnp.sum(gathered.astype(jnp.float32), axis=0).astype(jnp.bfloat16)  2.45 us
    sub x1, other arithmetic, twiddles(): cosines = (cos_c * cos_f - sin_c * sin_f).reshape(frames, frames)  2.06 us
  transfers between devices with their start and end apart: 2, of which 2 were waited for; matrix products, arithmetic and copies ran while one was open for 4% of the time, Pallas kernels for 0%

profile of v5, /device:TPU:1, one launch (start us, length us, event | category | flops | bytes accessed | tf_op | source)
XLA Modules:
  0.0 94.7 jit_solution(3651239005918099298)
XLA Ops:
  0.0 0.0 copy-start
  0.1 0.7 fusion.32
  0.8 0.6 fusion.31
  1.4 1.0 %reshape.265 = s32[32,8,2,3]{2,1,0,3:T(8,128)S(1)} reshape(s32[512,3]{0,1:T(4,128)} %param.6) | data formatting | bytes 12288 | tf_op jit(solution)/shard_map/reshape | solution.py:54
  2.4 0.1 copy.15
  2.5 0.3 reshape.266
  2.8 0.1 mul.247
  2.9 0.1 mul.252
  2.9 0.1 mul.257
  3.0 0.8 fusion.30
  3.8 6.1 %negate_select_fusion.1 = (bf16[8,1,64,512]{3,2,1,0:T(8,128)(2,1)S(1)}, bf16[8,1,64,512]{3,2,1,0:T(8,128)(2,1)S(1)}) fusion(bf16[]{:T(256)} %bitcast.11, bf16[]{:T(256)} %bitcast.10, bf16[]{:T(256)} %bitcast.9, bf16[]{:T(256)} %bitcast.8, bf16[]{:T(256)} %bitcast.7, bf16[]{:T(256)} %bitcast.6, bf16[]{:T(256)} %bitcast.5, bf16[]{:T(256)} %bitcast.4, ...), kind=kLoop, calls=%fused_computation.15 | loop fusion | flops 8388608 | bytes 1060880 | tf_op jit(solution)/shard_map/jit(_where)/select_n | solution.py:27
  9.9 0.1 pad_maximum_fusion
  10.0 0.0 copy-done
  10.0 3.5 %convolution_convert_fusion = bf16[1024,1536]{1,0:T(8,128)(2,1)} fusion(bf16[1024,512]{1,0:T(8,128)(2,1)S(1)} %bitcast.53, bf16[512,1536]{0,1:T(8,128)(2,1)S(1)} %bitcast.46), kind=kOutput, calls=%fused_computation | convolution fusion | flops 1612185600 | bytes 5767168 | tf_op jit(solution)/shard_map/dot_general | solution.py:65
  13.5 0.0 copy-start.3
  13.5 7.6 %all-to-all-start = ((bf16[8,128,1536]{2,1,0:T(8,128)(2,1)}), bf16[8,128,1536]{2,1,0:T(8,128)(2,1)}, u32[]{:S(2)}, u32[]{:S(2)}) async-start(bf16[8,128,1536]{2,1,0:T(8,128)(2,1)} %bitcast.49), calls=%async_computation | async-start | bytes 6291456 | tf_op jit(solution)/shard_map/all_to_all | solution.py:69
  21.2 0.0 copy-done.3
  21.2 0.1 copy.23
  21.3 0.6 fusion.28
  21.9 38.1 %all-to-all-done = bf16[8,128,1536]{2,1,0:T(8,128)(2,1)} async-done(((bf16[8,128,1536]{2,1,0:T(8,128)(2,1)}), bf16[8,128,1536]{2,1,0:T(8,128)(2,1)}, u32[]{:S(2)}, u32[]{:S(2)}) %all-to-all-start) | async-done | bytes 3145760 | tf_op jit(solution)/shard_map/all_to_all | solution.py:69
  60.0 2.4 %reduce_sum.12 = bf16[128,1536]{1,0:T(8,128)(2,1)S(1)} reduce(bf16[8,128,1536]{2,1,0:T(8,128)(2,1)} %all-to-all-done, bf16[]{:T(256)} %constant.43.clone.1), dimensions={0}, to_apply=%region_0.1 | reduce | flops 1376256 | bytes 3538946 | tf_op jit(solution)/shard_map/reduce_sum | solution.py:70
  62.5 0.5 reshape.270
  62.9 0.0 copy-start.2
  62.9 0.9 copy.16
  63.8 10.6 %all-to-all-start.1 = ((bf16[2,32,2,16,96]{4,3,2,0,1:T(8,128)(2,1)}), bf16[2,32,2,16,96]{4,3,2,0,1:T(8,128)(2,1)S(1)}, u32[]{:S(2)}, u32[]{:S(2)}) async-start(bf16[2,32,2,16,96]{4,3,2,0,1:T(8,128)(2,1)} %copy.16), calls=%async_computation.1 | async-start | bytes 1048576 | tf_op jit(solution)/shard_map/all_to_all | solution.py:72
  74.4 0.8 fusion.24
  75.2 0.1 copy.22
  75.3 0.3 fusion.21
  75.6 0.0 copy-done.2
  75.6 2.1 %multiply_subtract_fusion = (f32[32,16,512]{2,1,0:T(8,128)S(1)}, f32[32,16,512]{2,1,0:T(8,128)}) fusion(f32[16,512]{1,0:T(8,128)} %get-tuple-element.31, f32[32,512]{1,0:T(8,128)S(1)} %get-tuple-element.29, f32[16,512]{1,0:T(8,128)} %get-tuple-element.32, f32[32,512]{1,0:T(8,128)S(1)} %get-tuple-element.30), kind=kLoop, calls=%fused_computation.8 | loop fusion | flops 1572864 | bytes 2293760 | tf_op jit(solution)/shard_map/sub | solution.py:41
  77.7 13.3 %all-to-all-done.1 = bf16[2,32,2,16,96]{4,3,2,0,1:T(8,128)(2,1)S(1)} async-done(((bf16[2,32,2,16,96]{4,3,2,0,1:T(8,128)(2,1)}), bf16[2,32,2,16,96]{4,3,2,0,1:T(8,128)(2,1)S(1)}, u32[]{:S(2)}, u32[]{:S(2)}) %all-to-all-start.1) | async-done | bytes 393248 | tf_op jit(solution)/shard_map/all_to_all | solution.py:72
  91.0 0.0 copy-start.1
  91.0 0.7 convolution_bitcast_fusion
  91.7 0.5 copy-done.1
  92.2 1.6 %fusion = f32[2,192,1024]{2,1,0:T(8,128)S(1)} fusion(f32[2,512,192]{1,2,0:T(8,128)S(1)} %convolution_bitcast_fusion, f32[512,512]{1,0:T(8,128)S(1)} %bitcast.48, f32[512,512]{1,0:T(8,128)S(1)} %bitcast.47), kind=kOutput, calls=%fused_computation.2 | convolution fusion | flops 1208483840 | bytes 4456448 | tf_op jit(solution)/shard_map/jts,tw->jsw/dot_general | solution.py:86
  93.8 0.9 fusion.5
  (7 shorter events, 0.2 us)
Async XLA Ops:
  0.0 10.0 %copy-start = (bf16[512,16,96]{0,2,1:T(8,128)(2,1)S(1)}, bf16[512,16,96]{0,2,1:T(8,128)(2,1)}, u32[]{:S(2)}) copy-start(bf16[512,16,96]{0,2,1:T(8,128)(2,1)} %param.4) | copy-start | bytes 4718596
  13.5 7.6 %copy-start.3 = (f32[2,2,96,96]{3,2,1,0:T(8,128)S(1)}, f32[2,2,96,96]{3,2,1,0:T(8,128)}, u32[]{:S(2)}) copy-start(f32[2,2,96,96]{3,2,1,0:T(8,128)} %param.7) | copy-start | bytes 442372
  13.5 46.5 %all-to-all-start = ((bf16[8,128,1536]{2,1,0:T(8,128)(2,1)}), bf16[8,128,1536]{2,1,0:T(8,128)(2,1)}, u32[]{:S(2)}, u32[]{:S(2)}) async-start(bf16[8,128,1536]{2,1,0:T(8,128)(2,1)} %bitcast.49), calls=%async_computation | async-start | bytes 6291456 | tf_op jit(solution)/shard_map/all_to_all | solution.py:69
  62.9 12.6 %copy-start.2 = (f32[2,96,96]{1,2,0:T(8,128)S(1)}, f32[2,96,96]{1,2,0:T(8,128)}, u32[]{:S(2)}) copy-start(f32[2,96,96]{1,2,0:T(8,128)} %fusion.28) | copy-start | bytes 221188
  63.8 27.1 %all-to-all-start.1 = ((bf16[2,32,2,16,96]{4,3,2,0,1:T(8,128)(2,1)}), bf16[2,32,2,16,96]{4,3,2,0,1:T(8,128)(2,1)S(1)}, u32[]{:S(2)}, u32[]{:S(2)}) async-start(bf16[2,32,2,16,96]{4,3,2,0,1:T(8,128)(2,1)} %copy.16), calls=%async_computation.1 | async-start | bytes 1048576 | tf_op jit(solution)/shard_map/all_to_all | solution.py:72
  91.0 1.2 %copy-start.1 = (f32[32,16,512]{2,1,0:T(8,128)S(1)}, f32[32,16,512]{2,1,0:T(8,128)}, u32[]{:S(2)}) copy-start(f32[32,16,512]{2,1,0:T(8,128)} %get-tuple-element.9) | copy-start | bytes 3145732

commit v6 on v2

--- a/solution.py
+++ b/solution.py
@@ -46,10 +46,10 @@
     cos_rows, sin_rows = phase_rows(ordered_coords, cell_coords)
     table = jnp.stack(
         [
-            cos_rows.reshape(n_cell, n_tm * q_local, cell_dev),
-            sin_rows.reshape(n_cell, n_tm * q_local, cell_dev),
+            cos_rows.reshape(n_cell, n_tm, q_local, cell_dev),
+            sin_rows.reshape(n_cell, n_tm, q_local, cell_dev),
         ],
-        axis=1,
+        axis=2,
     ).reshape(2 * q_total, cell_dev)
     velocity_rows = velocity.reshape(cell_dev, frames_dev * branches)
     partial_term = jnp.dot(table, velocity_rows, preferred_element_type=jnp.float32)
@@ -58,9 +58,9 @@
     )
     gathered = lax.all_to_all(partial_term, "cell", split_axis=0, concat_axis=0, tiled=True)
     summed = jnp.sum(gathered.astype(jnp.float32), axis=0).astype(jnp.bfloat16)
-    blocks = summed.reshape(2, n_tm, q_local, frames_dev, branches)
-    collected = lax.all_to_all(blocks, "tm", split_axis=1, concat_axis=3, tiled=True)
-    collected = collected.reshape(2, q_local, frames, branches).astype(jnp.float32)
+    blocks = summed.reshape(n_tm, 2, q_local, frames_dev, branches)
+    collected = lax.all_to_all(blocks, "tm", split_axis=0, concat_axis=0, tiled=True)
+    collected = collected.astype(jnp.float32)
 
     scale = 1.0 / math.sqrt(cell_dev * n_cell)
     e_real = eigvecs[:, 0] * scale
@@ -70,10 +70,12 @@
         axis=1,
     )
     highest = lax.Precision.HIGHEST
-    amplitude = jnp.einsum("rjtk,jrks->jts", collected, e_block, precision=highest)
+    amplitude = jnp.einsum("arjtk,jrks->jats", collected, e_block, precision=highest).reshape(
+        q_local, frames, 2 * branches
+    )
     cosines, sines = twiddles(frames)
     basis = jnp.concatenate([cosines, sines], axis=1)
-    projected = jnp.einsum("jts,tw->jsw", amplitude, basis, precision=highest)
+    projected = jnp.einsum("jts,tw->jsw", amplitude, basis, precision=lax.Precision.HIGH)
     on_cos = projected[:, :, :frames]
     on_sin = projected[:, :, frames:]
     out_real = on_cos[:, :branches] + on_sin[:, branches:]

time: 93.8 us -> 95.9 us (1.022)
  waiting for transfers between devices: 51.4 us -> 53.5 us
  other arithmetic: 12.1 us -> 10.2 us
  local copies, waits for them, and re-layouts: 4.62 us -> 6.48 us
    all_to_all x1, waiting for transfers between devices: 13.3 us -> 14.7 us  [local(): lax.all_to_all(blocks, 'tm', split_axis=0, concat_axis=0, tiled=True)]
    reshape x2 -> x3, local copies, waits for them, and re-layouts: 1.33 us -> 2.52 us  [the longest x2 1.3 us: local(): blocks = summed.reshape(n_tm, 2, q_local, frames_dev, branches)]
    dot_general x1, matrix products: 3.52 us -> 4.69 us  [local(): jnp.dot(table, velocity_rows, preferred_element_type=jnp.float32)]
    dot_general x2, matrix products: 3.39 us -> 2.28 us  [the longest x1 1.64 us: local(): jnp.einsum('jts,tw->jsw', amplitude, basis, precision=lax.Precision.HIGH)]
    another operation x0 -> x1, local copies, waits for them, and re-layouts: none -> 1.08 us  [local(): jnp.stack([cos_rows.reshape(n_cell, n_tm, q_local, cell_dev), sin_rows.re...]
  transfers between devices with their start and end apart: 2 -> 2, of which waited for: 2 -> 2; matrix products, arithmetic and copies ran while one was open for 4% -> 2% of each run, Pallas kernels for 0% -> 0%
where the time goes in v6:
time: 95.9 us; the launch traced here: 95.5 us
  waiting for transfers between devices  53.5 us (56%)
  starting transfers between devices  18.2 us (19%)
  other arithmetic  10.2 us (11%)
  matrix products  6.98 us (7%)
  local copies, waits for them, and re-layouts  6.48 us (7%)
    all_to_all x1, waiting for transfers between devices, local(): lax.all_to_all(partial_term, 'cell', split_axis=0, concat_axis=0, tiled=T...  38.8 us
    all_to_all x1, waiting for transfers between devices, local(): lax.all_to_all(blocks, 'tm', split_axis=0, concat_axis=0, tiled=True)  14.7 us
    all_to_all x1, starting transfers between devices, local(): lax.all_to_all(blocks, 'tm', split_axis=0, concat_axis=0, tiled=True)  10.6 us
    all_to_all x1, starting transfers between devices, local(): lax.all_to_all(partial_term, 'cell', split_axis=0, concat_axis=0, tiled=T...  7.61 us
    convert_element_type x1, other arithmetic, phase_rows(): jnp.cos(angles).astype(jnp.bfloat16)  4.85 us
    dot_general x1, matrix products, local(): jnp.dot(table, velocity_rows, preferred_element_type=jnp.float32)  4.69 us
    reduce_sum x1, other arithmetic, local(): summed = jnp.sum(gathered.astype(jnp.float32), axis=0).astype(jnp.bfloat16)  2.45 us
  transfers between devices with their start and end apart: 2, of which 2 were waited for; matrix products, arithmetic and copies ran while one was open for 2% of the time, Pallas kernels for 0%

profile of v6, /device:TPU:1, one launch (start us, length us, event | category | flops | bytes accessed | tf_op | source)
XLA Modules:
  0.0 95.5 jit_solution(7436793224335316292)
XLA Ops:
  0.0 0.0 copy-start
  0.0 0.0 copy-start.3
  0.0 1.2 %reshape.255 = s32[32,8,2,3]{2,1,0,3:T(8,128)S(1)} reshape(s32[512,3]{0,1:T(4,128)} %param.6) | data formatting | bytes 12288 | tf_op jit(solution)/shard_map/reshape | solution.py:44
  1.2 0.1 copy.32
  1.3 0.3 reshape.256
  1.5 0.1 mul.261
  1.7 0.1 copy.33
  1.8 0.1 mul.266
  2.0 0.1 copy.34
  2.1 0.1 mul.271
  2.2 0.1 copy.35
  2.3 0.0 copy-done.3
  2.4 4.8 %cosine_convert_fusion = (bf16[8,32,1,2,512]{4,1,3,2,0:T(8,128)(2,1)S(1)}, bf16[8,32,1,2,512]{4,1,3,2,0:T(8,128)(2,1)S(1)}) fusion(s32[512]{0:T(512)S(1)} %bitcast.58, s32[8,32,2]{1,2,0:T(2,128)S(1)} %copy.35, s32[512]{0:T(512)S(1)} %bitcast.59, s32[8,32,2]{1,2,0:T(2,128)S(1)} %copy.34, s32[512]{0:T(512)S(1)} %bitcast.57, s32[8,32,2]{1,2,0:T(2,128)S(1)} %copy.33), kind=kLoop, calls=%fused_computation.15 | loop fusion | flops 5505024 | bytes 1060864 | tf_op jit(solution)/shard_map/convert_element_type | solution.py:18
  7.2 0.1 pad_maximum_fusion
  7.3 1.1 %copy.36 = bf16[8,32,2,2,512]{4,3,2,1,0:T(2,128)(2,1)S(1)} copy(bf16[8,32,2,2,512]{4,1,3,2,0:T(8,128)(2,1)S(1)} %pad_maximum_fusion) | data formatting | bytes 2097152 | tf_op jit(solution)/shard_map/stack | solution.py:47
  8.4 1.2 %reshape.257 = bf16[1024,512]{1,0:T(8,128)(2,1)} reshape(bf16[8,32,2,2,512]{4,3,2,1,0:T(2,128)(2,1)S(1)} %copy.36) | data formatting | bytes 2097152 | tf_op jit(solution)/shard_map/reshape | solution.py:53
  9.6 0.0 copy-done
  9.6 4.7 %convolution_convert_fusion = bf16[1024,1536]{1,0:T(8,128)(2,1)} fusion(bf16[1024,512]{1,0:T(8,128)(2,1)} %reshape.257, bf16[512,1536]{0,1:T(8,128)(2,1)S(1)} %bitcast.51), kind=kOutput, calls=%fused_computation | convolution fusion | flops 1612185600 | bytes 5767168 | tf_op jit(solution)/shard_map/dot_general | solution.py:55
  14.3 0.0 copy-start.2
  14.3 7.6 %all-to-all-start = ((bf16[8,128,1536]{2,1,0:T(8,128)(2,1)}), bf16[8,128,1536]{2,1,0:T(8,128)(2,1)}, u32[]{:S(2)}, u32[]{:S(2)}) async-start(bf16[8,128,1536]{2,1,0:T(8,128)(2,1)} %bitcast.55), calls=%async_computation | async-start | bytes 6291456 | tf_op jit(solution)/shard_map/all_to_all | solution.py:59
  21.9 0.0 copy-done.2
  22.0 38.8 %all-to-all-done = bf16[8,128,1536]{2,1,0:T(8,128)(2,1)} async-done(((bf16[8,128,1536]{2,1,0:T(8,128)(2,1)}), bf16[8,128,1536]{2,1,0:T(8,128)(2,1)}, u32[]{:S(2)}, u32[]{:S(2)}) %all-to-all-start) | async-done | bytes 3145760 | tf_op jit(solution)/shard_map/all_to_all | solution.py:59
  60.8 2.4 %reduce_sum.12 = bf16[128,1536]{1,0:T(8,128)(2,1)S(1)} reduce(bf16[8,128,1536]{2,1,0:T(8,128)(2,1)} %all-to-all-done, bf16[]{:T(256)} %constant.48.clone.1), dimensions={0}, to_apply=%region_0.1 | reduce | flops 1376256 | bytes 3538946 | tf_op jit(solution)/shard_map/reduce_sum | solution.py:60
  63.3 0.5 reshape.260
  63.7 0.8 copy.37
  64.6 10.6 %all-to-all-start.1 = ((bf16[32,2,2,16,96]{4,3,1,2,0:T(8,128)(2,1)}), bf16[32,2,2,16,96]{4,3,1,2,0:T(8,128)(2,1)S(1)}, u32[]{:S(2)}, u32[]{:S(2)}) async-start(bf16[32,2,2,16,96]{4,3,1,2,0:T(8,128)(2,1)} %copy.37), calls=%async_computation.1 | async-start | bytes 1048576 | tf_op jit(solution)/shard_map/all_to_all | solution.py:62
  75.1 0.1 fusion.30
  75.3 0.3 fusion.27
  75.6 0.2 maximum_bitcast_fusion.4
  75.8 1.3 %multiply_subtract_fusion = (f32[32,16,512]{2,1,0:T(8,128)S(1)}, f32[32,16,512]{2,1,0:T(8,128)}) fusion(f32[16,512]{1,0:T(8,128)S(1)} %get-tuple-element.21, f32[32,512]{1,0:T(8,128)S(1)} %get-tuple-element.19, f32[16,512]{1,0:T(8,128)S(1)} %get-tuple-element.22, f32[32,512]{1,0:T(8,128)S(1)} %get-tuple-element.20), kind=kLoop, calls=%fused_computation.13 | loop fusion | flops 1572864 | bytes 2293760 | tf_op jit(solution)/shard_map/sub | solution.py:31
  77.0 14.7 %all-to-all-done.1 = bf16[32,2,2,16,96]{4,3,1,2,0:T(8,128)(2,1)S(1)} async-done(((bf16[32,2,2,16,96]{4,3,1,2,0:T(8,128)(2,1)}), bf16[32,2,2,16,96]{4,3,1,2,0:T(8,128)(2,1)S(1)}, u32[]{:S(2)}, u32[]{:S(2)}) %all-to-all-start.1) | async-done | bytes 393248 | tf_op jit(solution)/shard_map/all_to_all | solution.py:62
  91.7 0.0 copy-start.1
  91.7 0.6 fusion.6
  92.4 0.6 copy-done.1
  92.9 1.6 %fusion = f32[2,192,1024]{2,1,0:T(8,128)S(1)} fusion(f32[2,512,192]{2,1,0:T(8,128)S(1)} %bitcast.54, f32[512,512]{1,0:T(8,128)S(1)} %bitcast.53, f32[512,512]{1,0:T(8,128)S(1)} %bitcast.52), kind=kOutput, calls=%fused_computation.2 | convolution fusion | flops 1208483840 | bytes 4456448 | tf_op jit(solution)/shard_map/jts,tw->jsw/dot_general | solution.py:78
  94.6 0.9 fusion.10
  (4 shorter events, 0.1 us)
Async XLA Ops:
  0.0 9.6 %copy-start = (bf16[512,16,96]{0,2,1:T(8,128)(2,1)S(1)}, bf16[512,16,96]{0,2,1:T(8,128)(2,1)}, u32[]{:S(2)}) copy-start(bf16[512,16,96]{0,2,1:T(8,128)(2,1)} %param.4) | copy-start | bytes 4718596
  0.0 2.3 %copy-start.3 = (s32[512,3]{0,1:T(4,128)S(1)}, s32[512,3]{0,1:T(4,128)}, u32[]{:S(2)}) copy-start(s32[512,3]{0,1:T(4,128)} %param.5) | copy-start | bytes 18436
  14.3 7.6 %copy-start.2 = (f32[2,2,96,96]{3,2,1,0:T(8,128)S(1)}, f32[2,2,96,96]{3,2,1,0:T(8,128)}, u32[]{:S(2)}) copy-start(f32[2,2,96,96]{3,2,1,0:T(8,128)} %param.7) | copy-start | bytes 442372
  14.3 46.5 %all-to-all-start = ((bf16[8,128,1536]{2,1,0:T(8,128)(2,1)}), bf16[8,128,1536]{2,1,0:T(8,128)(2,1)}, u32[]{:S(2)}, u32[]{:S(2)}) async-start(bf16[8,128,1536]{2,1,0:T(8,128)(2,1)} %bitcast.55), calls=%async_computation | async-start | bytes 6291456 | tf_op jit(solution)/shard_map/all_to_all | solution.py:59
  64.6 27.1 %all-to-all-start.1 = ((bf16[32,2,2,16,96]{4,3,1,2,0:T(8,128)(2,1)}), bf16[32,2,2,16,96]{4,3,1,2,0:T(8,128)(2,1)S(1)}, u32[]{:S(2)}, u32[]{:S(2)}) async-start(bf16[32,2,2,16,96]{4,3,1,2,0:T(8,128)(2,1)} %copy.37), calls=%async_computation.1 | async-start | bytes 1048576 | tf_op jit(solution)/shard_map/all_to_all | solution.py:62
  91.7 1.2 %copy-start.1 = (f32[32,16,512]{2,1,0:T(8,128)S(1)}, f32[32,16,512]{2,1,0:T(8,128)}, u32[]{:S(2)}) copy-start(f32[32,16,512]{2,1,0:T(8,128)} %get-tuple-element.9) | copy-start | bytes 3145732

commit v7 on v4

v7 whole, which is shorter than its diff:
```python
import math

import jax
import jax.numpy as jnp
from jax import lax
from jax.sharding import PartitionSpec as P

L = 16


def twiddles(frames):
    inner = 16
    outer = frames // inner
    w = jnp.arange(frames, dtype=jnp.int32)
    a = jnp.arange(outer, dtype=jnp.int32)
    b = jnp.arange(inner, dtype=jnp.int32)
    coarse = (a[:, None] * w[None, :] % outer).astype(jnp.float32) * (2.0 * math.pi / outer)
    fine = (b[:, None] * w[None, :] % frames).astype(jnp.float32) * (2.0 * math.pi / frames)
    cos_c, sin_c = jnp.cos(coarse)[:, None, :], jnp.sin(coarse)[:, None, :]
    cos_f, sin_f = jnp.cos(fine)[None, :, :], jnp.sin(fine)[None, :, :]
    cosines = (cos_c * cos_f - sin_c * sin_f).reshape(frames, frames)
    sines = (sin_c * cos_f + cos_c * sin_f).reshape(frames, frames)
    return cosines, sines


def lattice_dft(on_lattice):
    high = lax.Precision.HIGH
    width = on_lattice.shape[1]
    k = jnp.arange(L, dtype=jnp.int32)
    angle = ((k[:, None] * k[None, :]) % L).astype(jnp.float32) * (2.0 * math.pi / L)
    w_re, w_im = jnp.cos(angle), -jnp.sin(angle)
    yz_re = (w_re[:, None, :, None] * w_re[None, :, None, :] - w_im[:, None, :, None] * w_im[None, :, None, :])
    yz_im = (w_re[:, None, :, None] * w_im[None, :, None, :] + w_im[:, None, :, None] * w_re[None, :, None, :])
    plane = jnp.stack([yz_re, yz_im]).reshape(2, L * L, L * L)
    grid = on_lattice.astype(jnp.float32).reshape(L, L * L, width)
    on_plane = jnp.einsum("rpm,xmf->rxpf", plane, grid, precision=high)
    line = jnp.stack(
        [jnp.stack([w_re, -w_im]), jnp.stack([w_im, w_re])]
    )
    full = jnp.einsum("rsax,sxpf->rapf", line, on_plane, precision=high)
    return full.reshape(2, L * L * L, width)


def local(velocity, cell_coords, q_coords, eigvecs):
    n_tm = lax.axis_size("tm")
    n_cell = lax.axis_size("cell")
    n_dev = n_tm * n_cell
    cell_dev, frames_dev, branches = velocity.shape
    q_total = q_coords.shape[0]
    q_local = q_total // n_dev
    frames = frames_dev * n_tm
    frames_each = frames_dev // n_cell
    width = frames_each * branches
    spread = velocity.reshape(cell_dev, n_cell, width)
    position = jnp.broadcast_to(cell_coords.astype(jnp.bfloat16)[:, None, :], (cell_dev, n_cell, 3))
    payload = jnp.concatenate([spread, position], axis=2)
    received = lax.all_to_all(payload, "cell", split_axis=1, concat_axis=0, tiled=True)
    received = received.reshape(cell_dev * n_cell, width + 3)
    where = received[:, width:].astype(jnp.int32)
    lattice = where[:, 0] * (L * L) + where[:, 1] * L + where[:, 2]
    order = jnp.argsort(lattice)
    on_lattice = jnp.take(received[:, :width], order, axis=0)
    full = lattice_dft(on_lattice)
    q_index = q_coords[:, 0] * (L * L) + q_coords[:, 1] * L + q_coords[:, 2]
    modes = jnp.take(full, q_index, axis=1).astype(jnp.bfloat16)
    modes = modes.reshape(2, n_dev, q_local, frames_each, branches)
    collected = lax.all_to_all(modes, ("tm", "cell"), split_axis=1, concat_axis=1, tiled=True)

    scale = 1.0 / math.sqrt(cell_dev * n_cell)
    e_real = eigvecs[:, 0] * scale
    e_imag = eigvecs[:, 1] * scale
    e_block = jnp.stack(
        [jnp.concatenate([e_real, -e_imag], axis=2), jnp.concatenate([e_imag, e_real], axis=2)],
        axis=1,
    )
    highest = lax.Precision.HIGHEST
    amplitude = jnp.einsum(
        "rsjfk,jrkc->jsfc", collected.astype(jnp.float32), e_block, precision=highest
    ).reshape(q_local, frames, 2 * branches)
    cosines, sines = twiddles(frames)
    basis = jnp.concatenate([cosines, sines], axis=1)
    projected = jnp.einsum("jts,tw->jsw", amplitude, basis, precision=lax.Precision.HIGH)
    on_cos = projected[:, :, :frames]
    on_sin = projected[:, :, frames:]
    out_real = on_cos[:, :branches] + on_sin[:, branches:]
    out_imag = on_cos[:, branches:] - on_sin[:, :branches]
    return (out_real * out_real + out_imag * out_imag) / frames


def solution(mesh):
    in_specs = (P("cell", "tm", None), P("cell", None), P(), P(("tm", "cell"), None, None, None))
    out_specs = P(("tm", "cell"), None, None)
    return jax.shard_map(local, mesh=mesh, in_specs=in_specs, out_specs=out_specs, check_vma=False)
```

time: 113 us -> 120 us (1.062)
  local copies, waits for them, and re-layouts: 6.07 us -> 40.4 us
  blocking collectives: 26.3 us -> 0 us
  waiting for transfers between devices: 19.2 us -> 35.9 us
  other arithmetic: 24.3 us -> 15.4 us
  starting transfers between devices: 25.8 us -> 19.3 us
  matrix products: 10.7 us -> 8.12 us
    all_gather x1 -> x0, blocking collectives: 26.3 us -> none  [local(): all_code = lax.all_gather(cell_code, 'cell', axis=0, tiled=True)]
    gather x0 -> x5, local copies, waits for them, and re-layouts: none -> 25.4 us  [the longest x2 20 us: local(): on_lattice = jnp.take(received[:, :width], order, axis=0)]
    all_to_all x1, waiting for transfers between devices: 0.01 us -> 16.6 us  [local(): lax.all_to_all(payload, 'cell', split_axis=1, concat_axis=0, tiled=True)]
    select_n x2 -> x0, other arithmetic: 14.3 us -> none  [the longest x1 14.2 us: phase_rows(): real, imag = (jnp.where(bit3, -real, real), jnp.where(bit3, -imag, imag))]
    all_to_all x1, starting transfers between devices: 20.6 us -> 11.8 us  [local(): lax.all_to_all(modes, ('tm', 'cell'), split_axis=1, concat_axis=1, tiled=...]
    another operation x1, other arithmetic: 7.45 us -> 0.01 us  [lattice_dft(): line = jnp.stack([jnp.stack([w_re, -w_im]), jnp.stack([w_im, w_re])])]
    sort x0 -> x1, other arithmetic: none -> 5.78 us  [local(): order = jnp.argsort(lattice)]
    reshape x2 -> x1, local copies, waits for them, and re-layouts: 1.89 us -> 5.66 us  [lattice_dft(): return full.reshape(2, L * L * L, width)]
  transfers between devices with their start and end apart: 2 -> 2, of which waited for: 1 -> 2; matrix products, arithmetic and copies ran while one was open for 22% -> 6% of each run, Pallas kernels for 0% -> 0%
where the time goes in v7:
time: 120 us; the launch traced here: 119 us
  local copies, waits for them, and re-layouts  40.4 us (34%)
  waiting for transfers between devices  35.9 us (30%)
  starting transfers between devices  19.3 us (16%)
  other arithmetic  15.4 us (13%)
  matrix products  8.12 us (7%)
    gather x2, local copies, waits for them, and re-layouts, local(): on_lattice = jnp.take(received[:, :width], order, axis=0)  20 us
    all_to_all x1, waiting for transfers between devices, local(): lax.all_to_all(modes, ('tm', 'cell'), split_axis=1, concat_axis=1, tiled=...  19.2 us
    all_to_all x1, waiting for transfers between devices, local(): lax.all_to_all(payload, 'cell', split_axis=1, concat_axis=0, tiled=True)  16.6 us
    all_to_all x1, starting transfers between devices, local(): lax.all_to_all(modes, ('tm', 'cell'), split_axis=1, concat_axis=1, tiled=...  11.8 us
    all_to_all x1, starting transfers between devices, local(): lax.all_to_all(payload, 'cell', split_axis=1, concat_axis=0, tiled=True)  7.48 us
    sort x1, other arithmetic, local(): order = jnp.argsort(lattice)  5.78 us
    reshape x1, local copies, waits for them, and re-layouts, lattice_dft(): return full.reshape(2, L * L * L, width)  5.66 us
    gather x3, local copies, waits for them, and re-layouts, local(): modes = jnp.take(full, q_index, axis=1).astype(jnp.bfloat16)  5.36 us
  transfers between devices with their start and end apart: 2, of which 2 were waited for; matrix products, arithmetic and copies ran while one was open for 6% of the time, Pallas kernels for 0%

profile of v7, /device:TPU:1, one launch (start us, length us, event | category | flops | bytes accessed | tf_op | source)
XLA Modules:
  0.0 119.3 jit_solution(16196416428850020041)
XLA Ops:
  0.0 0.7 convert_element_type.79
  0.7 2.7 %pad_maximum_fusion = bf16[512,8,195]{0,2,1:T(8,128)(2,1)} fusion(bf16[512,8,3]{0,2,1:T(4,128)(2,1)S(1)} %broadcast_in_dim.30, bf16[512,8,192]{0,2,1:T(8,128)(2,1)} %bitcast.77), kind=kLoop, calls=%fused_computation.16 | loop fusion | flops 3194880 | bytes 3194880 | tf_op jit(solution)/shard_map/concatenate | solution.py:56
  3.5 7.5 %all-to-all-start = ((bf16[512,8,195]{0,2,1:T(8,128)(2,1)}), bf16[512,8,195]{0,2,1:T(8,128)(2,1)}, u32[]{:S(2)}, u32[]{:S(2)}) async-start(bf16[512,8,195]{0,2,1:T(8,128)(2,1)} %pad_maximum_fusion), calls=%async_computation | async-start | bytes 3276800 | tf_op jit(solution)/shard_map/all_to_all | solution.py:57
  10.9 0.1 sine_negate_fusion
  11.0 2.0 %multiply_subtract_fusion = (f32[16,16,16,16]{3,2,1,0:T(8,128)S(1)}, f32[16,16,16,16]{3,2,1,0:T(8,128)}) fusion(f32[16,16]{1,0:T(8,128)S(1)} %get-tuple-element.23, f32[16,16]{1,0:T(8,128)S(1)} %get-tuple-element.24), kind=kLoop, calls=%fused_computation.15 | loop fusion | flops 393216 | bytes 526336 | tf_op jit(solution)/shard_map/sub | solution.py:32
  13.0 0.0 copy-start.1
  13.0 0.0 copy-start
  13.0 2.5 %add.152 = f32[1,256,256]{2,1,0:T(8,128)S(1)} reshape(f32[16,16,16,16]{3,2,1,0:T(8,128)} %get-tuple-element.16) | data formatting | bytes 524288 | tf_op jit(solution)/shard_map/add | solution.py:33
  15.5 0.9 sub.25
  16.4 0.0 copy-done.1
  16.4 0.2 broadcast_in_dim.28
  16.6 0.1 copy.33
  16.7 0.0 copy-done
  16.7 0.1 copy.55
  16.9 0.1 fusion.59
  16.9 0.1 fusion.57
  17.0 16.6 %all-to-all-done = bf16[512,8,195]{0,2,1:T(8,128)(2,1)} async-done(((bf16[512,8,195]{0,2,1:T(8,128)(2,1)}), bf16[512,8,195]{0,2,1:T(8,128)(2,1)}, u32[]{:S(2)}, u32[]{:S(2)}) %all-to-all-start) | async-done | bytes 1597472 | tf_op jit(solution)/shard_map/all_to_all | solution.py:57
  33.7 2.7 %copy.34 = bf16[8,512,1,195]{3,1,0,2:T(8,128)(2,1)S(1)} copy(bf16[8,512,1,195]{1,3,0,2:T(8,128)(2,1)} %bitcast.6) | data formatting | bytes 3194880 | tf_op jit(solution)/shard_map/all_to_all | solution.py:57
  36.4 0.5 slice_convert_fusion
  36.9 1.7 %fusion.5 = s32[4096]{0:T(1024)S(1)} fusion(s32[4096,3]{1,0:T(8,128)S(1)} %slice_convert_fusion), kind=kLoop, calls=%fused_computation.6 | loop fusion | flops 16384 | bytes 65536 | tf_op jit(solution)/shard_map/add | solution.py:60
  38.6 5.8 %sort.17 = (s32[4096]{0:T(1024)}, s32[4096]{0:T(1024)S(1)}) sort(s32[4096]{0:T(1024)S(1)} %fusion.5, s32[4096]{0:T(1024)S(1)} %iota.107), dimensions={0}, to_apply=%region_0.0 | sort | flops 49152 | bytes 65536 | tf_op jit(solution)/shard_map/jit(argsort)/sort | solution.py:61
  44.4 16.9 %gather_fusion = bf16[4096,192]{1,0:T(8,128)(2,1)} fusion(bf16[4096,192]{1,0:T(8,128)(2,1)S(1)} %bitcast.70, s32[4096]{0:T(1024)S(1)} %fusion.43), kind=kCustom, calls=%fused_computation | custom fusion | bytes 3162112 | tf_op jit(solution)/shard_map/jit(_take)/gather | solution.py:62
  61.3 3.1 %copy.35 = bf16[16,256,192]{1,0,2:T(8,128)(2,1)S(1)} copy(bf16[16,256,192]{2,1,0:T(8,128)(2,1)} %bitcast.71) | data formatting | bytes 3145728 | tf_op jit(solution)/shard_map/jit(_take)/gather | solution.py:62
  64.5 1.9 %fusion.10 = f32[16,192,2,256]{3,0,2,1:T(8,128)S(1)} fusion(bf16[16,256,192]{1,0,2:T(8,128)(2,1)S(1)} %copy.35, pred[16,256]{1,0:T(8,128)(4,1)S(1)} %broadcast_in_dim.31, f32[1,256,256]{2,1,0:T(8,128)S(1)} %add.152, f32[1,256,256]{2,1,0:T(8,128)S(1)} %sub.25), kind=kOutput, calls=%fused_computation.17 | convolution fusion | flops 2416836608 | bytes 8392704 | tf_op jit(solution)/shard_map/rpm,xmf->rxpf/dot_general | solution.py:36
  66.3 3.1 %fusion.2 = bf16[2,16,256,192]{2,1,3,0:T(8,128)(2,1)S(1)} fusion(f32[16,192,2,256]{3,0,2,1:T(8,128)S(1)} %fusion.10, f32[1,2,16,16]{3,2,1,0:T(8,128)S(1)} %get-tuple-element.18, f32[1,2,16,16]{3,2,1,0:T(8,128)S(1)} %get-tuple-element.17), kind=kOutput, calls=%fused_computation.4 | convolution fusion | flops 301990912 | bytes 9441280 | tf_op jit(solution)/shard_map/rsax,sxpf->rapf/dot_general | solution.py:40
  69.5 5.7 %copy.51 = bf16[2,16,256,192]{3,0,2,1:T(2,128)(2,1)} copy(bf16[2,16,256,192]{2,1,3,0:T(8,128)(2,1)S(1)} %fusion.2) | data formatting | bytes 6291456 | tf_op jit(solution)/shard_map/reshape | solution.py:41
  75.1 4.2 %gather_fusion.1 = bf16[512,2,192]{2,1,0:T(2,128)(2,1)S(1)} fusion(bf16[2,4096,192]{2,0,1:T(2,128)(2,1)} %bitcast.72, s32[1024]{0:T(1024)S(1)} %pad_clamp_fusion), kind=kCustom, calls=%fused_computation.1 | custom fusion | bytes 788480 | tf_op jit(solution)/shard_map/jit(_take)/gather | solution.py:65
  79.3 0.5 reshape.410
  79.8 0.7 copy.38
  80.5 0.1 select_convert_fusion
  80.6 1.1 copy.39
  81.7 11.8 %all-to-all-start.1 = ((bf16[2,256,2,2,96]{4,0,3,2,1:T(2,128)(2,1)}), bf16[2,256,2,2,96]{4,0,3,2,1:T(2,128)(2,1)S(1)}, u32[]{:S(2)}, u32[]{:S(2)}) async-start(bf16[2,256,2,2,96]{4,0,3,2,1:T(2,128)(2,1)} %copy.39), calls=%async_computation.1 | async-start | bytes 1048576 | tf_op jit(solution)/shard_map/all_to_all | solution.py:67
  93.6 0.1 fusion.41
  93.7 0.1 copy.54
  93.8 0.3 fusion.38
  94.2 0.3 multiply_subtract_fusion.1
  94.5 19.2 %all-to-all-done.1 = bf16[2,256,2,2,96]{4,0,3,2,1:T(2,128)(2,1)S(1)} async-done(((bf16[2,256,2,2,96]{4,0,3,2,1:T(2,128)(2,1)}), bf16[2,256,2,2,96]{4,0,3,2,1:T(2,128)(2,1)S(1)}, u32[]{:S(2)}, u32[]{:S(2)}) %all-to-all-start.1) | async-done | bytes 393248 | tf_op jit(solution)/shard_map/all_to_all | solution.py:67
  113.7 1.6 %convolution_bitcast_fusion = f32[2,256,2,192]{1,3,2,0:T(8,128)} fusion(bf16[2,256,2,2,96]{4,0,3,2,1:T(2,128)(2,1)S(1)} %all-to-all-done.1, f32[2,1,96,192]{2,3,1,0:T(8,128)S(1)} %get-tuple-element.14, f32[2,1,96,192]{2,3,1,0:T(8,128)S(1)} %get-tuple-element.13), kind=kOutput, calls=%fused_computation.21 | convolution fusion | flops 453058560 | bytes 1474560 | tf_op jit(solution)/shard_map/rsjfk,jrkc->jsfc/dot_general | solution.py:77
  115.3 1.5 %copy.44 = f32[2,256,2,192]{3,0,2,1:T(2,128)S(1)} copy(f32[2,256,2,192]{1,3,2,0:T(8,128)} %convolution_bitcast_fusion) | data formatting | bytes 1572864 | tf_op jit(solution)/shard_map/rsjfk,jrkc->jsfc/dot_general | solution.py:77
  116.8 1.6 %fusion.7 = f32[2,192,1024]{2,1,0:T(8,128)S(1)} fusion(f32[512,512]{1,0:T(8,128)S(1)} %bitcast.75, f32[512,512]{1,0:T(8,128)S(1)} %bitcast.74, f32[2,512,192]{2,0,1:T(2,128)S(1)} %bitcast.73), kind=kOutput, calls=%fused_computation.11 | convolution fusion | flops 1208483840 | bytes 4456448 | tf_op jit(solution)/shard_map/jts,tw->jsw/dot_general | solution.py:82
  118.4 0.9 fusion.21
  (12 shorter events, 0.2 us)
Async XLA Ops:
  3.5 30.2 %all-to-all-start = ((bf16[512,8,195]{0,2,1:T(8,128)(2,1)}), bf16[512,8,195]{0,2,1:T(8,128)(2,1)}, u32[]{:S(2)}, u32[]{:S(2)}) async-start(bf16[512,8,195]{0,2,1:T(8,128)(2,1)} %pad_maximum_fusion), calls=%async_computation | async-start | bytes 3276800 | tf_op jit(solution)/shard_map/all_to_all | solution.py:57
  13.0 3.4 %copy-start.1 = (s32[512,3]{0,1:T(4,128)S(1)}, s32[512,3]{0,1:T(4,128)}, u32[]{:S(2)}) copy-start(s32[512,3]{0,1:T(4,128)} %param.6) | copy-start | bytes 18436
  13.0 3.7 %copy-start = (f32[2,2,96,96]{3,2,1,0:T(8,128)S(1)}, f32[2,2,96,96]{3,2,1,0:T(8,128)}, u32[]{:S(2)}) copy-start(f32[2,2,96,96]{3,2,1,0:T(8,128)} %param.7) | copy-start | bytes 442372
  81.7 32.0 %all-to-all-start.1 = ((bf16[2,256,2,2,96]{4,0,3,2,1:T(2,128)(2,1)}), bf16[2,256,2,2,96]{4,0,3,2,1:T(2,128)(2,1)S(1)}, u32[]{:S(2)}, u32[]{:S(2)}) async-start(bf16[2,256,2,2,96]{4,0,3,2,1:T(2,128)(2,1)} %copy.39), calls=%async_computation.1 | async-start | bytes 1048576 | tf_op jit(solution)/shard_map/all_to_all | solution.py:67

commit v8 on v6

--- a/solution.py
+++ b/solution.py
@@ -10,9 +10,9 @@
 
 def phase_rows(q_coords, cell_coords):
     products = (
-        q_coords[:, None, 0] * cell_coords[None, :, 0]
-        + q_coords[:, None, 1] * cell_coords[None, :, 1]
-        + q_coords[:, None, 2] * cell_coords[None, :, 2]
+        q_coords[0][:, None] * cell_coords[None, :, 0]
+        + q_coords[1][:, None] * cell_coords[None, :, 1]
+        + q_coords[2][:, None] * cell_coords[None, :, 2]
     ) % L
     angles = products.astype(jnp.float32) * (2.0 * math.pi / L)
     return jnp.cos(angles).astype(jnp.bfloat16), (-jnp.sin(angles)).astype(jnp.bfloat16)
@@ -40,16 +40,17 @@
     q_total = q_coords.shape[0]
     q_local = q_total // (n_tm * n_cell)
     frames = frames_dev * n_tm
-    ordered_coords = (
-        q_coords.reshape(n_tm, n_cell, q_local, 3).transpose(1, 0, 2, 3).reshape(q_total, 3)
-    )
+    ordered_coords = [
+        q_coords[:, d].reshape(n_tm, n_cell, q_local).transpose(1, 0, 2).reshape(q_total)
+        for d in range(3)
+    ]
     cos_rows, sin_rows = phase_rows(ordered_coords, cell_coords)
     table = jnp.stack(
         [
-            cos_rows.reshape(n_cell, n_tm, q_local, cell_dev),
-            sin_rows.reshape(n_cell, n_tm, q_local, cell_dev),
+            cos_rows.reshape(n_cell, n_tm * q_local, cell_dev),
+            sin_rows.reshape(n_cell, n_tm * q_local, cell_dev),
         ],
-        axis=2,
+        axis=1,
     ).reshape(2 * q_total, cell_dev)
     velocity_rows = velocity.reshape(cell_dev, frames_dev * branches)
     partial_term = jnp.dot(table, velocity_rows, preferred_element_type=jnp.float32)
@@ -58,7 +59,7 @@
     )
     gathered = lax.all_to_all(partial_term, "cell", split_axis=0, concat_axis=0, tiled=True)
     summed = jnp.sum(gathered.astype(jnp.float32), axis=0).astype(jnp.bfloat16)
-    blocks = summed.reshape(n_tm, 2, q_local, frames_dev, branches)
+    blocks = summed.reshape(2, n_tm, q_local, frames_dev, branches).transpose(1, 0, 2, 3, 4)
     collected = lax.all_to_all(blocks, "tm", split_axis=0, concat_axis=0, tiled=True)
     collected = collected.astype(jnp.float32)
 

time: 95.9 us -> 93.2 us (0.972)
  local copies, waits for them, and re-layouts: 6.48 us -> 5.02 us
  matrix products: 6.98 us -> 5.79 us
    reshape x5 -> x1, local copies, waits for them, and re-layouts: 3.93 us -> 0.45 us  [local(): summed.reshape(2, n_tm, q_local, frames_dev, branches)]
    transpose x1 -> x4, local copies, waits for them, and re-layouts: 0.07 us -> 1.63 us  [the longest x1 0.87 us: local(): summed.reshape(2, n_tm, q_local, frames_dev, branches)]
    dot_general x1, matrix products: 4.69 us -> 3.51 us  [local(): jnp.dot(table, velocity_rows, preferred_element_type=jnp.float32)]
where the time goes in v8:
time: 93.2 us; the launch traced here: 92.8 us
  waiting for transfers between devices  53.5 us (57%)
  starting transfers between devices  18.2 us (20%)
  other arithmetic  10.2 us (11%)
  matrix products  5.79 us (6%)
  local copies, waits for them, and re-layouts  5.02 us (5%)
    all_to_all x1, waiting for transfers between devices, local(): lax.all_to_all(partial_term, 'cell', split_axis=0, concat_axis=0, tiled=T...  38.8 us
    all_to_all x1, waiting for transfers between devices, local(): lax.all_to_all(blocks, 'tm', split_axis=0, concat_axis=0, tiled=True)  14.7 us
    all_to_all x1, starting transfers between devices, local(): lax.all_to_all(blocks, 'tm', split_axis=0, concat_axis=0, tiled=True)  10.6 us
    all_to_all x1, starting transfers between devices, local(): lax.all_to_all(partial_term, 'cell', split_axis=0, concat_axis=0, tiled=T...  7.61 us
    convert_element_type x1, other arithmetic, phase_rows(): jnp.cos(angles).astype(jnp.bfloat16)  4.84 us
    dot_general x1, matrix products, local(): jnp.dot(table, velocity_rows, preferred_element_type=jnp.float32)  3.51 us
    reduce_sum x1, other arithmetic, local(): summed = jnp.sum(gathered.astype(jnp.float32), axis=0).astype(jnp.bfloat16)  2.45 us
  transfers between devices with their start and end apart: 2, of which 2 were waited for; matrix products, arithmetic and copies ran while one was open for 2% of the time, Pallas kernels for 0%

profile of v8, /device:TPU:1, one launch (start us, length us, event | category | flops | bytes accessed | tf_op | source)
XLA Modules:
  0.0 92.8 jit_solution(9976441073236053252)
XLA Ops:
  0.0 0.0 copy-start
  0.0 0.9 slice_reduce_fusion.2
  0.9 0.1 reshape_squeeze.9
  1.0 0.3 copy.20
  1.3 0.1 copy.21
  1.3 0.2 reshape_squeeze.10
  1.5 0.3 copy.22
  1.8 0.1 copy.23
  1.8 0.2 reshape_squeeze.11
  2.0 0.3 copy.24
  2.2 0.1 copy.25
  2.3 0.8 fusion.35
  3.2 4.8 %cosine_convert_fusion = (bf16[8,1,64,512]{3,2,1,0:T(8,128)(2,1)S(1)}, bf16[8,1,64,512]{3,2,1,0:T(8,128)(2,1)S(1)}) fusion(s32[512]{0:T(512)S(1)} %bitcast.66, s32[8,64]{1,0:T(8,128)S(1)} %copy.25, s32[512]{0:T(512)S(1)} %bitcast.67, s32[8,64]{1,0:T(8,128)S(1)} %copy.23, s32[512]{0:T(512)S(1)} %bitcast.65, s32[8,64]{1,0:T(8,128)S(1)} %copy.21), kind=kLoop, calls=%fused_computation.15 | loop fusion | flops 5505024 | bytes 1060864 | tf_op jit(solution)/shard_map/convert_element_type | solution.py:18
  8.0 0.1 pad_maximum_fusion
  8.1 0.0 copy-done
  8.1 3.5 %convolution_convert_fusion = bf16[1024,1536]{1,0:T(8,128)(2,1)} fusion(bf16[1024,512]{1,0:T(8,128)(2,1)S(1)} %bitcast.58, bf16[512,1536]{0,1:T(8,128)(2,1)S(1)} %bitcast.52), kind=kOutput, calls=%fused_computation | convolution fusion | flops 1612185600 | bytes 5767168 | tf_op jit(solution)/shard_map/dot_general | solution.py:56
  11.6 0.0 copy-start.2
  11.6 7.6 %all-to-all-start = ((bf16[8,128,1536]{2,1,0:T(8,128)(2,1)}), bf16[8,128,1536]{2,1,0:T(8,128)(2,1)}, u32[]{:S(2)}, u32[]{:S(2)}) async-start(bf16[8,128,1536]{2,1,0:T(8,128)(2,1)} %bitcast.56), calls=%async_computation | async-start | bytes 6291456 | tf_op jit(solution)/shard_map/all_to_all | solution.py:60
  19.2 0.0 copy-done.2
  19.3 38.8 %all-to-all-done = bf16[8,128,1536]{2,1,0:T(8,128)(2,1)} async-done(((bf16[8,128,1536]{2,1,0:T(8,128)(2,1)}), bf16[8,128,1536]{2,1,0:T(8,128)(2,1)}, u32[]{:S(2)}, u32[]{:S(2)}) %all-to-all-start) | async-done | bytes 3145760 | tf_op jit(solution)/shard_map/all_to_all | solution.py:60
  58.1 2.4 %reduce_sum.12 = bf16[128,1536]{1,0:T(8,128)(2,1)S(1)} reduce(bf16[8,128,1536]{2,1,0:T(8,128)(2,1)} %all-to-all-done, bf16[]{:T(256)} %constant.48.clone.1), dimensions={0}, to_apply=%region_0.1 | reduce | flops 1376256 | bytes 3538946 | tf_op jit(solution)/shard_map/reduce_sum | solution.py:61
  60.6 0.5 reshape.255
  61.0 0.9 copy.26
  61.9 10.6 %all-to-all-start.1 = ((bf16[32,2,2,16,96]{4,3,1,2,0:T(8,128)(2,1)}), bf16[32,2,2,16,96]{4,3,1,2,0:T(8,128)(2,1)S(1)}, u32[]{:S(2)}, u32[]{:S(2)}) async-start(bf16[32,2,2,16,96]{4,3,1,2,0:T(8,128)(2,1)} %copy.26), calls=%async_computation.1 | async-start | bytes 1048576 | tf_op jit(solution)/shard_map/all_to_all | solution.py:63
  72.5 0.1 fusion.30
  72.6 0.3 fusion.27
  72.9 0.2 maximum_bitcast_fusion.4
  73.1 1.3 %multiply_subtract_fusion = (f32[32,16,512]{2,1,0:T(8,128)S(1)}, f32[32,16,512]{2,1,0:T(8,128)}) fusion(f32[16,512]{1,0:T(8,128)S(1)} %get-tuple-element.21, f32[32,512]{1,0:T(8,128)S(1)} %get-tuple-element.19, f32[16,512]{1,0:T(8,128)S(1)} %get-tuple-element.22, f32[32,512]{1,0:T(8,128)S(1)} %get-tuple-element.20), kind=kLoop, calls=%fused_computation.13 | loop fusion | flops 1572864 | bytes 2293760 | tf_op jit(solution)/shard_map/sub | solution.py:31
  74.4 14.7 %all-to-all-done.1 = bf16[32,2,2,16,96]{4,3,1,2,0:T(8,128)(2,1)S(1)} async-done(((bf16[32,2,2,16,96]{4,3,1,2,0:T(8,128)(2,1)}), bf16[32,2,2,16,96]{4,3,1,2,0:T(8,128)(2,1)S(1)}, u32[]{:S(2)}, u32[]{:S(2)}) %all-to-all-start.1) | async-done | bytes 393248 | tf_op jit(solution)/shard_map/all_to_all | solution.py:63
  89.0 0.0 copy-start.1
  89.0 0.6 fusion.6
  89.7 0.6 copy-done.1
  90.3 1.6 %fusion = f32[2,192,1024]{2,1,0:T(8,128)S(1)} fusion(f32[2,512,192]{2,1,0:T(8,128)S(1)} %bitcast.55, f32[512,512]{1,0:T(8,128)S(1)} %bitcast.54, f32[512,512]{1,0:T(8,128)S(1)} %bitcast.53), kind=kOutput, calls=%fused_computation.2 | convolution fusion | flops 1208483840 | bytes 4456448 | tf_op jit(solution)/shard_map/jts,tw->jsw/dot_general | solution.py:79
  91.9 0.9 fusion.10
  (2 shorter events, 0.0 us)
Async XLA Ops:
  0.0 8.1 %copy-start = (bf16[512,16,96]{0,2,1:T(8,128)(2,1)S(1)}, bf16[512,16,96]{0,2,1:T(8,128)(2,1)}, u32[]{:S(2)}) copy-start(bf16[512,16,96]{0,2,1:T(8,128)(2,1)} %param.4) | copy-start | bytes 4718596
  11.6 7.6 %copy-start.2 = (f32[2,2,96,96]{3,2,1,0:T(8,128)S(1)}, f32[2,2,96,96]{3,2,1,0:T(8,128)}, u32[]{:S(2)}) copy-start(f32[2,2,96,96]{3,2,1,0:T(8,128)} %param.7) | copy-start | bytes 442372
  11.6 46.5 %all-to-all-start = ((bf16[8,128,1536]{2,1,0:T(8,128)(2,1)}), bf16[8,128,1536]{2,1,0:T(8,128)(2,1)}, u32[]{:S(2)}, u32[]{:S(2)}) async-start(bf16[8,128,1536]{2,1,0:T(8,128)(2,1)} %bitcast.56), calls=%async_computation | async-start | bytes 6291456 | tf_op jit(solution)/shard_map/all_to_all | solution.py:60
  61.9 27.1 %all-to-all-start.1 = ((bf16[32,2,2,16,96]{4,3,1,2,0:T(8,128)(2,1)}), bf16[32,2,2,16,96]{4,3,1,2,0:T(8,128)(2,1)S(1)}, u32[]{:S(2)}, u32[]{:S(2)}) async-start(bf16[32,2,2,16,96]{4,3,1,2,0:T(8,128)(2,1)} %copy.26), calls=%async_computation.1 | async-start | bytes 1048576 | tf_op jit(solution)/shard_map/all_to_all | solution.py:63
  89.0 1.2 %copy-start.1 = (f32[32,16,512]{2,1,0:T(8,128)S(1)}, f32[32,16,512]{2,1,0:T(8,128)}, u32[]{:S(2)}) copy-start(f32[32,16,512]{2,1,0:T(8,128)} %get-tuple-element.9) | copy-start | bytes 3145732

commit v9 on v8

--- a/solution.py
+++ b/solution.py
@@ -3,19 +3,56 @@
 import jax
 import jax.numpy as jnp
 from jax import lax
+from jax.experimental import pallas as pl
 from jax.sharding import PartitionSpec as P
+import numpy as np
 
 L = 16
 
 
-def phase_rows(q_coords, cell_coords):
-    products = (
-        q_coords[0][:, None] * cell_coords[None, :, 0]
-        + q_coords[1][:, None] * cell_coords[None, :, 1]
-        + q_coords[2][:, None] * cell_coords[None, :, 2]
-    ) % L
-    angles = products.astype(jnp.float32) * (2.0 * math.pi / L)
-    return jnp.cos(angles).astype(jnp.bfloat16), (-jnp.sin(angles)).astype(jnp.bfloat16)
+def quarter_tables():
+    step = np.arange(4, dtype=np.float32) * np.float32(2.0 * math.pi / L)
+    cos_k = np.cos(step).astype(jnp.bfloat16).astype(np.float32)
+    sin_k = (-np.sin(step)).astype(jnp.bfloat16).astype(np.float32)
+    return [float(v) for v in cos_k], [float(v) for v in sin_k]
+
+
+def phase_sum_kernel(qx_ref, qy_ref, qz_ref, cx_ref, cy_ref, cz_ref, v_ref, o_ref):
+    cos_k, sin_k = quarter_tables()
+    m = (qx_ref[0] * cx_ref[...] + qy_ref[0] * cy_ref[...] + qz_ref[0] * cz_ref[...]) & (L - 1)
+    bit0 = (m & 1) != 0
+    bit1 = (m & 2) != 0
+    bit2 = (m & 4) != 0
+    bit3 = (m & 8) != 0
+    real = jnp.where(bit1, jnp.where(bit0, cos_k[3], cos_k[2]), jnp.where(bit0, cos_k[1], cos_k[0]))
+    imag = jnp.where(bit1, jnp.where(bit0, sin_k[3], sin_k[2]), jnp.where(bit0, sin_k[1], sin_k[0]))
+    real, imag = jnp.where(bit2, imag, real), jnp.where(bit2, -real, imag)
+    real, imag = jnp.where(bit3, -real, real), jnp.where(bit3, -imag, imag)
+    v = v_ref[...]
+    o_ref[0, 0] = jnp.dot(real.astype(jnp.bfloat16), v, preferred_element_type=jnp.float32).astype(o_ref.dtype)
+    o_ref[0, 1] = jnp.dot(imag.astype(jnp.bfloat16), v, preferred_element_type=jnp.float32).astype(o_ref.dtype)
+
+
+def phase_sums(q_columns, cell_coords, velocity_rows, groups):
+    q_total = q_columns[0].shape[0]
+    rows = q_total // groups
+    cells, width = velocity_rows.shape
+    q_in = [col.reshape(groups, rows, 1) for col in q_columns]
+    c_in = [cell_coords[:, d].reshape(1, cells) for d in range(3)]
+    q_spec = pl.BlockSpec((1, rows, 1), lambda i: (i, 0, 0))
+    c_spec = pl.BlockSpec((1, cells), lambda i: (0, 0))
+    return pl.pallas_call(
+        phase_sum_kernel,
+        grid=(groups,),
+        in_specs=[q_spec] * 3 + [c_spec] * 3 + [pl.BlockSpec((cells, width), lambda i: (0, 0))],
+        out_specs=pl.BlockSpec((1, 2, rows, width), lambda i: (i, 0, 0, 0)),
+        out_shape=jax.ShapeDtypeStruct((groups, 2, rows, width), jnp.bfloat16),
+        cost_estimate=pl.CostEstimate(
+            flops=4 * q_total * cells * width,
+            transcendentals=0,
+            bytes_accessed=2 * cells * width + 4 * q_total * width,
+        ),
+    )(*q_in, *c_in, velocity_rows)
 
 
 def twiddles(frames):
@@ -44,17 +81,8 @@
         q_coords[:, d].reshape(n_tm, n_cell, q_local).transpose(1, 0, 2).reshape(q_total)
         for d in range(3)
     ]
-    cos_rows, sin_rows = phase_rows(ordered_coords, cell_coords)
-    table = jnp.stack(
-        [
-            cos_rows.reshape(n_cell, n_tm * q_local, cell_dev),
-            sin_rows.reshape(n_cell, n_tm * q_local, cell_dev),
-        ],
-        axis=1,
-    ).reshape(2 * q_total, cell_dev)
     velocity_rows = velocity.reshape(cell_dev, frames_dev * branches)
-    partial_term = jnp.dot(table, velocity_rows, preferred_element_type=jnp.float32)
-    partial_term = partial_term.astype(jnp.bfloat16).reshape(
+    partial_term = phase_sums(ordered_coords, cell_coords, velocity_rows, n_cell).reshape(
         n_cell, 2 * n_tm * q_local, frames_dev * branches
     )
     gathered = lax.all_to_all(partial_term, "cell", split_axis=0, concat_axis=0, tiled=True)

time: 93.2 us -> 97 us (1.041)
  Pallas kernels: 0 us -> 8.96 us
  other arithmetic: 10.2 us -> 3.06 us
  local copies, waits for them, and re-layouts: 5.02 us -> 9.85 us
  matrix products: 5.79 us -> 2.23 us
    pallas_call x0 -> x1, Pallas kernels: none -> 8.96 us  [phase_sums(): pl.pallas_call(phase_sum_kernel, grid=(groups,), in_specs=[q_spec] * 3 +...]
    another operation x0 -> x4, local copies, waits for them, and re-layouts: none -> 4.92 us  [the longest x3 3.51 us: phase_sums(): q_in = [col.reshape(groups, rows, 1) for col in q_columns]]
    convert_element_type x1 -> x0, other arithmetic: 4.84 us -> none  [phase_rows(): jnp.cos(angles).astype(jnp.bfloat16)]
    dot_general x1 -> x0, matrix products: 3.51 us -> none  [local(): jnp.dot(table, velocity_rows, preferred_element_type=jnp.float32)]
    reduce_sum x1, other arithmetic: 2.45 us -> 0.58 us  [local(): summed = jnp.sum(gathered.astype(jnp.float32), axis=0).astype(jnp.bfloat16)]
    reshape x0 -> x1, local copies, waits for them, and re-layouts: none -> 1.57 us  [local(): velocity_rows = velocity.reshape(cell_dev, frames_dev * branches)]
    sub x1, other arithmetic: 1.29 us -> 0.31 us  [twiddles(): cosines = (cos_c * cos_f - sin_c * sin_f).reshape(frames, frames)]
where the time goes in v9:
time: 97 us; the launch traced here: 96.1 us
  waiting for transfers between devices  53.7 us (55%)
  starting transfers between devices  18.2 us (19%)
  local copies, waits for them, and re-layouts  9.85 us (10%)
  Pallas kernels  8.96 us (9%)
  other arithmetic  3.06 us (3%)
  matrix products  2.23 us (2%)
    all_to_all x1, waiting for transfers between devices, local(): lax.all_to_all(partial_term, 'cell', split_axis=0, concat_axis=0, tiled=T...  38.1 us
    all_to_all x1, waiting for transfers between devices, local(): lax.all_to_all(blocks, 'tm', split_axis=0, concat_axis=0, tiled=True)  15.6 us
    all_to_all x1, starting transfers between devices, local(): lax.all_to_all(blocks, 'tm', split_axis=0, concat_axis=0, tiled=True)  10.6 us
    pallas_call x1, Pallas kernels, phase_sums(): pl.pallas_call(phase_sum_kernel, grid=(groups,), in_specs=[q_spec] * 3 +...  8.96 us
    all_to_all x1, starting transfers between devices, local(): lax.all_to_all(partial_term, 'cell', split_axis=0, concat_axis=0, tiled=T...  7.61 us
    another operation x3, local copies, waits for them, and re-layouts, phase_sums(): q_in = [col.reshape(groups, rows, 1) for col in q_columns]  3.51 us
  transfers between devices with their start and end apart: 2, of which 2 were waited for; matrix products, arithmetic and copies ran while one was open for 2% of the time, Pallas kernels for 0%

profile of v9, /device:TPU:1, one launch (start us, length us, event | category | flops | bytes accessed | tf_op | source)
XLA Modules:
  0.0 96.1 jit_solution(13933196893313635066)
XLA Ops:
  0.0 0.0 copy-start
  0.0 0.9 slice_reduce_fusion
  0.9 0.1 reshape_squeeze.18
  1.0 0.3 copy.25
  1.3 1.2 %copy.28.qx_ref = s32[8,64,1]{2,1,0:T(8,128)} copy(s32[8,64,1]{0,1,2:T(8,128)S(1)} %bitcast.61) | data formatting | bytes 4096 | tf_op jit(solution)/shard_map/reshape;reshape | solution.py:40
  2.4 0.1 reshape_squeeze.19
  2.6 0.3 copy.26
  2.8 1.2 %copy.29.qy_ref = s32[8,64,1]{2,1,0:T(8,128)} copy(s32[8,64,1]{0,1,2:T(8,128)S(1)} %bitcast.62) | data formatting | bytes 4096 | tf_op jit(solution)/shard_map/reshape;reshape | solution.py:40
  4.0 0.1 reshape_squeeze.20
  4.2 0.3 copy.27
  4.4 1.2 %copy.30.qz_ref = s32[8,64,1]{2,1,0:T(8,128)} copy(s32[8,64,1]{0,1,2:T(8,128)S(1)} %bitcast.63) | data formatting | bytes 4096 | tf_op jit(solution)/shard_map/reshape;reshape | solution.py:40
  5.6 1.4 %slice_bitcast_fusion = (s32[1,512]{1,0:T(1,128)}, s32[1,512]{1,0:T(1,128)}, s32[1,512]{1,0:T(1,128)}) fusion(s32[512,3]{0,1:T(4,128)} %param.5), kind=kLoop, calls=%fused_computation.45 | loop fusion | bytes 12288 | tf_op jit(solution)/shard_map/reshape;squeeze | solution.py:41
  7.0 0.0 copy-done
  7.0 1.6 %copy.31.v_ref = bf16[512,1536]{1,0:T(8,128)(2,1)} copy(bf16[512,1536]{0,1:T(8,128)(2,1)S(1)} %bitcast.57) | data formatting | bytes 3145728 | tf_op jit(solution)/shard_map/reshape | solution.py:84
  8.6 9.0 %shard_map.46 = bf16[8,2,64,1536]{3,2,1,0:T(8,128)(2,1)} custom-call(s32[8,64,1]{2,1,0:T(8,128)} %copy.28.qx_ref, s32[8,64,1]{2,1,0:T(8,128)} %copy.29.qy_ref, s32[8,64,1]{2,1,0:T(8,128)} %copy.30.qz_ref, s32[1,512]{1,0:T(1,128)} %get-tuple-element.15.cx_ref, s32[1,512]{1,0:T(1,128)} %get-tuple-element.16.cy_ref, s32[1,512]{1,0:T(1,128)} %get-tuple-element.14.cz_ref, ...), custom_call_target="tpu_custom_call" | custom-call | flops 1610612736 | bytes 4718592 | tf_op jit(solution)/shard_map/pallas_call | solution.py:44
  17.5 0.0 copy-start.1
  17.5 7.6 %all-to-all-start = ((bf16[8,128,1536]{2,1,0:T(8,128)(2,1)}), bf16[8,128,1536]{2,1,0:T(8,128)(2,1)S(1)}, u32[]{:S(2)}, u32[]{:S(2)}) async-start(bf16[8,128,1536]{2,1,0:T(8,128)(2,1)} %bitcast.55), calls=%async_computation | async-start | bytes 6291456 | tf_op jit(solution)/shard_map/all_to_all | solution.py:88
  25.1 0.0 copy-done.1
  25.1 0.6 fusion.31
  25.8 38.1 %all-to-all-done = bf16[8,128,1536]{2,1,0:T(8,128)(2,1)S(1)} async-done(((bf16[8,128,1536]{2,1,0:T(8,128)(2,1)}), bf16[8,128,1536]{2,1,0:T(8,128)(2,1)S(1)}, u32[]{:S(2)}, u32[]{:S(2)}) %all-to-all-start) | async-done | bytes 3145760 | tf_op jit(solution)/shard_map/all_to_all | solution.py:88
  63.8 0.6 reduce_sum.12
  64.4 0.0 copy-start.2
  64.4 0.0 copy-start.3
  64.5 0.5 reshape.104
  64.9 0.9 copy.32
  65.8 10.6 %all-to-all-start.1 = ((bf16[32,2,2,16,96]{4,3,1,2,0:T(8,128)(2,1)}), bf16[32,2,2,16,96]{4,3,1,2,0:T(8,128)(2,1)S(1)}, u32[]{:S(2)}, u32[]{:S(2)}) async-start(bf16[32,2,2,16,96]{4,3,1,2,0:T(8,128)(2,1)} %copy.32), calls=%async_computation.1 | async-start | bytes 1048576 | tf_op jit(solution)/shard_map/all_to_all | solution.py:91
  76.4 0.1 fusion.27
  76.5 0.3 fusion.24
  76.8 0.0 copy-done.2
  76.8 0.0 copy-done.3
  76.9 0.2 maximum_bitcast_fusion.4
  77.0 0.3 multiply_subtract_fusion
  77.3 15.6 %all-to-all-done.1 = bf16[32,2,2,16,96]{4,3,1,2,0:T(8,128)(2,1)S(1)} async-done(((bf16[32,2,2,16,96]{4,3,1,2,0:T(8,128)(2,1)}), bf16[32,2,2,16,96]{4,3,1,2,0:T(8,128)(2,1)S(1)}, u32[]{:S(2)}, u32[]{:S(2)}) %all-to-all-start.1) | async-done | bytes 393248 | tf_op jit(solution)/shard_map/all_to_all | solution.py:91
  93.0 0.7 fusion.3
  93.6 1.6 %fusion = f32[2,192,1024]{2,1,0:T(8,128)S(1)} fusion(f32[2,512,192]{2,1,0:T(8,128)S(1)} %bitcast.54, f32[512,512]{1,0:T(8,128)S(1)} %bitcast.53, f32[512,512]{1,0:T(8,128)S(1)} %bitcast.52), kind=kOutput, calls=%fused_computation.1 | convolution fusion | flops 1208483840 | bytes 4456448 | tf_op jit(solution)/shard_map/jts,tw->jsw/dot_general | solution.py:107
  95.2 0.9 fusion.7
  (1 shorter events, 0.0 us)
Async XLA Ops:
  0.0 7.0 %copy-start = (bf16[512,16,96]{0,2,1:T(8,128)(2,1)S(1)}, bf16[512,16,96]{0,2,1:T(8,128)(2,1)}, u32[]{:S(2)}) copy-start(bf16[512,16,96]{0,2,1:T(8,128)(2,1)} %param.4) | copy-start | bytes 4718596
  17.5 7.6 %copy-start.1 = (f32[2,2,96,96]{3,2,1,0:T(8,128)S(1)}, f32[2,2,96,96]{3,2,1,0:T(8,128)}, u32[]{:S(2)}) copy-start(f32[2,2,96,96]{3,2,1,0:T(8,128)} %param.7) | copy-start | bytes 442372
  17.5 46.3 %all-to-all-start = ((bf16[8,128,1536]{2,1,0:T(8,128)(2,1)}), bf16[8,128,1536]{2,1,0:T(8,128)(2,1)S(1)}, u32[]{:S(2)}, u32[]{:S(2)}) async-start(bf16[8,128,1536]{2,1,0:T(8,128)(2,1)} %bitcast.55), calls=%async_computation | async-start | bytes 6291456 | tf_op jit(solution)/shard_map/all_to_all | solution.py:88
  64.4 12.4 %copy-start.2 = (f32[2,2,96,96]{3,2,1,0:T(8,128)S(1)}, f32[2,2,96,96]{3,2,1,0:T(8,128)}, u32[]{:S(2)}) copy-start(f32[2,2,96,96]{3,2,1,0:T(8,128)} %param.7) | copy-start | bytes 442372
  64.4 12.4 %copy-start.3 = (f32[2,96,96]{2,1,0:T(8,128)S(1)}, f32[2,96,96]{2,1,0:T(8,128)}, u32[]{:S(2)}) copy-start(f32[2,96,96]{2,1,0:T(8,128)} %fusion.31) | copy-start | bytes 221188
  65.8 27.2 %all-to-all-start.1 = ((bf16[32,2,2,16,96]{4,3,1,2,0:T(8,128)(2,1)}), bf16[32,2,2,16,96]{4,3,1,2,0:T(8,128)(2,1)S(1)}, u32[]{:S(2)}, u32[]{:S(2)}) async-start(bf16[32,2,2,16,96]{4,3,1,2,0:T(8,128)(2,1)} %copy.32), calls=%async_computation.1 | async-start | bytes 1048576 | tf_op jit(solution)/shard_map/all_to_all | solution.py:91

commit v10 on v9

--- a/solution.py
+++ b/solution.py
@@ -17,9 +17,10 @@
     return [float(v) for v in cos_k], [float(v) for v in sin_k]
 
 
-def phase_sum_kernel(qx_ref, qy_ref, qz_ref, cx_ref, cy_ref, cz_ref, v_ref, o_ref):
+def phase_sum_kernel(c_ref, q_ref, vt_ref, o_ref):
     cos_k, sin_k = quarter_tables()
-    m = (qx_ref[0] * cx_ref[...] + qy_ref[0] * cy_ref[...] + qz_ref[0] * cz_ref[...]) & (L - 1)
+    dots = jnp.dot(c_ref[...], q_ref[0], preferred_element_type=jnp.float32)
+    m = dots.astype(jnp.int32) & (L - 1)
     bit0 = (m & 1) != 0
     bit1 = (m & 2) != 0
     bit2 = (m & 4) != 0
@@ -28,31 +29,34 @@
     imag = jnp.where(bit1, jnp.where(bit0, sin_k[3], sin_k[2]), jnp.where(bit0, sin_k[1], sin_k[0]))
     real, imag = jnp.where(bit2, imag, real), jnp.where(bit2, -real, imag)
     real, imag = jnp.where(bit3, -real, real), jnp.where(bit3, -imag, imag)
-    v = v_ref[...]
-    o_ref[0, 0] = jnp.dot(real.astype(jnp.bfloat16), v, preferred_element_type=jnp.float32).astype(o_ref.dtype)
-    o_ref[0, 1] = jnp.dot(imag.astype(jnp.bfloat16), v, preferred_element_type=jnp.float32).astype(o_ref.dtype)
+    column = lax.broadcasted_iota(jnp.int32, m.shape, 1)
+    phase = jnp.where(column < m.shape[1] // 2, real, imag).astype(jnp.bfloat16)
+    o_ref[0] = jnp.dot(vt_ref[...], phase, preferred_element_type=jnp.float32).astype(o_ref.dtype)
 
 
-def phase_sums(q_columns, cell_coords, velocity_rows, groups):
-    q_total = q_columns[0].shape[0]
-    rows = q_total // groups
-    cells, width = velocity_rows.shape
-    q_in = [col.reshape(groups, rows, 1) for col in q_columns]
-    c_in = [cell_coords[:, d].reshape(1, cells) for d in range(3)]
-    q_spec = pl.BlockSpec((1, rows, 1), lambda i: (i, 0, 0))
-    c_spec = pl.BlockSpec((1, cells), lambda i: (0, 0))
+def phase_sums(q_columns, cell_coords, velocity_t):
+    groups, _, rows = q_columns.shape
+    width, cells = velocity_t.shape
+    pad = 8
+    c_in = jnp.pad(cell_coords, ((0, 0), (0, pad - 3))).astype(jnp.bfloat16)
+    q_in = jnp.pad(jnp.concatenate([q_columns, q_columns], axis=2), ((0, 0), (0, pad - 3), (0, 0)))
+    q_in = q_in.astype(jnp.bfloat16)
     return pl.pallas_call(
         phase_sum_kernel,
         grid=(groups,),
-        in_specs=[q_spec] * 3 + [c_spec] * 3 + [pl.BlockSpec((cells, width), lambda i: (0, 0))],
-        out_specs=pl.BlockSpec((1, 2, rows, width), lambda i: (i, 0, 0, 0)),
-        out_shape=jax.ShapeDtypeStruct((groups, 2, rows, width), jnp.bfloat16),
+        in_specs=[
+            pl.BlockSpec((cells, pad), lambda i: (0, 0)),
+            pl.BlockSpec((1, pad, 2 * rows), lambda i: (i, 0, 0)),
+            pl.BlockSpec((width, cells), lambda i: (0, 0)),
+        ],
+        out_specs=pl.BlockSpec((1, width, 2 * rows), lambda i: (i, 0, 0)),
+        out_shape=jax.ShapeDtypeStruct((groups, width, 2 * rows), jnp.bfloat16),
         cost_estimate=pl.CostEstimate(
-            flops=4 * q_total * cells * width,
+            flops=4 * groups * rows * cells * width,
             transcendentals=0,
-            bytes_accessed=2 * cells * width + 4 * q_total * width,
+            bytes_accessed=2 * cells * width + 4 * groups * rows * width,
         ),
-    )(*q_in, *c_in, velocity_rows)
+    )(c_in, q_in, velocity_t)
 
 
 def twiddles(frames):
@@ -77,17 +81,13 @@
     q_total = q_coords.shape[0]
     q_local = q_total // (n_tm * n_cell)
     frames = frames_dev * n_tm
-    ordered_coords = [
-        q_coords[:, d].reshape(n_tm, n_cell, q_local).transpose(1, 0, 2).reshape(q_total)
-        for d in range(3)
-    ]
-    velocity_rows = velocity.reshape(cell_dev, frames_dev * branches)
-    partial_term = phase_sums(ordered_coords, cell_coords, velocity_rows, n_cell).reshape(
-        n_cell, 2 * n_tm * q_local, frames_dev * branches
-    )
+    q_columns = q_coords.reshape(n_tm, n_cell, q_local, 3).transpose(1, 3, 0, 2)
+    q_columns = q_columns.reshape(n_cell, 3, n_tm * q_local)
+    velocity_t = velocity.reshape(cell_dev, frames_dev * branches).T
+    partial_term = phase_sums(q_columns, cell_coords, velocity_t)
     gathered = lax.all_to_all(partial_term, "cell", split_axis=0, concat_axis=0, tiled=True)
     summed = jnp.sum(gathered.astype(jnp.float32), axis=0).astype(jnp.bfloat16)
-    blocks = summed.reshape(2, n_tm, q_local, frames_dev, branches).transpose(1, 0, 2, 3, 4)
+    blocks = summed.reshape(frames_dev, branches, 2, n_tm, q_local).transpose(3, 2, 4, 0, 1)
     collected = lax.all_to_all(blocks, "tm", split_axis=0, concat_axis=0, tiled=True)
     collected = collected.astype(jnp.float32)
 

time: 97 us -> 92.5 us (0.954)
  local copies, waits for them, and re-layouts: 9.85 us -> 3.5 us
  other arithmetic: 3.06 us -> 5.23 us
    another operation x7 -> x4, local copies, waits for them, and re-layouts: 5.33 us -> 1.3 us  [the longest x3 3.51 us: phase_sums(): q_in = [col.reshape(groups, rows, 1) for col in q_columns]]
    reshape x2 -> x1, local copies, waits for them, and re-layouts: 2.02 us -> 0.45 us  [local(): summed.reshape(frames_dev, branches, 2, n_tm, q_local)]
    another operation x0 -> x2, other arithmetic: none -> 1.41 us
where the time goes in v10:
time: 92.5 us; the launch traced here: 92.1 us
  waiting for transfers between devices  53.7 us (58%)
  starting transfers between devices  18.2 us (20%)
  Pallas kernels  9.15 us (10%)
  other arithmetic  5.23 us (6%)
  local copies, waits for them, and re-layouts  3.5 us (4%)
  matrix products  2.23 us (2%)
    all_to_all x1, waiting for transfers between devices, local(): lax.all_to_all(partial_term, 'cell', split_axis=0, concat_axis=0, tiled=T...  38.1 us
    all_to_all x1, waiting for transfers between devices, local(): lax.all_to_all(blocks, 'tm', split_axis=0, concat_axis=0, tiled=True)  15.6 us
    all_to_all x1, starting transfers between devices, local(): lax.all_to_all(blocks, 'tm', split_axis=0, concat_axis=0, tiled=True)  10.6 us
    pallas_call x1, Pallas kernels, phase_sums(): pl.pallas_call(phase_sum_kernel, grid=(groups,), in_specs=[pl.BlockSpec((...  9.15 us
    all_to_all x1, starting transfers between devices, local(): lax.all_to_all(partial_term, 'cell', split_axis=0, concat_axis=0, tiled=T...  7.61 us
  transfers between devices with their start and end apart: 2, of which 2 were waited for; matrix products, arithmetic and copies ran while one was open for 2% of the time, Pallas kernels for 0%

profile of v10, /device:TPU:1, one launch (start us, length us, event | category | flops | bytes accessed | tf_op | source)
XLA Modules:
  0.0 92.1 jit_solution(796268963516697834)
XLA Ops:
  0.0 0.7 convert.11
  0.7 0.2 copy.31
  0.9 0.7 convert.15
  1.6 0.4 reshape.111
  2.0 0.6 copy.32
  2.6 0.1 copy.33
  2.7 0.7 fusion.29.q_ref
  3.4 0.7 pad.10.c_ref
  4.1 9.2 %shard_map.46 = bf16[8,1536,128]{2,1,0:T(8,128)(2,1)} custom-call(bf16[512,8]{1,0:T(8,128)(2,1)} %pad.10.c_ref, bf16[8,8,128]{2,1,0:T(8,128)(2,1)} %fusion.29.q_ref, bf16[1536,512]{1,0:T(8,128)(2,1)} %bitcast.53), custom_call_target="tpu_custom_call" | custom-call | flops 1610612736 | bytes 4718592 | tf_op jit(solution)/shard_map/pallas_call | solution.py:44
  13.3 0.0 copy-start
  13.3 7.6 %all-to-all-start = ((bf16[8,1536,128]{2,1,0:T(8,128)(2,1)}), bf16[8,1536,128]{2,1,0:T(8,128)(2,1)S(1)}, u32[]{:S(2)}, u32[]{:S(2)}) async-start(bf16[8,1536,128]{2,1,0:T(8,128)(2,1)} %shard_map.46), calls=%async_computation | async-start | bytes 6291456 | tf_op jit(solution)/shard_map/all_to_all | solution.py:88
  20.9 0.0 copy-done
  20.9 0.6 fusion.34
  21.5 38.1 %all-to-all-done = bf16[8,1536,128]{2,1,0:T(8,128)(2,1)S(1)} async-done(((bf16[8,1536,128]{2,1,0:T(8,128)(2,1)}), bf16[8,1536,128]{2,1,0:T(8,128)(2,1)S(1)}, u32[]{:S(2)}, u32[]{:S(2)}) %all-to-all-start) | async-done | bytes 3145760 | tf_op jit(solution)/shard_map/all_to_all | solution.py:88
  59.6 0.7 reduce_sum.12
  60.3 0.0 copy-start.1
  60.3 0.0 copy-start.2
  60.3 0.2 copy.35
  60.5 0.5 reshape.108
  61.0 0.9 copy.36
  61.8 10.6 %all-to-all-start.1 = ((bf16[32,2,2,16,96]{4,3,1,2,0:T(8,128)(2,1)}), bf16[32,2,2,16,96]{4,3,1,2,0:T(8,128)(2,1)S(1)}, u32[]{:S(2)}, u32[]{:S(2)}) async-start(bf16[32,2,2,16,96]{4,3,1,2,0:T(8,128)(2,1)} %copy.36), calls=%async_computation.1 | async-start | bytes 1048576 | tf_op jit(solution)/shard_map/all_to_all | solution.py:91
  72.4 0.1 fusion.30
  72.5 0.3 fusion.26
  72.8 0.0 copy-done.1
  72.9 0.0 copy-done.2
  72.9 0.2 maximum_bitcast_fusion.4
  73.0 0.3 multiply_subtract_fusion
  73.4 15.6 %all-to-all-done.1 = bf16[32,2,2,16,96]{4,3,1,2,0:T(8,128)(2,1)S(1)} async-done(((bf16[32,2,2,16,96]{4,3,1,2,0:T(8,128)(2,1)}), bf16[32,2,2,16,96]{4,3,1,2,0:T(8,128)(2,1)S(1)}, u32[]{:S(2)}, u32[]{:S(2)}) %all-to-all-start.1) | async-done | bytes 393248 | tf_op jit(solution)/shard_map/all_to_all | solution.py:91
  89.0 0.7 fusion.3
  89.6 1.6 %fusion = f32[2,192,1024]{2,1,0:T(8,128)S(1)} fusion(f32[2,512,192]{2,1,0:T(8,128)S(1)} %bitcast.49, f32[512,512]{1,0:T(8,128)S(1)} %bitcast.48, f32[512,512]{1,0:T(8,128)S(1)} %bitcast.47), kind=kOutput, calls=%fused_computation.1 | convolution fusion | flops 1208483840 | bytes 4456448 | tf_op jit(solution)/shard_map/jts,tw->jsw/dot_general | solution.py:107
  91.2 0.9 fusion.7
  (1 shorter events, 0.0 us)
Async XLA Ops:
  13.3 7.6 %copy-start = (f32[2,2,96,96]{3,2,1,0:T(8,128)S(1)}, f32[2,2,96,96]{3,2,1,0:T(8,128)}, u32[]{:S(2)}) copy-start(f32[2,2,96,96]{3,2,1,0:T(8,128)} %param.7) | copy-start | bytes 442372
  13.3 46.4 %all-to-all-start = ((bf16[8,1536,128]{2,1,0:T(8,128)(2,1)}), bf16[8,1536,128]{2,1,0:T(8,128)(2,1)S(1)}, u32[]{:S(2)}, u32[]{:S(2)}) async-start(bf16[8,1536,128]{2,1,0:T(8,128)(2,1)} %shard_map.46), calls=%async_computation | async-start | bytes 6291456 | tf_op jit(solution)/shard_map/all_to_all | solution.py:88
  60.3 12.5 %copy-start.1 = (f32[2,2,96,96]{3,2,1,0:T(8,128)S(1)}, f32[2,2,96,96]{3,2,1,0:T(8,128)}, u32[]{:S(2)}) copy-start(f32[2,2,96,96]{3,2,1,0:T(8,128)} %param.7) | copy-start | bytes 442372
  60.3 12.6 %copy-start.2 = (f32[2,96,96]{2,1,0:T(8,128)S(1)}, f32[2,96,96]{2,1,0:T(8,128)}, u32[]{:S(2)}) copy-start(f32[2,96,96]{2,1,0:T(8,128)} %fusion.34) | copy-start | bytes 221188
  61.8 27.1 %all-to-all-start.1 = ((bf16[32,2,2,16,96]{4,3,1,2,0:T(8,128)(2,1)}), bf16[32,2,2,16,96]{4,3,1,2,0:T(8,128)(2,1)S(1)}, u32[]{:S(2)}, u32[]{:S(2)}) async-start(bf16[32,2,2,16,96]{4,3,1,2,0:T(8,128)(2,1)} %copy.36), calls=%async_computation.1 | async-start | bytes 1048576 | tf_op jit(solution)/shard_map/all_to_all | solution.py:91

commit v11 on v10

--- a/solution.py
+++ b/solution.py
@@ -4,6 +4,7 @@
 import jax.numpy as jnp
 from jax import lax
 from jax.experimental import pallas as pl
+from jax.experimental.pallas import tpu as pltpu
 from jax.sharding import PartitionSpec as P
 import numpy as np
 
@@ -17,40 +18,49 @@
     return [float(v) for v in cos_k], [float(v) for v in sin_k]
 
 
-def phase_sum_kernel(c_ref, q_ref, vt_ref, o_ref):
-    cos_k, sin_k = quarter_tables()
-    dots = jnp.dot(c_ref[...], q_ref[0], preferred_element_type=jnp.float32)
-    m = dots.astype(jnp.int32) & (L - 1)
-    bit0 = (m & 1) != 0
-    bit1 = (m & 2) != 0
-    bit2 = (m & 4) != 0
-    bit3 = (m & 8) != 0
-    real = jnp.where(bit1, jnp.where(bit0, cos_k[3], cos_k[2]), jnp.where(bit0, cos_k[1], cos_k[0]))
-    imag = jnp.where(bit1, jnp.where(bit0, sin_k[3], sin_k[2]), jnp.where(bit0, sin_k[1], sin_k[0]))
-    real, imag = jnp.where(bit2, imag, real), jnp.where(bit2, -real, imag)
-    real, imag = jnp.where(bit3, -real, real), jnp.where(bit3, -imag, imag)
-    column = lax.broadcasted_iota(jnp.int32, m.shape, 1)
-    phase = jnp.where(column < m.shape[1] // 2, real, imag).astype(jnp.bfloat16)
-    o_ref[0] = jnp.dot(vt_ref[...], phase, preferred_element_type=jnp.float32).astype(o_ref.dtype)
+def phase_sum_kernel(c_ref, q_ref, vt_ref, o_ref, phase_ref):
+    groups, _, group_width = o_ref.shape
+
+    @pl.when(pl.program_id(0) == 0)
+    def _():
+        cos_k, sin_k = quarter_tables()
+        dots = jnp.dot(c_ref[...], q_ref[...], preferred_element_type=jnp.float32)
+        m = dots.astype(jnp.int32) & (L - 1)
+        bit0 = (m & 1) != 0
+        bit1 = (m & 2) != 0
+        bit2 = (m & 4) != 0
+        bit3 = (m & 8) != 0
+        real = jnp.where(bit1, jnp.where(bit0, cos_k[3], cos_k[2]), jnp.where(bit0, cos_k[1], cos_k[0]))
+        imag = jnp.where(bit1, jnp.where(bit0, sin_k[3], sin_k[2]), jnp.where(bit0, sin_k[1], sin_k[0]))
+        real, imag = jnp.where(bit2, imag, real), jnp.where(bit2, -real, imag)
+        real, imag = jnp.where(bit3, -real, real), jnp.where(bit3, -imag, imag)
+        column = lax.broadcasted_iota(jnp.int32, m.shape, 1) % group_width
+        phase_ref[...] = jnp.where(column < group_width // 2, real, imag).astype(jnp.bfloat16)
+
+    sums = jnp.dot(vt_ref[...], phase_ref[...], preferred_element_type=jnp.float32)
+    for g in range(groups):
+        o_ref[g] = sums[:, g * group_width:(g + 1) * group_width].astype(o_ref.dtype)
 
 
 def phase_sums(q_columns, cell_coords, velocity_t):
     groups, _, rows = q_columns.shape
     width, cells = velocity_t.shape
     pad = 8
+    block = 256
     c_in = jnp.pad(cell_coords, ((0, 0), (0, pad - 3))).astype(jnp.bfloat16)
-    q_in = jnp.pad(jnp.concatenate([q_columns, q_columns], axis=2), ((0, 0), (0, pad - 3), (0, 0)))
-    q_in = q_in.astype(jnp.bfloat16)
+    q_in = jnp.concatenate([q_columns, q_columns], axis=2).transpose(1, 0, 2).reshape(3, groups * 2 * rows)
+    q_in = jnp.pad(q_in, ((0, pad - 3), (0, 0))).astype(jnp.bfloat16)
     return pl.pallas_call(
         phase_sum_kernel,
-        grid=(groups,),
+        grid=(width // block,),
         in_specs=[
             pl.BlockSpec((cells, pad), lambda i: (0, 0)),
-            pl.BlockSpec((1, pad, 2 * rows), lambda i: (i, 0, 0)),
-            pl.BlockSpec((width, cells), lambda i: (0, 0)),
+            pl.BlockSpec((pad, groups * 2 * rows), lambda i: (0, 0)),
+            pl.BlockSpec((block, cells), lambda i: (i, 0)),
         ],
-        out_specs=pl.BlockSpec((1, width, 2 * rows), lambda i: (i, 0, 0)),
+        out_specs=pl.BlockSpec((groups, block, 2 * rows), lambda i: (0, i, 0)),
         out_shape=jax.ShapeDtypeStruct((groups, width, 2 * rows), jnp.bfloat16),
+        scratch_shapes=[pltpu.VMEM((cells, groups * 2 * rows), jnp.bfloat16)],
         cost_estimate=pl.CostEstimate(
             flops=4 * groups * rows * cells * width,
             transcendentals=0,

time: 92.5 us -> 91.3 us (0.987)
  Pallas kernels: 9.15 us -> 7.93 us
    pallas_call x1, Pallas kernels: 9.15 us -> 7.93 us  [phase_sums(): pl.pallas_call(phase_sum_kernel, grid=(width // block,), in_specs=[pl.Blo...]
where the time goes in v11:
time: 91.3 us; the launch traced here: 90.9 us
  waiting for transfers between devices  53.7 us (59%)
  starting transfers between devices  18.2 us (20%)
  Pallas kernels  7.93 us (9%)
  other arithmetic  4.62 us (5%)
  local copies, waits for them, and re-layouts  4.12 us (5%)
  matrix products  2.23 us (2%)
    all_to_all x1, waiting for transfers between devices, local(): lax.all_to_all(partial_term, 'cell', split_axis=0, concat_axis=0, tiled=T...  38.1 us
    all_to_all x1, waiting for transfers between devices, local(): lax.all_to_all(blocks, 'tm', split_axis=0, concat_axis=0, tiled=True)  15.6 us
    all_to_all x1, starting transfers between devices, local(): lax.all_to_all(blocks, 'tm', split_axis=0, concat_axis=0, tiled=True)  10.6 us
    pallas_call x1, Pallas kernels, phase_sums(): pl.pallas_call(phase_sum_kernel, grid=(width // block,), in_specs=[pl.Blo...  7.93 us
    all_to_all x1, starting transfers between devices, local(): lax.all_to_all(partial_term, 'cell', split_axis=0, concat_axis=0, tiled=T...  7.61 us
  transfers between devices with their start and end apart: 2, of which 2 were waited for; matrix products, arithmetic and copies ran while one was open for 2% of the time, Pallas kernels for 0%

profile of v11, /device:TPU:1, one launch (start us, length us, event | category | flops | bytes accessed | tf_op | source)
XLA Modules:
  0.0 90.9 jit_solution(14486218005111461729)
XLA Ops:
  0.0 0.7 convert.13
  0.7 0.2 copy.30
  0.9 0.7 convert.17
  1.6 0.4 reshape.116
  2.0 0.6 copy.31
  2.6 0.1 copy.32
  2.7 0.1 maximum_bitcast_fusion.6
  2.8 0.7 pad.10.c_ref
  3.5 0.6 pad.11.q_ref
  4.1 7.9 %shard_map.46 = bf16[8,1536,128]{2,1,0:T(8,128)(2,1)} custom-call(bf16[512,8]{1,0:T(8,128)(2,1)} %pad.10.c_ref, bf16[8,1024]{1,0:T(8,128)(2,1)} %pad.11.q_ref, bf16[1536,512]{1,0:T(8,128)(2,1)} %bitcast.60), custom_call_target="tpu_custom_call" | custom-call | flops 1610612736 | bytes 4718592 | tf_op jit(solution)/shard_map/pallas_call | solution.py:53
  12.0 0.0 copy-start
  12.0 7.6 %all-to-all-start = ((bf16[8,1536,128]{2,1,0:T(8,128)(2,1)}), bf16[8,1536,128]{2,1,0:T(8,128)(2,1)S(1)}, u32[]{:S(2)}, u32[]{:S(2)}) async-start(bf16[8,1536,128]{2,1,0:T(8,128)(2,1)} %shard_map.46), calls=%async_computation | async-start | bytes 6291456 | tf_op jit(solution)/shard_map/all_to_all | solution.py:98
  19.7 0.0 copy-done
  19.7 0.6 fusion.31
  20.3 38.1 %all-to-all-done = bf16[8,1536,128]{2,1,0:T(8,128)(2,1)S(1)} async-done(((bf16[8,1536,128]{2,1,0:T(8,128)(2,1)}), bf16[8,1536,128]{2,1,0:T(8,128)(2,1)S(1)}, u32[]{:S(2)}, u32[]{:S(2)}) %all-to-all-start) | async-done | bytes 3145760 | tf_op jit(solution)/shard_map/all_to_all | solution.py:98
  58.4 0.7 reduce_sum.12
  59.1 0.0 copy-start.1
  59.1 0.0 copy-start.2
  59.1 0.2 copy.34
  59.3 0.5 reshape.113
  59.8 0.9 copy.35
  60.6 10.6 %all-to-all-start.1 = ((bf16[32,2,2,16,96]{4,3,1,2,0:T(8,128)(2,1)}), bf16[32,2,2,16,96]{4,3,1,2,0:T(8,128)(2,1)S(1)}, u32[]{:S(2)}, u32[]{:S(2)}) async-start(bf16[32,2,2,16,96]{4,3,1,2,0:T(8,128)(2,1)} %copy.35), calls=%async_computation.1 | async-start | bytes 1048576 | tf_op jit(solution)/shard_map/all_to_all | solution.py:101
  71.2 0.1 fusion.27
  71.3 0.3 fusion.24
  71.6 0.0 copy-done.1
  71.7 0.0 copy-done.2
  71.7 0.2 maximum_bitcast_fusion.4
  71.8 0.3 multiply_subtract_fusion
  72.2 15.6 %all-to-all-done.1 = bf16[32,2,2,16,96]{4,3,1,2,0:T(8,128)(2,1)S(1)} async-done(((bf16[32,2,2,16,96]{4,3,1,2,0:T(8,128)(2,1)}), bf16[32,2,2,16,96]{4,3,1,2,0:T(8,128)(2,1)S(1)}, u32[]{:S(2)}, u32[]{:S(2)}) %all-to-all-start.1) | async-done | bytes 393248 | tf_op jit(solution)/shard_map/all_to_all | solution.py:101
  87.8 0.7 fusion.3
  88.4 1.6 %fusion = f32[2,192,1024]{2,1,0:T(8,128)S(1)} fusion(f32[2,512,192]{2,1,0:T(8,128)S(1)} %bitcast.55, f32[512,512]{1,0:T(8,128)S(1)} %bitcast.54, f32[512,512]{1,0:T(8,128)S(1)} %bitcast.53), kind=kOutput, calls=%fused_computation.1 | convolution fusion | flops 1208483840 | bytes 4456448 | tf_op jit(solution)/shard_map/jts,tw->jsw/dot_general | solution.py:117
  90.0 0.9 fusion.7
  (2 shorter events, 0.0 us)
Async XLA Ops:
  12.0 7.6 %copy-start = (f32[2,2,96,96]{3,2,1,0:T(8,128)S(1)}, f32[2,2,96,96]{3,2,1,0:T(8,128)}, u32[]{:S(2)}) copy-start(f32[2,2,96,96]{3,2,1,0:T(8,128)} %param.7) | copy-start | bytes 442372
  12.0 46.4 %all-to-all-start = ((bf16[8,1536,128]{2,1,0:T(8,128)(2,1)}), bf16[8,1536,128]{2,1,0:T(8,128)(2,1)S(1)}, u32[]{:S(2)}, u32[]{:S(2)}) async-start(bf16[8,1536,128]{2,1,0:T(8,128)(2,1)} %shard_map.46), calls=%async_computation | async-start | bytes 6291456 | tf_op jit(solution)/shard_map/all_to_all | solution.py:98
  59.1 12.5 %copy-start.1 = (f32[2,2,96,96]{3,2,1,0:T(8,128)S(1)}, f32[2,2,96,96]{3,2,1,0:T(8,128)}, u32[]{:S(2)}) copy-start(f32[2,2,96,96]{3,2,1,0:T(8,128)} %param.7) | copy-start | bytes 442372
  59.1 12.6 %copy-start.2 = (f32[2,96,96]{2,1,0:T(8,128)S(1)}, f32[2,96,96]{2,1,0:T(8,128)}, u32[]{:S(2)}) copy-start(f32[2,96,96]{2,1,0:T(8,128)} %fusion.31) | copy-start | bytes 221188
  60.6 27.1 %all-to-all-start.1 = ((bf16[32,2,2,16,96]{4,3,1,2,0:T(8,128)(2,1)}), bf16[32,2,2,16,96]{4,3,1,2,0:T(8,128)(2,1)S(1)}, u32[]{:S(2)}, u32[]{:S(2)}) async-start(bf16[32,2,2,16,96]{4,3,1,2,0:T(8,128)(2,1)} %copy.35), calls=%async_computation.1 | async-start | bytes 1048576 | tf_op jit(solution)/shard_map/all_to_all | solution.py:101

commit v12 on v10

--- a/solution.py
+++ b/solution.py
@@ -4,6 +4,7 @@
 import jax.numpy as jnp
 from jax import lax
 from jax.experimental import pallas as pl
+from jax.experimental.pallas import tpu as pltpu
 from jax.sharding import PartitionSpec as P
 import numpy as np
 
@@ -17,9 +18,9 @@
     return [float(v) for v in cos_k], [float(v) for v in sin_k]
 
 
-def phase_sum_kernel(c_ref, q_ref, vt_ref, o_ref):
+def phase_block(c_ref, q_ref, block, group_width):
     cos_k, sin_k = quarter_tables()
-    dots = jnp.dot(c_ref[...], q_ref[0], preferred_element_type=jnp.float32)
+    dots = jnp.dot(c_ref[...], q_ref[block], preferred_element_type=jnp.float32)
     m = dots.astype(jnp.int32) & (L - 1)
     bit0 = (m & 1) != 0
     bit1 = (m & 2) != 0
@@ -29,28 +30,50 @@
     imag = jnp.where(bit1, jnp.where(bit0, sin_k[3], sin_k[2]), jnp.where(bit0, sin_k[1], sin_k[0]))
     real, imag = jnp.where(bit2, imag, real), jnp.where(bit2, -real, imag)
     real, imag = jnp.where(bit3, -real, real), jnp.where(bit3, -imag, imag)
-    column = lax.broadcasted_iota(jnp.int32, m.shape, 1)
-    phase = jnp.where(column < m.shape[1] // 2, real, imag).astype(jnp.bfloat16)
-    o_ref[0] = jnp.dot(vt_ref[...], phase, preferred_element_type=jnp.float32).astype(o_ref.dtype)
+    column = lax.broadcasted_iota(jnp.int32, m.shape, 1) % group_width
+    return jnp.where(column < group_width // 2, real, imag).astype(jnp.bfloat16)
+
+
+def phase_sum_kernel(c_ref, q_ref, vt_ref, o_ref, phase_ref):
+    per_step, _, group_width = o_ref.shape
+    step = pl.program_id(0)
+    steps = pl.num_programs(0)
+    slot = step % 2
+
+    @pl.when(step == 0)
+    def _():
+        phase_ref[0] = phase_block(c_ref, q_ref, 0, group_width)
+
+    @pl.when(step + 1 < steps)
+    def _():
+        phase_ref[1 - slot] = phase_block(c_ref, q_ref, step + 1, group_width)
+
+    sums = jnp.dot(vt_ref[...], phase_ref[slot], preferred_element_type=jnp.float32)
+    for g in range(per_step):
+        o_ref[g] = sums[:, g * group_width:(g + 1) * group_width].astype(o_ref.dtype)
 
 
 def phase_sums(q_columns, cell_coords, velocity_t):
     groups, _, rows = q_columns.shape
     width, cells = velocity_t.shape
     pad = 8
+    per_step = 2
+    steps = groups // per_step
+    block_width = per_step * 2 * rows
     c_in = jnp.pad(cell_coords, ((0, 0), (0, pad - 3))).astype(jnp.bfloat16)
-    q_in = jnp.pad(jnp.concatenate([q_columns, q_columns], axis=2), ((0, 0), (0, pad - 3), (0, 0)))
-    q_in = q_in.astype(jnp.bfloat16)
+    q_in = jnp.concatenate([q_columns, q_columns], axis=2).transpose(1, 0, 2).reshape(3, steps, block_width)
+    q_in = jnp.pad(q_in, ((0, pad - 3), (0, 0), (0, 0))).transpose(1, 0, 2).astype(jnp.bfloat16)
     return pl.pallas_call(
         phase_sum_kernel,
-        grid=(groups,),
+        grid=(steps,),
         in_specs=[
             pl.BlockSpec((cells, pad), lambda i: (0, 0)),
-            pl.BlockSpec((1, pad, 2 * rows), lambda i: (i, 0, 0)),
+            pl.BlockSpec((steps, pad, block_width), lambda i: (0, 0, 0)),
             pl.BlockSpec((width, cells), lambda i: (0, 0)),
         ],
-        out_specs=pl.BlockSpec((1, width, 2 * rows), lambda i: (i, 0, 0)),
+        out_specs=pl.BlockSpec((per_step, width, 2 * rows), lambda i: (i, 0, 0)),
         out_shape=jax.ShapeDtypeStruct((groups, width, 2 * rows), jnp.bfloat16),
+        scratch_shapes=[pltpu.VMEM((2, cells, block_width), jnp.bfloat16)],
         cost_estimate=pl.CostEstimate(
             flops=4 * groups * rows * cells * width,
             transcendentals=0,

time: 92.5 us -> 90.3 us (0.976)
  Pallas kernels: 9.15 us -> 6.97 us
    pallas_call x1, Pallas kernels: 9.15 us -> 6.97 us  [phase_sums(): pl.pallas_call(phase_sum_kernel, grid=(steps,), in_specs=[pl.BlockSpec((c...]
where the time goes in v12:
time: 90.3 us; the launch traced here: 90 us
  waiting for transfers between devices  53.7 us (59%)
  starting transfers between devices  18.2 us (20%)
  Pallas kernels  6.97 us (8%)
  other arithmetic  4.62 us (5%)
  local copies, waits for them, and re-layouts  4.12 us (5%)
  matrix products  2.23 us (2%)
    all_to_all x1, waiting for transfers between devices, local(): lax.all_to_all(partial_term, 'cell', split_axis=0, concat_axis=0, tiled=T...  38.1 us
    all_to_all x1, waiting for transfers between devices, local(): lax.all_to_all(blocks, 'tm', split_axis=0, concat_axis=0, tiled=True)  15.6 us
    all_to_all x1, starting transfers between devices, local(): lax.all_to_all(blocks, 'tm', split_axis=0, concat_axis=0, tiled=True)  10.6 us
    all_to_all x1, starting transfers between devices, local(): lax.all_to_all(partial_term, 'cell', split_axis=0, concat_axis=0, tiled=T...  7.61 us
    pallas_call x1, Pallas kernels, phase_sums(): pl.pallas_call(phase_sum_kernel, grid=(steps,), in_specs=[pl.BlockSpec((c...  6.97 us
  transfers between devices with their start and end apart: 2, of which 2 were waited for; matrix products, arithmetic and copies ran while one was open for 2% of the time, Pallas kernels for 0%

profile of v12, /device:TPU:1, one launch (start us, length us, event | category | flops | bytes accessed | tf_op | source)
XLA Modules:
  0.0 90.0 jit_solution(14135183750121157272)
XLA Ops:
  0.0 0.7 convert.13
  0.7 0.2 copy.38
  0.9 0.7 convert.17
  1.6 0.4 reshape.116
  2.0 0.6 copy.39
  2.6 0.1 copy.40
  2.7 0.1 maximum_bitcast_fusion.6
  2.8 0.6 pad_bitcast_fusion.q_ref
  3.4 0.7 pad.10.c_ref
  4.1 7.0 %shard_map.46 = bf16[8,1536,128]{2,1,0:T(8,128)(2,1)} custom-call(bf16[512,8]{1,0:T(8,128)(2,1)} %pad.10.c_ref, bf16[4,8,256]{2,1,0:T(8,128)(2,1)} %pad_bitcast_fusion.q_ref, bf16[1536,512]{1,0:T(8,128)(2,1)} %bitcast.57), custom_call_target="tpu_custom_call" | custom-call | flops 1610612736 | bytes 4718592 | tf_op jit(solution)/shard_map/pallas_call | solution.py:66
  11.1 0.0 copy-start
  11.1 7.6 %all-to-all-start = ((bf16[8,1536,128]{2,1,0:T(8,128)(2,1)}), bf16[8,1536,128]{2,1,0:T(8,128)(2,1)S(1)}, u32[]{:S(2)}, u32[]{:S(2)}) async-start(bf16[8,1536,128]{2,1,0:T(8,128)(2,1)} %shard_map.46), calls=%async_computation | async-start | bytes 6291456 | tf_op jit(solution)/shard_map/all_to_all | solution.py:111
  18.7 0.0 copy-done
  18.7 0.6 fusion.31
  19.4 38.1 %all-to-all-done = bf16[8,1536,128]{2,1,0:T(8,128)(2,1)S(1)} async-done(((bf16[8,1536,128]{2,1,0:T(8,128)(2,1)}), bf16[8,1536,128]{2,1,0:T(8,128)(2,1)S(1)}, u32[]{:S(2)}, u32[]{:S(2)}) %all-to-all-start) | async-done | bytes 3145760 | tf_op jit(solution)/shard_map/all_to_all | solution.py:111
  57.5 0.7 reduce_sum.12
  58.1 0.0 copy-start.1
  58.2 0.0 copy-start.2
  58.2 0.2 copy.43
  58.4 0.5 reshape.113
  58.8 0.9 copy.44
  59.7 10.6 %all-to-all-start.1 = ((bf16[32,2,2,16,96]{4,3,1,2,0:T(8,128)(2,1)}), bf16[32,2,2,16,96]{4,3,1,2,0:T(8,128)(2,1)S(1)}, u32[]{:S(2)}, u32[]{:S(2)}) async-start(bf16[32,2,2,16,96]{4,3,1,2,0:T(8,128)(2,1)} %copy.44), calls=%async_computation.1 | async-start | bytes 1048576 | tf_op jit(solution)/shard_map/all_to_all | solution.py:114
  70.2 0.1 fusion.27
  70.4 0.3 fusion.24
  70.7 0.0 copy-done.1
  70.7 0.0 copy-done.2
  70.7 0.2 maximum_bitcast_fusion.4
  70.9 0.3 multiply_subtract_fusion
  71.2 15.6 %all-to-all-done.1 = bf16[32,2,2,16,96]{4,3,1,2,0:T(8,128)(2,1)S(1)} async-done(((bf16[32,2,2,16,96]{4,3,1,2,0:T(8,128)(2,1)}), bf16[32,2,2,16,96]{4,3,1,2,0:T(8,128)(2,1)S(1)}, u32[]{:S(2)}, u32[]{:S(2)}) %all-to-all-start.1) | async-done | bytes 393248 | tf_op jit(solution)/shard_map/all_to_all | solution.py:114
  86.8 0.6 fusion.3
  87.5 1.6 %fusion = f32[2,192,1024]{2,1,0:T(8,128)S(1)} fusion(f32[2,512,192]{2,1,0:T(8,128)S(1)} %bitcast.53, f32[512,512]{1,0:T(8,128)S(1)} %bitcast.52, f32[512,512]{1,0:T(8,128)S(1)} %bitcast.51), kind=kOutput, calls=%fused_computation.1 | convolution fusion | flops 1208483840 | bytes 4456448 | tf_op jit(solution)/shard_map/jts,tw->jsw/dot_general | solution.py:130
  89.1 0.9 %fusion.7 = f32[2,96,512]{2,1,0:T(8,128)} fusion(f32[2,192,1024]{2,1,0:T(8,128)S(1)} %fusion), kind=kLoop, calls=%fused_computation.11 | loop fusion | flops 589824 | bytes 1966080 | tf_op jit(solution)/shard_map/div | solution.py:135
  (3 shorter events, 0.0 us)
Async XLA Ops:
  11.1 7.6 %copy-start = (f32[2,2,96,96]{3,2,1,0:T(8,128)S(1)}, f32[2,2,96,96]{3,2,1,0:T(8,128)}, u32[]{:S(2)}) copy-start(f32[2,2,96,96]{3,2,1,0:T(8,128)} %param.7) | copy-start | bytes 442372
  11.1 46.4 %all-to-all-start = ((bf16[8,1536,128]{2,1,0:T(8,128)(2,1)}), bf16[8,1536,128]{2,1,0:T(8,128)(2,1)S(1)}, u32[]{:S(2)}, u32[]{:S(2)}) async-start(bf16[8,1536,128]{2,1,0:T(8,128)(2,1)} %shard_map.46), calls=%async_computation | async-start | bytes 6291456 | tf_op jit(solution)/shard_map/all_to_all | solution.py:111
  58.1 12.5 %copy-start.1 = (f32[2,2,96,96]{3,2,1,0:T(8,128)S(1)}, f32[2,2,96,96]{3,2,1,0:T(8,128)}, u32[]{:S(2)}) copy-start(f32[2,2,96,96]{3,2,1,0:T(8,128)} %param.7) | copy-start | bytes 442372
  58.2 12.6 %copy-start.2 = (f32[2,96,96]{2,1,0:T(8,128)S(1)}, f32[2,96,96]{2,1,0:T(8,128)}, u32[]{:S(2)}) copy-start(f32[2,96,96]{2,1,0:T(8,128)} %fusion.31) | copy-start | bytes 221188
  59.7 27.1 %all-to-all-start.1 = ((bf16[32,2,2,16,96]{4,3,1,2,0:T(8,128)(2,1)}), bf16[32,2,2,16,96]{4,3,1,2,0:T(8,128)(2,1)S(1)}, u32[]{:S(2)}, u32[]{:S(2)}) async-start(bf16[32,2,2,16,96]{4,3,1,2,0:T(8,128)(2,1)} %copy.44), calls=%async_computation.1 | async-start | bytes 1048576 | tf_op jit(solution)/shard_map/all_to_all | solution.py:114

commit v13 on v12

--- a/solution.py
+++ b/solution.py
@@ -20,7 +20,9 @@
 
 def phase_block(c_ref, q_ref, block, group_width):
     cos_k, sin_k = quarter_tables()
-    dots = jnp.dot(c_ref[...], q_ref[block], preferred_element_type=jnp.float32)
+    cells = c_ref[...].astype(jnp.float32).astype(jnp.bfloat16)
+    points = q_ref[block].astype(jnp.float32).astype(jnp.bfloat16)
+    dots = jnp.dot(cells, points, preferred_element_type=jnp.float32)
     m = dots.astype(jnp.int32) & (L - 1)
     bit0 = (m & 1) != 0
     bit1 = (m & 2) != 0
@@ -60,9 +62,9 @@
     per_step = 2
     steps = groups // per_step
     block_width = per_step * 2 * rows
-    c_in = jnp.pad(cell_coords, ((0, 0), (0, pad - 3))).astype(jnp.bfloat16)
+    c_in = jnp.pad(cell_coords, ((0, 0), (0, pad - 3)))
     q_in = jnp.concatenate([q_columns, q_columns], axis=2).transpose(1, 0, 2).reshape(3, steps, block_width)
-    q_in = jnp.pad(q_in, ((0, pad - 3), (0, 0), (0, 0))).transpose(1, 0, 2).astype(jnp.bfloat16)
+    q_in = jnp.pad(q_in, ((0, pad - 3), (0, 0), (0, 0))).transpose(1, 0, 2)
     return pl.pallas_call(
         phase_sum_kernel,
         grid=(steps,),

time: 90.3 us -> 90.3 us (level)
  other arithmetic: 4.62 us -> 3.21 us
  local copies, waits for them, and re-layouts: 4.12 us -> 5.46 us
    another operation x2 -> x0, other arithmetic: 1.41 us -> none
    another operation x4 -> x0, local copies, waits for them, and re-layouts: 1.3 us -> none
    transpose x0 -> x2, local copies, waits for them, and re-layouts: none -> 1.25 us  [the longest x1 0.64 us: local(): q_columns = q_coords.reshape(n_tm, n_cell, q_local, 3).transpose(1, 3, 0, 2)]
    reshape x0 -> x2, local copies, waits for them, and re-layouts: none -> 1.11 us  [the longest x1 1.04 us: local(): q_columns = q_coords.reshape(n_tm, n_cell, q_local, 3).transpose(1, 3, 0, 2)]
where the time goes in v13:
time: 90.3 us; the launch traced here: 89.9 us
  waiting for transfers between devices  53.7 us (59%)
  starting transfers between devices  18.2 us (20%)
  Pallas kernels  6.99 us (8%)
  local copies, waits for them, and re-layouts  5.46 us (6%)
  other arithmetic  3.21 us (4%)
  matrix products  2.23 us (2%)
    all_to_all x1, waiting for transfers between devices, local(): lax.all_to_all(partial_term, 'cell', split_axis=0, concat_axis=0, tiled=T...  38.1 us
    all_to_all x1, waiting for transfers between devices, local(): lax.all_to_all(blocks, 'tm', split_axis=0, concat_axis=0, tiled=True)  15.6 us
    all_to_all x1, starting transfers between devices, local(): lax.all_to_all(blocks, 'tm', split_axis=0, concat_axis=0, tiled=True)  10.6 us
    all_to_all x1, starting transfers between devices, local(): lax.all_to_all(partial_term, 'cell', split_axis=0, concat_axis=0, tiled=T...  7.61 us
    pallas_call x1, Pallas kernels, phase_sums(): pl.pallas_call(phase_sum_kernel, grid=(steps,), in_specs=[pl.BlockSpec((c...  6.99 us
  transfers between devices with their start and end apart: 2, of which 2 were waited for; matrix products, arithmetic and copies ran while one was open for 2% of the time, Pallas kernels for 0%

profile of v13, /device:TPU:1, one launch (start us, length us, event | category | flops | bytes accessed | tf_op | source)
XLA Modules:
  0.0 89.9 jit_solution(2380509080673384011)
XLA Ops:
  0.0 0.8 copy.26
  0.8 1.0 %reshape.108 = s32[32,8,2,3]{2,1,0,3:T(8,128)S(1)} reshape(s32[512,3]{0,1:T(4,128)} %param.6) | data formatting | bytes 12288 | tf_op jit(solution)/shard_map/reshape | solution.py:109
  1.9 0.6 copy.27
  2.5 0.1 copy.28
  2.6 0.1 add_bitcast_fusion
  2.7 0.6 pad_bitcast_fusion.q_ref
  3.3 0.7 pad.8.c_ref
  4.1 7.0 %shard_map.46 = bf16[8,1536,128]{2,1,0:T(8,128)(2,1)} custom-call(s32[512,8]{1,0:T(8,128)} %pad.8.c_ref, s32[4,8,256]{2,1,0:T(8,128)} %pad_bitcast_fusion.q_ref, bf16[1536,512]{1,0:T(8,128)(2,1)} %bitcast.57), custom_call_target="tpu_custom_call" | custom-call | flops 1610612736 | bytes 4718592 | tf_op jit(solution)/shard_map/pallas_call | solution.py:68
  11.1 0.0 copy-start
  11.1 7.6 %all-to-all-start = ((bf16[8,1536,128]{2,1,0:T(8,128)(2,1)}), bf16[8,1536,128]{2,1,0:T(8,128)(2,1)S(1)}, u32[]{:S(2)}, u32[]{:S(2)}) async-start(bf16[8,1536,128]{2,1,0:T(8,128)(2,1)} %shard_map.46), calls=%async_computation | async-start | bytes 6291456 | tf_op jit(solution)/shard_map/all_to_all | solution.py:113
  18.7 0.0 copy-done
  18.7 0.6 fusion.31
  19.3 38.1 %all-to-all-done = bf16[8,1536,128]{2,1,0:T(8,128)(2,1)S(1)} async-done(((bf16[8,1536,128]{2,1,0:T(8,128)(2,1)}), bf16[8,1536,128]{2,1,0:T(8,128)(2,1)S(1)}, u32[]{:S(2)}, u32[]{:S(2)}) %all-to-all-start) | async-done | bytes 3145760 | tf_op jit(solution)/shard_map/all_to_all | solution.py:113
  57.4 0.7 reduce_sum.12
  58.1 0.0 copy-start.1
  58.1 0.0 copy-start.2
  58.1 0.2 copy.31
  58.3 0.5 reshape.112
  58.8 0.9 copy.32
  59.6 10.6 %all-to-all-start.1 = ((bf16[32,2,2,16,96]{4,3,1,2,0:T(8,128)(2,1)}), bf16[32,2,2,16,96]{4,3,1,2,0:T(8,128)(2,1)S(1)}, u32[]{:S(2)}, u32[]{:S(2)}) async-start(bf16[32,2,2,16,96]{4,3,1,2,0:T(8,128)(2,1)} %copy.32), calls=%async_computation.1 | async-start | bytes 1048576 | tf_op jit(solution)/shard_map/all_to_all | solution.py:116
  70.2 0.1 fusion.27
  70.3 0.3 fusion.24
  70.6 0.0 copy-done.1
  70.7 0.0 copy-done.2
  70.7 0.2 maximum_bitcast_fusion.4
  70.8 0.3 multiply_subtract_fusion
  71.2 15.6 %all-to-all-done.1 = bf16[32,2,2,16,96]{4,3,1,2,0:T(8,128)(2,1)S(1)} async-done(((bf16[32,2,2,16,96]{4,3,1,2,0:T(8,128)(2,1)}), bf16[32,2,2,16,96]{4,3,1,2,0:T(8,128)(2,1)S(1)}, u32[]{:S(2)}, u32[]{:S(2)}) %all-to-all-start.1) | async-done | bytes 393248 | tf_op jit(solution)/shard_map/all_to_all | solution.py:116
  86.8 0.7 fusion.3
  87.4 1.6 %fusion = f32[2,192,1024]{2,1,0:T(8,128)S(1)} fusion(f32[2,512,192]{2,1,0:T(8,128)S(1)} %bitcast.53, f32[512,512]{1,0:T(8,128)S(1)} %bitcast.52, f32[512,512]{1,0:T(8,128)S(1)} %bitcast.51), kind=kOutput, calls=%fused_computation.1 | convolution fusion | flops 1208483840 | bytes 4456448 | tf_op jit(solution)/shard_map/jts,tw->jsw/dot_general | solution.py:132
  89.0 0.9 %fusion.7 = f32[2,96,512]{2,1,0:T(8,128)} fusion(f32[2,192,1024]{2,1,0:T(8,128)S(1)} %fusion), kind=kLoop, calls=%fused_computation.11 | loop fusion | flops 589824 | bytes 1966080 | tf_op jit(solution)/shard_map/div | solution.py:137
  (3 shorter events, 0.0 us)
Async XLA Ops:
  11.1 7.6 %copy-start = (f32[2,2,96,96]{3,2,1,0:T(8,128)S(1)}, f32[2,2,96,96]{3,2,1,0:T(8,128)}, u32[]{:S(2)}) copy-start(f32[2,2,96,96]{3,2,1,0:T(8,128)} %param.7) | copy-start | bytes 442372
  11.1 46.4 %all-to-all-start = ((bf16[8,1536,128]{2,1,0:T(8,128)(2,1)}), bf16[8,1536,128]{2,1,0:T(8,128)(2,1)S(1)}, u32[]{:S(2)}, u32[]{:S(2)}) async-start(bf16[8,1536,128]{2,1,0:T(8,128)(2,1)} %shard_map.46), calls=%async_computation | async-start | bytes 6291456 | tf_op jit(solution)/shard_map/all_to_all | solution.py:113
  58.1 12.5 %copy-start.1 = (f32[2,2,96,96]{3,2,1,0:T(8,128)S(1)}, f32[2,2,96,96]{3,2,1,0:T(8,128)}, u32[]{:S(2)}) copy-start(f32[2,2,96,96]{3,2,1,0:T(8,128)} %param.7) | copy-start | bytes 442372
  58.1 12.6 %copy-start.2 = (f32[2,96,96]{2,1,0:T(8,128)S(1)}, f32[2,96,96]{2,1,0:T(8,128)}, u32[]{:S(2)}) copy-start(f32[2,96,96]{2,1,0:T(8,128)} %fusion.31) | copy-start | bytes 221188
  59.6 27.1 %all-to-all-start.1 = ((bf16[32,2,2,16,96]{4,3,1,2,0:T(8,128)(2,1)}), bf16[32,2,2,16,96]{4,3,1,2,0:T(8,128)(2,1)S(1)}, u32[]{:S(2)}, u32[]{:S(2)}) async-start(bf16[32,2,2,16,96]{4,3,1,2,0:T(8,128)(2,1)} %copy.32), calls=%async_computation.1 | async-start | bytes 1048576 | tf_op jit(solution)/shard_map/all_to_all | solution.py:116

commit v14 on v13

--- a/solution.py
+++ b/solution.py
@@ -129,7 +129,10 @@
     )
     cosines, sines = twiddles(frames)
     basis = jnp.concatenate([cosines, sines], axis=1)
-    projected = jnp.einsum("jts,tw->jsw", amplitude, basis, precision=lax.Precision.HIGH)
+    projected = jnp.einsum(
+        "jts,tw->jsw", amplitude.astype(jnp.bfloat16), basis.astype(jnp.bfloat16),
+        preferred_element_type=jnp.float32,
+    )
     on_cos = projected[:, :, :frames]
     on_sin = projected[:, :, frames:]
     out_real = on_cos[:, :branches] + on_sin[:, branches:]

time: 90.3 us -> 89.3 us (0.989)
  matrix products: 2.23 us -> 1.24 us
    dot_general x1, matrix products: 1.58 us -> 0.59 us  [local(): jnp.einsum('jts,tw->jsw', amplitude.astype(jnp.bfloat16), basis.astype(jn...]
where the time goes in v14:
time: 89.3 us; the launch traced here: 88.9 us
  waiting for transfers between devices  53.7 us (60%)
  starting transfers between devices  18.2 us (20%)
  Pallas kernels  6.99 us (8%)
  local copies, waits for them, and re-layouts  5.46 us (6%)
  other arithmetic  3.27 us (4%)
  matrix products  1.24 us (1%)
    all_to_all x1, waiting for transfers between devices, local(): lax.all_to_all(partial_term, 'cell', split_axis=0, concat_axis=0, tiled=T...  38.1 us
    all_to_all x1, waiting for transfers between devices, local(): lax.all_to_all(blocks, 'tm', split_axis=0, concat_axis=0, tiled=True)  15.5 us
    all_to_all x1, starting transfers between devices, local(): lax.all_to_all(blocks, 'tm', split_axis=0, concat_axis=0, tiled=True)  10.6 us
    all_to_all x1, starting transfers between devices, local(): lax.all_to_all(partial_term, 'cell', split_axis=0, concat_axis=0, tiled=T...  7.61 us
    pallas_call x1, Pallas kernels, phase_sums(): pl.pallas_call(phase_sum_kernel, grid=(steps,), in_specs=[pl.BlockSpec((c...  6.99 us
  transfers between devices with their start and end apart: 2, of which 2 were waited for; matrix products, arithmetic and copies ran while one was open for 2% of the time, Pallas kernels for 0%

profile of v14, /device:TPU:1, one launch (start us, length us, event | category | flops | bytes accessed | tf_op | source)
XLA Modules:
  0.0 88.9 jit_solution(17599653190421781531)
XLA Ops:
  0.0 0.8 copy.26
  0.8 1.0 %reshape.109 = s32[32,8,2,3]{2,1,0,3:T(8,128)S(1)} reshape(s32[512,3]{0,1:T(4,128)} %param.6) | data formatting | bytes 12288 | tf_op jit(solution)/shard_map/reshape | solution.py:109
  1.9 0.6 copy.27
  2.5 0.1 copy.28
  2.6 0.1 add_bitcast_fusion
  2.7 0.6 pad_bitcast_fusion.q_ref
  3.3 0.7 pad.8.c_ref
  4.1 7.0 %shard_map.46 = bf16[8,1536,128]{2,1,0:T(8,128)(2,1)} custom-call(s32[512,8]{1,0:T(8,128)} %pad.8.c_ref, s32[4,8,256]{2,1,0:T(8,128)} %pad_bitcast_fusion.q_ref, bf16[1536,512]{1,0:T(8,128)(2,1)} %bitcast.59), custom_call_target="tpu_custom_call" | custom-call | flops 1610612736 | bytes 4718592 | tf_op jit(solution)/shard_map/pallas_call | solution.py:68
  11.1 0.0 copy-start
  11.1 7.6 %all-to-all-start = ((bf16[8,1536,128]{2,1,0:T(8,128)(2,1)}), bf16[8,1536,128]{2,1,0:T(8,128)(2,1)S(1)}, u32[]{:S(2)}, u32[]{:S(2)}) async-start(bf16[8,1536,128]{2,1,0:T(8,128)(2,1)} %shard_map.46), calls=%async_computation | async-start | bytes 6291456 | tf_op jit(solution)/shard_map/all_to_all | solution.py:113
  18.7 0.0 copy-done
  18.7 0.6 fusion.31
  19.3 38.1 %all-to-all-done = bf16[8,1536,128]{2,1,0:T(8,128)(2,1)S(1)} async-done(((bf16[8,1536,128]{2,1,0:T(8,128)(2,1)}), bf16[8,1536,128]{2,1,0:T(8,128)(2,1)S(1)}, u32[]{:S(2)}, u32[]{:S(2)}) %all-to-all-start) | async-done | bytes 3145760 | tf_op jit(solution)/shard_map/all_to_all | solution.py:113
  57.4 0.7 reduce_sum.12
  58.1 0.0 copy-start.1
  58.1 0.0 copy-start.2
  58.1 0.2 copy.31
  58.3 0.5 reshape.113
  58.8 0.9 copy.32
  59.6 10.6 %all-to-all-start.1 = ((bf16[32,2,2,16,96]{4,3,1,2,0:T(8,128)(2,1)}), bf16[32,2,2,16,96]{4,3,1,2,0:T(8,128)(2,1)S(1)}, u32[]{:S(2)}, u32[]{:S(2)}) async-start(bf16[32,2,2,16,96]{4,3,1,2,0:T(8,128)(2,1)} %copy.32), calls=%async_computation.1 | async-start | bytes 1048576 | tf_op jit(solution)/shard_map/all_to_all | solution.py:116
  70.2 0.1 fusion.27
  70.3 0.3 fusion.24
  70.6 0.0 copy-done.1
  70.7 0.0 copy-done.2
  70.7 0.2 maximum_bitcast_fusion.4
  70.8 0.4 subtract_convert_fusion
  71.2 15.5 %all-to-all-done.1 = bf16[32,2,2,16,96]{4,3,1,2,0:T(8,128)(2,1)S(1)} async-done(((bf16[32,2,2,16,96]{4,3,1,2,0:T(8,128)(2,1)}), bf16[32,2,2,16,96]{4,3,1,2,0:T(8,128)(2,1)S(1)}, u32[]{:S(2)}, u32[]{:S(2)}) %all-to-all-start.1) | async-done | bytes 393248 | tf_op jit(solution)/shard_map/all_to_all | solution.py:116
  86.8 0.6 fusion
  87.4 0.6 fusion.1
  88.0 0.9 %fusion.7 = f32[2,96,512]{2,1,0:T(8,128)} fusion(f32[2,192,1024]{2,1,0:T(8,128)S(1)} %fusion.1), kind=kLoop, calls=%fused_computation.12 | loop fusion | flops 589824 | bytes 1966080 | tf_op jit(solution)/shard_map/div | solution.py:140
  (3 shorter events, 0.0 us)
Async XLA Ops:
  11.1 7.6 %copy-start = (f32[2,2,96,96]{3,2,1,0:T(8,128)S(1)}, f32[2,2,96,96]{3,2,1,0:T(8,128)}, u32[]{:S(2)}) copy-start(f32[2,2,96,96]{3,2,1,0:T(8,128)} %param.7) | copy-start | bytes 442372
  11.1 46.4 %all-to-all-start = ((bf16[8,1536,128]{2,1,0:T(8,128)(2,1)}), bf16[8,1536,128]{2,1,0:T(8,128)(2,1)S(1)}, u32[]{:S(2)}, u32[]{:S(2)}) async-start(bf16[8,1536,128]{2,1,0:T(8,128)(2,1)} %shard_map.46), calls=%async_computation | async-start | bytes 6291456 | tf_op jit(solution)/shard_map/all_to_all | solution.py:113
  58.1 12.5 %copy-start.1 = (f32[2,2,96,96]{3,2,1,0:T(8,128)S(1)}, f32[2,2,96,96]{3,2,1,0:T(8,128)}, u32[]{:S(2)}) copy-start(f32[2,2,96,96]{3,2,1,0:T(8,128)} %param.7) | copy-start | bytes 442372
  58.1 12.6 %copy-start.2 = (f32[2,96,96]{2,1,0:T(8,128)S(1)}, f32[2,96,96]{2,1,0:T(8,128)}, u32[]{:S(2)}) copy-start(f32[2,96,96]{2,1,0:T(8,128)} %fusion.31) | copy-start | bytes 221188
  59.6 27.1 %all-to-all-start.1 = ((bf16[32,2,2,16,96]{4,3,1,2,0:T(8,128)(2,1)}), bf16[32,2,2,16,96]{4,3,1,2,0:T(8,128)(2,1)S(1)}, u32[]{:S(2)}, u32[]{:S(2)}) async-start(bf16[32,2,2,16,96]{4,3,1,2,0:T(8,128)(2,1)} %copy.32), calls=%async_computation.1 | async-start | bytes 1048576 | tf_op jit(solution)/shard_map/all_to_all | solution.py:116

commit v15 on v14

--- a/solution.py
+++ b/solution.py
@@ -58,13 +58,13 @@
 def phase_sums(q_columns, cell_coords, velocity_t):
     groups, _, rows = q_columns.shape
     width, cells = velocity_t.shape
-    pad = 8
+    pad = 3
     per_step = 2
     steps = groups // per_step
     block_width = per_step * 2 * rows
-    c_in = jnp.pad(cell_coords, ((0, 0), (0, pad - 3)))
+    c_in = cell_coords
     q_in = jnp.concatenate([q_columns, q_columns], axis=2).transpose(1, 0, 2).reshape(3, steps, block_width)
-    q_in = jnp.pad(q_in, ((0, pad - 3), (0, 0), (0, 0))).transpose(1, 0, 2)
+    q_in = q_in.transpose(1, 0, 2)
     return pl.pallas_call(
         phase_sum_kernel,
         grid=(steps,),
@@ -114,7 +114,6 @@
     summed = jnp.sum(gathered.astype(jnp.float32), axis=0).astype(jnp.bfloat16)
     blocks = summed.reshape(frames_dev, branches, 2, n_tm, q_local).transpose(3, 2, 4, 0, 1)
     collected = lax.all_to_all(blocks, "tm", split_axis=0, concat_axis=0, tiled=True)
-    collected = collected.astype(jnp.float32)
 
     scale = 1.0 / math.sqrt(cell_dev * n_cell)
     e_real = eigvecs[:, 0] * scale
@@ -123,8 +122,9 @@
         [jnp.concatenate([e_real, -e_imag], axis=2), jnp.concatenate([e_imag, e_real], axis=2)],
         axis=1,
     )
-    highest = lax.Precision.HIGHEST
-    amplitude = jnp.einsum("arjtk,jrks->jats", collected, e_block, precision=highest).reshape(
+    amplitude = jnp.einsum(
+        "arjtk,jrks->jats", collected, e_block.astype(jnp.bfloat16), preferred_element_type=jnp.float32
+    ).reshape(
         q_local, frames, 2 * branches
     )
     cosines, sines = twiddles(frames)

time: 89.3 us -> 89.2 us (level)
  blocking collectives: 0 us -> 46.2 us
  waiting for transfers between devices: 53.7 us -> 15.6 us
  starting transfers between devices: 18.2 us -> 10.9 us
    all_to_all x0 -> x1, blocking collectives: none -> 46.2 us  [local(): lax.all_to_all(partial_term, 'cell', split_axis=0, concat_axis=0, tiled=T...]
    all_to_all x1 -> x0, waiting for transfers between devices: 38.1 us -> none  [local(): lax.all_to_all(partial_term, 'cell', split_axis=0, concat_axis=0, tiled=T...]
    all_to_all x1 -> x0, starting transfers between devices: 7.61 us -> none  [local(): lax.all_to_all(partial_term, 'cell', split_axis=0, concat_axis=0, tiled=T...]
  transfers between devices with their start and end apart: 2 -> 1, of which waited for: 2 -> 1; matrix products, arithmetic and copies ran while one was open for 2% -> 1% of each run, Pallas kernels for 0% -> 0%
where the time goes in v15:
time: 89.2 us; the launch traced here: 88.8 us
  blocking collectives  46.2 us (52%)
  waiting for transfers between devices  15.6 us (17%)
  starting transfers between devices  10.9 us (12%)
  Pallas kernels  7 us (8%)
  local copies, waits for them, and re-layouts  5.42 us (6%)
  other arithmetic  2.58 us (3%)
  matrix products  0.94 us (1%)
    all_to_all x1, blocking collectives, local(): lax.all_to_all(partial_term, 'cell', split_axis=0, concat_axis=0, tiled=T...  46.2 us
    all_to_all x1, waiting for transfers between devices, local(): lax.all_to_all(blocks, 'tm', split_axis=0, concat_axis=0, tiled=True)  15.6 us
    all_to_all x1, starting transfers between devices, local(): lax.all_to_all(blocks, 'tm', split_axis=0, concat_axis=0, tiled=True)  10.9 us
    pallas_call x1, Pallas kernels, phase_sums(): pl.pallas_call(phase_sum_kernel, grid=(steps,), in_specs=[pl.BlockSpec((c...  7 us
  transfers between devices with their start and end apart: 1, of which 1 were waited for; matrix products, arithmetic and copies ran while one was open for 1% of the time, Pallas kernels for 0%

profile of v15, /device:TPU:1, one launch (start us, length us, event | category | flops | bytes accessed | tf_op | source)
XLA Modules:
  0.0 88.8 jit_solution(3050857983306185891)
XLA Ops:
  0.0 1.5 %copy.30.c_ref = s32[512,3]{1,0:T(8,128)} copy(s32[512,3]{0,1:T(4,128)} %param.5) | data formatting | bytes 12288 | tf_op args[1]
  1.6 1.0 %reshape.109 = s32[32,8,2,3]{2,1,0,3:T(8,128)S(1)} reshape(s32[512,3]{0,1:T(4,128)} %param.6) | data formatting | bytes 12288 | tf_op jit(solution)/shard_map/reshape | solution.py:109
  2.6 0.6 copy.26
  3.2 0.1 copy.27
  3.3 0.1 add_bitcast_fusion
  3.4 0.6 copy.46
  4.0 7.0 %shard_map.46 = bf16[8,1536,128]{2,1,0:T(8,128)(2,1)} custom-call(s32[512,3]{1,0:T(8,128)} %copy.30.c_ref, s32[4,3,256]{2,1,0:T(4,128)} %bitcast.65, bf16[1536,512]{1,0:T(8,128)(2,1)} %bitcast.66), custom_call_target="tpu_custom_call" | custom-call | flops 1610612736 | bytes 4718592 | tf_op jit(solution)/shard_map/pallas_call | solution.py:68
  11.0 46.2 %all_to_all.10 = bf16[8,1536,128]{2,1,0:T(8,128)(2,1)S(1)} all-to-all(bf16[8,1536,128]{2,1,0:T(8,128)(2,1)} %shard_map.46), channel_id=1, replica_groups=mesh['tm'=32,'cell'=8] {'cell'}, dimensions={0} | all-to-all | bytes 6291456 | tf_op jit(solution)/shard_map/all_to_all | solution.py:113
  57.3 0.7 reduce_sum.12
  57.9 0.0 copy-start
  57.9 0.2 copy.31
  58.1 0.5 reshape.113
  58.6 0.9 copy.32
  59.4 10.9 %all-to-all-start.1 = ((bf16[32,2,2,16,96]{4,3,1,2,0:T(8,128)(2,1)}), bf16[32,2,2,16,96]{4,3,1,2,0:T(8,128)(2,1)S(1)}, u32[]{:S(2)}, u32[]{:S(2)}) async-start(bf16[32,2,2,16,96]{4,3,1,2,0:T(8,128)(2,1)} %copy.32), calls=%async_computation.1 | async-start | bytes 1048576 | tf_op jit(solution)/shard_map/all_to_all | solution.py:116
  70.4 0.1 fusion.30
  70.5 0.3 fusion.27
  70.8 0.0 copy-done
  70.9 0.1 maximum_bitcast_fusion.4
  71.0 0.4 subtract_convert_fusion
  71.4 15.6 %all-to-all-done.1 = bf16[32,2,2,16,96]{4,3,1,2,0:T(8,128)(2,1)S(1)} async-done(((bf16[32,2,2,16,96]{4,3,1,2,0:T(8,128)(2,1)}), bf16[32,2,2,16,96]{4,3,1,2,0:T(8,128)(2,1)S(1)}, u32[]{:S(2)}, u32[]{:S(2)}) %all-to-all-start.1) | async-done | bytes 393248 | tf_op jit(solution)/shard_map/all_to_all | solution.py:116
  87.0 0.4 fusion
  87.3 0.6 fusion.1
  87.9 0.9 %fusion.7 = f32[2,96,512]{2,1,0:T(8,128)} fusion(f32[2,192,1024]{2,1,0:T(8,128)S(1)} %fusion.1), kind=kLoop, calls=%fused_computation.12 | loop fusion | flops 589824 | bytes 1966080 | tf_op jit(solution)/shard_map/div | solution.py:140
  (2 shorter events, 0.1 us)
Async XLA Ops:
  57.9 12.9 %copy-start = (f32[2,2,96,96]{3,2,1,0:T(8,128)S(1)}, f32[2,2,96,96]{3,2,1,0:T(8,128)}, u32[]{:S(2)}) copy-start(f32[2,2,96,96]{3,2,1,0:T(8,128)} %param.7) | copy-start | bytes 442372
  59.4 27.5 %all-to-all-start.1 = ((bf16[32,2,2,16,96]{4,3,1,2,0:T(8,128)(2,1)}), bf16[32,2,2,16,96]{4,3,1,2,0:T(8,128)(2,1)S(1)}, u32[]{:S(2)}, u32[]{:S(2)}) async-start(bf16[32,2,2,16,96]{4,3,1,2,0:T(8,128)(2,1)} %copy.32), calls=%async_computation.1 | async-start | bytes 1048576 | tf_op jit(solution)/shard_map/all_to_all | solution.py:116

commit v16 on v14

--- a/solution.py
+++ b/solution.py
@@ -59,7 +59,7 @@
     groups, _, rows = q_columns.shape
     width, cells = velocity_t.shape
     pad = 8
-    per_step = 2
+    per_step = 4
     steps = groups // per_step
     block_width = per_step * 2 * rows
     c_in = jnp.pad(cell_coords, ((0, 0), (0, pad - 3)))

time: 89.3 us -> 88.9 us (level)
  no operation moved by 1% of the time
where the time goes in v16:
time: 88.9 us; the launch traced here: 88.6 us
  waiting for transfers between devices  53.6 us (60%)
  starting transfers between devices  18.2 us (20%)
  Pallas kernels  6.65 us (7%)
  local copies, waits for them, and re-layouts  5.46 us (6%)
  other arithmetic  3.27 us (4%)
  matrix products  1.24 us (1%)
    all_to_all x1, waiting for transfers between devices, local(): lax.all_to_all(partial_term, 'cell', split_axis=0, concat_axis=0, tiled=T...  38.1 us
    all_to_all x1, waiting for transfers between devices, local(): lax.all_to_all(blocks, 'tm', split_axis=0, concat_axis=0, tiled=True)  15.5 us
    all_to_all x1, starting transfers between devices, local(): lax.all_to_all(blocks, 'tm', split_axis=0, concat_axis=0, tiled=True)  10.6 us
    all_to_all x1, starting transfers between devices, local(): lax.all_to_all(partial_term, 'cell', split_axis=0, concat_axis=0, tiled=T...  7.61 us
    pallas_call x1, Pallas kernels, phase_sums(): pl.pallas_call(phase_sum_kernel, grid=(steps,), in_specs=[pl.BlockSpec((c...  6.65 us
  transfers between devices with their start and end apart: 2, of which 2 were waited for; matrix products, arithmetic and copies ran while one was open for 2% of the time, Pallas kernels for 0%

profile of v16, /device:TPU:1, one launch (start us, length us, event | category | flops | bytes accessed | tf_op | source)
XLA Modules:
  0.0 88.6 jit_solution(17225183044905235113)
XLA Ops:
  0.0 0.8 copy.26
  0.8 1.0 %reshape.109 = s32[32,8,2,3]{2,1,0,3:T(8,128)S(1)} reshape(s32[512,3]{0,1:T(4,128)} %param.6) | data formatting | bytes 12288 | tf_op jit(solution)/shard_map/reshape | solution.py:109
  1.9 0.6 copy.27
  2.5 0.1 copy.28
  2.6 0.1 add_bitcast_fusion
  2.7 0.6 pad_bitcast_fusion.q_ref
  3.3 0.7 pad.8.c_ref
  4.1 6.6 %shard_map.46 = bf16[8,1536,128]{2,1,0:T(8,128)(2,1)} custom-call(s32[512,8]{1,0:T(8,128)} %pad.8.c_ref, s32[2,8,512]{2,1,0:T(8,128)} %pad_bitcast_fusion.q_ref, bf16[1536,512]{1,0:T(8,128)(2,1)} %bitcast.59), custom_call_target="tpu_custom_call" | custom-call | flops 1610612736 | bytes 4718592 | tf_op jit(solution)/shard_map/pallas_call | solution.py:68
  10.7 0.0 copy-start
  10.7 7.6 %all-to-all-start = ((bf16[8,1536,128]{2,1,0:T(8,128)(2,1)}), bf16[8,1536,128]{2,1,0:T(8,128)(2,1)S(1)}, u32[]{:S(2)}, u32[]{:S(2)}) async-start(bf16[8,1536,128]{2,1,0:T(8,128)(2,1)} %shard_map.46), calls=%async_computation | async-start | bytes 6291456 | tf_op jit(solution)/shard_map/all_to_all | solution.py:113
  18.3 0.0 copy-done
  18.3 0.6 fusion.31
  19.0 38.1 %all-to-all-done = bf16[8,1536,128]{2,1,0:T(8,128)(2,1)S(1)} async-done(((bf16[8,1536,128]{2,1,0:T(8,128)(2,1)}), bf16[8,1536,128]{2,1,0:T(8,128)(2,1)S(1)}, u32[]{:S(2)}, u32[]{:S(2)}) %all-to-all-start) | async-done | bytes 3145760 | tf_op jit(solution)/shard_map/all_to_all | solution.py:113
  57.1 0.7 reduce_sum.12
  57.7 0.0 copy-start.1
  57.7 0.0 copy-start.2
  57.8 0.2 copy.31
  57.9 0.5 reshape.113
  58.4 0.9 copy.32
  59.3 10.6 %all-to-all-start.1 = ((bf16[32,2,2,16,96]{4,3,1,2,0:T(8,128)(2,1)}), bf16[32,2,2,16,96]{4,3,1,2,0:T(8,128)(2,1)S(1)}, u32[]{:S(2)}, u32[]{:S(2)}) async-start(bf16[32,2,2,16,96]{4,3,1,2,0:T(8,128)(2,1)} %copy.32), calls=%async_computation.1 | async-start | bytes 1048576 | tf_op jit(solution)/shard_map/all_to_all | solution.py:116
  69.9 0.1 fusion.27
  70.0 0.3 fusion.24
  70.3 0.0 copy-done.1
  70.3 0.0 copy-done.2
  70.3 0.2 maximum_bitcast_fusion.4
  70.5 0.4 subtract_convert_fusion
  70.9 15.5 %all-to-all-done.1 = bf16[32,2,2,16,96]{4,3,1,2,0:T(8,128)(2,1)S(1)} async-done(((bf16[32,2,2,16,96]{4,3,1,2,0:T(8,128)(2,1)}), bf16[32,2,2,16,96]{4,3,1,2,0:T(8,128)(2,1)S(1)}, u32[]{:S(2)}, u32[]{:S(2)}) %all-to-all-start.1) | async-done | bytes 393248 | tf_op jit(solution)/shard_map/all_to_all | solution.py:116
  86.4 0.7 fusion
  87.1 0.6 fusion.1
  87.7 0.9 %fusion.7 = f32[2,96,512]{2,1,0:T(8,128)} fusion(f32[2,192,1024]{2,1,0:T(8,128)S(1)} %fusion.1), kind=kLoop, calls=%fused_computation.12 | loop fusion | flops 589824 | bytes 1966080 | tf_op jit(solution)/shard_map/div | solution.py:140
  (3 shorter events, 0.0 us)
Async XLA Ops:
  10.7 7.6 %copy-start = (f32[2,2,96,96]{3,2,1,0:T(8,128)S(1)}, f32[2,2,96,96]{3,2,1,0:T(8,128)}, u32[]{:S(2)}) copy-start(f32[2,2,96,96]{3,2,1,0:T(8,128)} %param.7) | copy-start | bytes 442372
  10.7 46.4 %all-to-all-start = ((bf16[8,1536,128]{2,1,0:T(8,128)(2,1)}), bf16[8,1536,128]{2,1,0:T(8,128)(2,1)S(1)}, u32[]{:S(2)}, u32[]{:S(2)}) async-start(bf16[8,1536,128]{2,1,0:T(8,128)(2,1)} %shard_map.46), calls=%async_computation | async-start | bytes 6291456 | tf_op jit(solution)/shard_map/all_to_all | solution.py:113
  57.7 12.6 %copy-start.1 = (f32[2,2,96,96]{3,2,1,0:T(8,128)S(1)}, f32[2,2,96,96]{3,2,1,0:T(8,128)}, u32[]{:S(2)}) copy-start(f32[2,2,96,96]{3,2,1,0:T(8,128)} %param.7) | copy-start | bytes 442372
  57.7 12.6 %copy-start.2 = (f32[2,96,96]{2,1,0:T(8,128)S(1)}, f32[2,96,96]{2,1,0:T(8,128)}, u32[]{:S(2)}) copy-start(f32[2,96,96]{2,1,0:T(8,128)} %fusion.31) | copy-start | bytes 221188
  59.3 27.2 %all-to-all-start.1 = ((bf16[32,2,2,16,96]{4,3,1,2,0:T(8,128)(2,1)}), bf16[32,2,2,16,96]{4,3,1,2,0:T(8,128)(2,1)S(1)}, u32[]{:S(2)}, u32[]{:S(2)}) async-start(bf16[32,2,2,16,96]{4,3,1,2,0:T(8,128)(2,1)} %copy.32), calls=%async_computation.1 | async-start | bytes 1048576 | tf_op jit(solution)/shard_map/all_to_all | solution.py:116

commit v17 on v16

--- a/solution.py
+++ b/solution.py
@@ -114,7 +114,6 @@
     summed = jnp.sum(gathered.astype(jnp.float32), axis=0).astype(jnp.bfloat16)
     blocks = summed.reshape(frames_dev, branches, 2, n_tm, q_local).transpose(3, 2, 4, 0, 1)
     collected = lax.all_to_all(blocks, "tm", split_axis=0, concat_axis=0, tiled=True)
-    collected = collected.astype(jnp.float32)
 
     scale = 1.0 / math.sqrt(cell_dev * n_cell)
     e_real = eigvecs[:, 0] * scale
@@ -123,8 +122,9 @@
         [jnp.concatenate([e_real, -e_imag], axis=2), jnp.concatenate([e_imag, e_real], axis=2)],
         axis=1,
     )
-    highest = lax.Precision.HIGHEST
-    amplitude = jnp.einsum("arjtk,jrks->jats", collected, e_block, precision=highest).reshape(
+    amplitude = jnp.einsum(
+        "arjtk,jrks->jats", collected, e_block.astype(jnp.bfloat16), preferred_element_type=jnp.float32
+    ).reshape(
         q_local, frames, 2 * branches
     )
     cosines, sines = twiddles(frames)

time: 88.9 us -> 88.9 us (level)
  blocking collectives: 0 us -> 46.2 us
  waiting for transfers between devices: 53.6 us -> 15.6 us
  starting transfers between devices: 18.2 us -> 11 us
    all_to_all x0 -> x1, blocking collectives: none -> 46.2 us  [local(): lax.all_to_all(partial_term, 'cell', split_axis=0, concat_axis=0, tiled=T...]
    all_to_all x1 -> x0, waiting for transfers between devices: 38.1 us -> none  [local(): lax.all_to_all(partial_term, 'cell', split_axis=0, concat_axis=0, tiled=T...]
    all_to_all x1 -> x0, starting transfers between devices: 7.61 us -> none  [local(): lax.all_to_all(partial_term, 'cell', split_axis=0, concat_axis=0, tiled=T...]
  transfers between devices with their start and end apart: 2 -> 1, of which waited for: 2 -> 1; matrix products, arithmetic and copies ran while one was open for 2% -> 1% of each run, Pallas kernels for 0% -> 0%
where the time goes in v17:
time: 88.9 us; the launch traced here: 88.5 us
  blocking collectives  46.2 us (52%)
  waiting for transfers between devices  15.6 us (18%)
  starting transfers between devices  11 us (12%)
  Pallas kernels  6.65 us (7%)
  local copies, waits for them, and re-layouts  5.44 us (6%)
  other arithmetic  2.58 us (3%)
  matrix products  0.94 us (1%)
    all_to_all x1, blocking collectives, local(): lax.all_to_all(partial_term, 'cell', split_axis=0, concat_axis=0, tiled=T...  46.2 us
    all_to_all x1, waiting for transfers between devices, local(): lax.all_to_all(blocks, 'tm', split_axis=0, concat_axis=0, tiled=True)  15.6 us
    all_to_all x1, starting transfers between devices, local(): lax.all_to_all(blocks, 'tm', split_axis=0, concat_axis=0, tiled=True)  11 us
    pallas_call x1, Pallas kernels, phase_sums(): pl.pallas_call(phase_sum_kernel, grid=(steps,), in_specs=[pl.BlockSpec((c...  6.65 us
  transfers between devices with their start and end apart: 1, of which 1 were waited for; matrix products, arithmetic and copies ran while one was open for 1% of the time, Pallas kernels for 0%

profile of v17, /device:TPU:1, one launch (start us, length us, event | category | flops | bytes accessed | tf_op | source)
XLA Modules:
  0.0 88.5 jit_solution(94583097792091922)
XLA Ops:
  0.0 0.8 copy.26
  0.8 1.0 %reshape.109 = s32[32,8,2,3]{2,1,0,3:T(8,128)S(1)} reshape(s32[512,3]{0,1:T(4,128)} %param.6) | data formatting | bytes 12288 | tf_op jit(solution)/shard_map/reshape | solution.py:109
  1.9 0.6 copy.27
  2.5 0.1 copy.28
  2.6 0.1 add_bitcast_fusion
  2.7 0.6 pad_bitcast_fusion.q_ref
  3.3 0.7 pad.8.c_ref
  4.1 6.6 %shard_map.46 = bf16[8,1536,128]{2,1,0:T(8,128)(2,1)} custom-call(s32[512,8]{1,0:T(8,128)} %pad.8.c_ref, s32[2,8,512]{2,1,0:T(8,128)} %pad_bitcast_fusion.q_ref, bf16[1536,512]{1,0:T(8,128)(2,1)} %bitcast.64), custom_call_target="tpu_custom_call" | custom-call | flops 1610612736 | bytes 4718592 | tf_op jit(solution)/shard_map/pallas_call | solution.py:68
  10.7 46.2 %all_to_all.10 = bf16[8,1536,128]{2,1,0:T(8,128)(2,1)S(1)} all-to-all(bf16[8,1536,128]{2,1,0:T(8,128)(2,1)} %shard_map.46), channel_id=1, replica_groups=mesh['tm'=32,'cell'=8] {'cell'}, dimensions={0} | all-to-all | bytes 6291456 | tf_op jit(solution)/shard_map/all_to_all | solution.py:113
  56.9 0.7 reduce_sum.12
  57.6 0.0 copy-start
  57.6 0.2 copy.31
  57.8 0.5 reshape.113
  58.3 0.9 copy.32
  59.1 11.0 %all-to-all-start.1 = ((bf16[32,2,2,16,96]{4,3,1,2,0:T(8,128)(2,1)}), bf16[32,2,2,16,96]{4,3,1,2,0:T(8,128)(2,1)S(1)}, u32[]{:S(2)}, u32[]{:S(2)}) async-start(bf16[32,2,2,16,96]{4,3,1,2,0:T(8,128)(2,1)} %copy.32), calls=%async_computation.1 | async-start | bytes 1048576 | tf_op jit(solution)/shard_map/all_to_all | solution.py:116
  70.1 0.1 fusion.30
  70.2 0.3 fusion.27
  70.5 0.0 copy-done
  70.6 0.1 maximum_bitcast_fusion.4
  70.7 0.4 subtract_convert_fusion
  71.1 15.6 %all-to-all-done.1 = bf16[32,2,2,16,96]{4,3,1,2,0:T(8,128)(2,1)S(1)} async-done(((bf16[32,2,2,16,96]{4,3,1,2,0:T(8,128)(2,1)}), bf16[32,2,2,16,96]{4,3,1,2,0:T(8,128)(2,1)S(1)}, u32[]{:S(2)}, u32[]{:S(2)}) %all-to-all-start.1) | async-done | bytes 393248 | tf_op jit(solution)/shard_map/all_to_all | solution.py:116
  86.7 0.4 fusion
  87.0 0.6 fusion.1
  87.6 0.9 %fusion.7 = f32[2,96,512]{2,1,0:T(8,128)} fusion(f32[2,192,1024]{2,1,0:T(8,128)S(1)} %fusion.1), kind=kLoop, calls=%fused_computation.12 | loop fusion | flops 589824 | bytes 1966080 | tf_op jit(solution)/shard_map/div | solution.py:140
  (3 shorter events, 0.1 us)
Async XLA Ops:
  57.6 12.9 %copy-start = (f32[2,2,96,96]{3,2,1,0:T(8,128)S(1)}, f32[2,2,96,96]{3,2,1,0:T(8,128)}, u32[]{:S(2)}) copy-start(f32[2,2,96,96]{3,2,1,0:T(8,128)} %param.7) | copy-start | bytes 442372
  59.1 27.5 %all-to-all-start.1 = ((bf16[32,2,2,16,96]{4,3,1,2,0:T(8,128)(2,1)}), bf16[32,2,2,16,96]{4,3,1,2,0:T(8,128)(2,1)S(1)}, u32[]{:S(2)}, u32[]{:S(2)}) async-start(bf16[32,2,2,16,96]{4,3,1,2,0:T(8,128)(2,1)} %copy.32), calls=%async_computation.1 | async-start | bytes 1048576 | tf_op jit(solution)/shard_map/all_to_all | solution.py:116
